TPU v7x, 256 devices: a whole 4x4x8 slice. The times are simulated.
256 devices in a mesh: fsdp: 32 (over x, z), expert: 8 (over y, core).
Axes of the slice: x: 4, y: 4, z: 8, core: 2. Of those that a mesh axis runs over, the one named last changes fastest.
Arguments:
- expert_rows: bfloat16 [32, 128, 8, 10, 2880], P('fsdp', 'expert'), may hold values from -6 to 6
- residual: bfloat16 [32768, 2880], P(('fsdp', 'expert')), may hold values from -3 to 3
- route_ids: int32 [32768, 4], P(('fsdp', 'expert')), may hold values from 0 to 127, as said below
- route_weights: float32 [32768, 4], P(('fsdp', 'expert')), may hold values from 0.05 to 1
- route_slots: int32 [32768, 4], P(('fsdp', 'expert')), may hold values from 0 to 9, as said below
- doc_start: int32 [32768], P('fsdp'), may hold values from 0 to 32767, as said below
- norm_gain: float32 [2880], replicated, may hold values from 0.5 to 12, as said below
- projection_weight: bfloat16 [2880, 8, 640], P('fsdp', 'expert'), may hold values from -0.109375 to 0.109375
- projection_bias: float32 [8, 640], P('expert'), may hold values from -3 to 3
- sinks: float32 [8, 8], P('expert'), may hold values from -2 to 5
- output_weight: bfloat16 [8, 512, 2880], P('expert', 'fsdp'), may hold values from -0.25 to 0.25
- b_out: float32 [2880], replicated, may hold values from -3 to 3
Outputs:
- block_out: bfloat16 [32768, 2880], P(('fsdp', 'expert'))
Inputs may be any that keep to these rules, and one draw needn't show every extreme that they name: `route_ids`: each token names 4 different experts. Among the tokens of each aligned block of 128 tokens (one device's), no expert is named more than 10 times, and some expert is named exactly 10 times in every block. `route_slots`: the slot of a token's route counts the earlier tokens of the same aligned block of 128 tokens that name the same expert. doc_start of a token is the position where its document begins: it never exceeds the token's position, equals it at each document's first token, and is the same for all tokens of a document. `norm_gain`: Positive.
All inputs are finite; a program needn't handle non-finite values.
Results may differ from a plain program's by a relative error of at most 0.04.
The roundings to bfloat16 on the way count: a program that leaves them out, or rounds other values in their place, can miss the bound.
Values may be sent and summed in bfloat16 or wider, within the bound.
No kernel may reach another device: no remote copies, remote signals or barrier semaphores. Data moves between devices by JAX's collectives and lax.ppermute only.
A program may use at most 128 MiB of HBM per device.

v0:
```python
import jax
import jax.numpy as jnp
from jax import lax
from jax.sharding import PartitionSpec as P

HEAD_SIZE = 64
QUERY_PER_KV = 8
TOPK = 4
KEYS_VISIBLE = 128


ROPE_BASE = 150000.0
EPSILON = 1e-05


def passed_along(block, axis, distance):
    devices = range(lax.axis_size(axis))
    route = [(i - distance, i) for i in devices if i - distance in devices]
    return lax.ppermute(block, axis, route)


def apply_rotation(values, positions):
    half_width = values.shape[-1] // 2
    steps_half = jnp.arange(half_width, dtype=jnp.float32)
    frequency = ROPE_BASE ** (-2.0 * steps_half / values.shape[-1])
    angles = positions.astype(jnp.float32)[:, None] * frequency[None, :]
    shape_out = (angles.shape[0],) + (1,) * (values.ndim - 2) + (half_width,)
    cosine = jnp.cos(angles).reshape(shape_out)
    sine_part = jnp.sin(angles).reshape(shape_out)
    front_half = values[..., :half_width]
    back_half = values[..., half_width:]
    return jnp.concatenate(
        [front_half * cosine - back_half * sine_part, back_half * cosine + front_half * sine_part],
        axis=-1,
    )


def attend_block(query_rows, key_rows, query_pos, key_pos, starts, sinks):
    keys_only = key_rows[..., :HEAD_SIZE]
    values_only = key_rows[..., HEAD_SIZE:]
    scores = jnp.einsum(
        "qjgd,kjd->jgqk", query_rows, keys_only, preferred_element_type=jnp.float32
    ) * HEAD_SIZE ** (-0.5)
    allowed = (
        (key_pos[None, :] <= query_pos[:, None])
        & (key_pos[None, :] > query_pos[:, None] - KEYS_VISIBLE)
        & (key_pos[None, :] >= starts[:, None])
    )
    masked = jnp.where(allowed[None, None], scores, -jnp.inf)
    row_peak = jnp.maximum(jnp.max(masked, axis=-1), sinks[:, :, None])
    exponent = jnp.exp(masked - row_peak[..., None])
    denominator = jnp.sum(exponent, axis=-1) + jnp.exp(sinks[:, :, None] - row_peak)
    weights_soft = (exponent / denominator[..., None]).astype(jnp.bfloat16)
    return jnp.einsum(
        "jgqk,kjd->qjgd", weights_soft, values_only, preferred_element_type=jnp.float32
    ).astype(jnp.bfloat16)


def shards(
    expert_rows,
    residual,
    route_ids,
    route_weights,
    route_slots,
    doc_start,
    norm_gain,
    projection_weight,
    projection_bias,
    sinks,
    output_weight,
    b_out,
):
    own_rows = residual.shape[0]
    model_width = residual.shape[1]
    returned = lax.all_to_all(expert_rows, "expert", split_axis=2, concat_axis=1, tiled=True)
    capacity = returned.shape[3]
    slot_table = returned.reshape(-1, model_width)
    flat_index = (route_ids * capacity + route_slots).reshape(-1)
    picked = jnp.take(slot_table, flat_index, axis=0).reshape(own_rows, TOPK, model_width)
    combined = route_weights[:, 0:1] * picked[:, 0].astype(jnp.float32)
    for route_number in range(1, TOPK):
        combined = combined + route_weights[:, route_number : route_number + 1] * picked[
            :, route_number
        ].astype(jnp.float32)
    hidden = (residual.astype(jnp.float32) + combined).astype(jnp.bfloat16)
    widened = hidden.astype(jnp.float32)
    normalized_rows = (
        widened
        * lax.rsqrt(jnp.mean(widened * widened, axis=-1, keepdims=True) + EPSILON)
        * norm_gain
    ).astype(jnp.bfloat16)
    gathered = lax.all_gather(normalized_rows, "expert", axis=0, tiled=True)
    block_rows = gathered.shape[0]
    local_heads = projection_weight.shape[1]
    qkv_full, out_full = (
        lax.all_gather(projection_weight, "fsdp", axis=0, tiled=True),
        lax.all_gather(output_weight, "fsdp", axis=1, tiled=True),
    )
    projected_rows = jnp.dot(
        gathered, qkv_full.reshape(model_width, -1), preferred_element_type=jnp.float32
    )
    projected_rows = projected_rows.reshape(block_rows, local_heads, -1) + projection_bias
    block_start = lax.axis_index("fsdp") * block_rows
    positions = block_start + jnp.arange(block_rows, dtype=jnp.int32)
    document_position = positions - doc_start
    query_rows = apply_rotation(
        projected_rows[..., : QUERY_PER_KV * HEAD_SIZE].reshape(
            block_rows, local_heads, QUERY_PER_KV, HEAD_SIZE
        ),
        document_position,
    ).astype(jnp.bfloat16)
    key_part = apply_rotation(
        projected_rows[..., QUERY_PER_KV * HEAD_SIZE : (QUERY_PER_KV + 1) * HEAD_SIZE],
        document_position,
    )
    keys_values = jnp.concatenate(
        [key_part, projected_rows[..., (QUERY_PER_KV + 1) * HEAD_SIZE :]], axis=-1
    ).astype(jnp.bfloat16)
    before = passed_along(keys_values[block_rows - KEYS_VISIBLE :], "fsdp", 1)
    extended = jnp.concatenate([before, keys_values], axis=0)
    query_block = min(512, block_rows)
    outputs_list = []
    for first_row in range(0, block_rows, query_block):
        key_rows = extended[first_row : first_row + query_block + KEYS_VISIBLE]
        key_pos = (
            block_start
            - KEYS_VISIBLE
            + first_row
            + jnp.arange(query_block + KEYS_VISIBLE, dtype=jnp.int32)
        )
        outputs_list.append(
            attend_block(
                query_rows[first_row : first_row + query_block],
                key_rows,
                positions[first_row : first_row + query_block],
                key_pos,
                doc_start[first_row : first_row + query_block],
                sinks,
            )
        )
    attention_result = jnp.concatenate(outputs_list, axis=0).reshape(block_rows, -1)
    output_weights = out_full.reshape(-1, model_width)
    projection_step = lax.psum_scatter(
        jnp.dot(attention_result, output_weights, preferred_element_type=jnp.float32).astype(
            jnp.bfloat16
        ),
        "expert",
        scatter_dimension=0,
        tiled=True,
    ).astype(jnp.float32)
    return (widened + projection_step + b_out).astype(jnp.bfloat16)


def solution(mesh):
    in_specs = (
        P("fsdp", "expert", None, None, None),
        P(("fsdp", "expert"), None),
        P(("fsdp", "expert"), None),
        P(("fsdp", "expert"), None),
        P(("fsdp", "expert"), None),
        P("fsdp"),
        P(),
        P("fsdp", "expert", None),
        P("expert", None),
        P("expert", None),
        P("expert", "fsdp", None),
        P(),
    )
    out_specs = P(("fsdp", "expert"), None)
    return jax.shard_map(shards, mesh=mesh, in_specs=in_specs, out_specs=out_specs, check_vma=False)
```

profile of v0, /device:TPU:2, one launch (start us, length us, event | category | flops | bytes accessed | tf_op | source)
XLA Modules:
  0.0 351.0 jit_solution(14437113953388859788)
XLA Ops:
  6.5 7.5 %copy.96 = bf16[1,16,8,10,2880]{4,1,3,0,2:T(8,128)(2,1)} copy(bf16[1,16,8,10,2880]{4,2,3,1,0:T(8,128)(2,1)} %param.12) | data formatting | bytes 14745600 | tf_op args[0]
  14.1 5.1 %all-to-all-start = ((bf16[1,16,8,10,2880]{4,1,3,0,2:T(8,128)(2,1)}), bf16[1,16,8,10,2880]{4,1,3,0,2:T(8,128)(2,1)}, u32[]{:S(2)}, u32[]{:S(2)}) async-start(bf16[1,16,8,10,2880]{4,1,3,0,2:T(8,128)(2,1)} %copy.96), calls=%async_computation | async-start | bytes 15073280 | tf_op jit(solution)/shard_map/all_to_all | solution.py:75
  19.1 0.0 all-gather.6.cloned.1.call-start
  19.2 0.0 copy-done.3
  19.2 0.9 copy.100
  20.1 0.0 all-gather.6.cloned.1.call-update
  20.1 0.0 all-gather.4.cloned.1.call-start
  20.1 0.0 copy-done.15
  20.2 0.0 copy-done.16
  20.2 0.1 copy.98
  20.3 0.1 reshape.637
  20.5 84.2 %all-to-all-done = bf16[1,16,8,10,2880]{4,1,3,0,2:T(8,128)(2,1)} async-done(((bf16[1,16,8,10,2880]{4,1,3,0,2:T(8,128)(2,1)}), bf16[1,16,8,10,2880]{4,1,3,0,2:T(8,128)(2,1)}, u32[]{:S(2)}, u32[]{:S(2)}) %all-to-all-start) | async-done | bytes 7372832 | tf_op jit(solution)/shard_map/all_to_all | solution.py:75
  104.6 12.1 %copy.97 = bf16[1,8,16,1,10,2880]{5,4,2,1,3,0:T(8,128)(2,1)} copy(bf16[1,8,16,1,10,2880]{5,2,4,1,3,0:T(8,128)(2,1)} %bitcast.2) | data formatting | bytes 14745600 | tf_op jit(solution)/shard_map/all_to_all | solution.py:75
  116.7 14.4 %reshape.636 = bf16[1280,2880]{1,0:T(8,128)(2,1)} reshape(bf16[1,8,16,1,10,2880]{5,4,2,1,3,0:T(8,128)(2,1)} %copy.97) | data formatting | bytes 14745600 | tf_op jit(solution)/shard_map/reshape | solution.py:77
  131.0 10.8 %gather_fusion = bf16[512,2880]{1,0:T(8,128)(2,1)} fusion(bf16[1280,2880]{1,0:T(8,128)(2,1)} %reshape.636, s32[1024]{0:T(1024)S(1)} %pad_clamp_fusion), kind=kCustom, calls=%fused_computation | custom fusion | bytes 5900288 | tf_op jit(solution)/shard_map/jit(_take)/gather | solution.py:79
  141.9 4.7 %gather.7 = bf16[128,4,2880]{2,1,0:T(4,128)(2,1)S(1)} reshape(bf16[512,2880]{1,0:T(8,128)(2,1)} %gather_fusion) | data formatting | bytes 5898240 | tf_op jit(solution)/shard_map/jit(_take)/gather | solution.py:79
  146.5 4.2 %copy.99 = bf16[128,4,2880]{0,2,1:T(8,128)(2,1)} copy(bf16[128,4,2880]{2,1,0:T(4,128)(2,1)S(1)} %gather.7) | data formatting | bytes 5898240 | tf_op jit(solution)/shard_map/jit(_take)/gather | solution.py:79
  150.8 2.2 broadcast_select_fusion
  152.9 0.0 copy-start.11
  152.9 0.0 copy-start.9
  152.9 0.0 copy-start.14
  153.0 0.8 fusion.14
  153.8 1.3 fusion.16
  155.1 0.0 all-gather.4.cloned.1.call-update
  155.1 0.0 all-gather.8.cloned.1.call-start
  155.2 0.7 all-gather.8.cloned.1.call-update
  155.8 0.2 reduce-scatter.4.cloned.1.call-start
  156.1 0.0 copy-done.9
  156.2 0.5 multiply_cosine_fusion
  156.7 0.4 compare_and_fusion
  157.2 0.4 compare_and_fusion.1
  157.6 0.0 all-gather.6.cloned.1.call-done
  157.6 44.4 %all-gather.4.cloned.1.call-done = bf16[1024,2880]{0,1:T(8,128)(2,1)} async-done(((bf16[128,2880]{0,1:T(8,128)(2,1)}), bf16[1024,2880]{0,1:T(8,128)(2,1)}) %all-gather.4.cloned.1.call-update) | async-done | bytes 5898256 | tf_op jit(solution)/shard_map/all_gather | solution.py:92
  202.0 8.5 %fusion.74 = (bf16[1024,1,640]{0,2,1:T(8,128)(2,1)S(1)}, f32[1024,1,640]{0,2,1:T(8,128)S(1)}) fusion(f32[640]{0:T(1024)S(1)} %reduce.4, bf16[1024,2880]{0,1:T(8,128)(2,1)} %all-gather.4.cloned.1.call-done, bf16[2880,1,640]{2,1,0:T(2,128)(2,1)} %all-gather.6.cloned.1.call-done), kind=kOutput, calls=%fused_computation.121 | convolution fusion | flops 3776184320 | bytes 13519360 | tf_op jit(solution)/shard_map/dot_general | solution.py:99
  210.6 0.1 slice.122
  210.7 0.6 fusion.49
  211.3 0.0 copy-start
  211.3 3.5 collective-permute-start
  214.8 0.3 subtract_convert_fusion
  215.1 1.7 fusion.3
  216.9 0.0 copy-start.13
  216.9 2.3 collective-permute-done
  219.2 0.0 copy-done
  219.2 1.7 fusion.2
  221.0 0.7 broadcast_maximum_fusion.1
  221.7 3.5 fusion
  225.1 1.4 exponential_add_fusion.1
  226.5 3.5 %fusion.1 = f32[8,512]{1,0:T(8,128)} fusion(f32[640,512,8]{1,0,2:T(8,128)S(1)} %get-tuple-element.32, f32[8,512]{1,0:T(8,128)} %get-tuple-element.26, pred[512,640]{0,1:T(8,128)(4,1)S(1)} %compare_and_fusion), kind=kLoop, calls=%fused_computation.8 | loop fusion | flops 10481664 | bytes 10846208 | tf_op jit(solution)/shard_map/reduce_sum | solution.py:52
  230.1 0.8 exponential_add_fusion
  230.9 0.0 copy-start.1
  230.9 0.0 copy-start.5
  230.9 0.0 copy-start.7
  230.9 0.0 copy-start.8
  230.9 4.2 %fusion.30 = bf16[512,1,8,64]{0,3,2,1:T(8,128)(2,1)S(1)} fusion(f32[8,512]{1,0:T(8,128)S(1)} %exponential_add_fusion, f32[8,512]{1,0:T(8,128)S(1)} %copy-done.4, f32[640,512,8]{1,0,2:T(8,128)S(1)} %get-tuple-element.32, pred[512,640]{0,1:T(8,128)(4,1)S(1)} %compare_and_fusion, bf16[1024,1,640]{0,2,1:T(8,128)(2,1)} %copy-done.10), kind=kOutput, calls=%fused_computation.43 | convolution fusion | flops 348913664 | bytes 11452416 | tf_op jit(solution)/shard_map/jgqk,kjd->qjgd/dot_general | solution.py:54
  235.2 3.1 fusion.33
  238.3 0.1 pad_maximum_fusion
  238.4 45.6 %all-gather.8.cloned.1.call-done = bf16[1,512,2880]{2,1,0:T(8,128)(2,1)} async-done(((bf16[1,16,2880]{2,1,0:T(8,128)(2,1)}), bf16[1,512,2880]{2,1,0:T(8,128)(2,1)}) %all-gather.8.cloned.1.call-update) | async-done | bytes 2949136 | tf_op jit(solution)/shard_map/all_gather | solution.py:97
  284.0 7.0 %convolution_convert_fusion = bf16[1024,2880]{0,1:T(8,128)(2,1)} fusion(bf16[1024,512]{0,1:T(8,128)(2,1)S(1)} %bitcast.143, bf16[1,512,2880]{2,1,0:T(8,128)(2,1)} %all-gather.8.cloned.1.call-done), kind=kOutput, calls=%fused_computation.11 | convolution fusion | flops 3022848000 | bytes 9895936 | tf_op jit(solution)/shard_map/dot_general | solution.py:144
  291.1 8.5 %copy.105 = bf16[1024,2880]{1,0:T(8,128)(2,1)} copy(bf16[1024,2880]{0,1:T(8,128)(2,1)} %convolution_convert_fusion) | data formatting | bytes 11796480
  299.6 0.0 reduce-scatter.4.cloned.1.call-update
  299.6 42.1 %reduce-scatter.4.cloned.1.call-done = bf16[128,2880]{1,0:T(8,128)(2,1)} async-done(((bf16[1024,2880]{1,0:T(8,128)(2,1)}), bf16[128,2880]{1,0:T(8,128)(2,1)}) %reduce-scatter.4.cloned.1.call-update) | async-done | bytes 737296
  341.7 1.5 copy.106
  343.2 0.0 copy-done.12
  343.2 1.3 fusion.18
  (35 shorter events, 0.1 us)
Async XLA Ops:
  14.1 5.1 %copy-start.3 = (bf16[90,1,640]{2,0,1:T(8,128)(2,1)S(1)}, bf16[90,1,640]{2,0,1:T(8,128)(2,1)}, u32[]{:S(2)}) copy-start(bf16[90,1,640]{2,0,1:T(8,128)(2,1)} %param.19) | copy-start | bytes 345604
  14.1 6.1 %copy-start.15 = (s32[128,4]{0,1:T(4,128)S(1)}, s32[128,4]{0,1:T(4,128)}, u32[]{:S(2)}) copy-start(s32[128,4]{0,1:T(4,128)} %param.16) | copy-start | bytes 6148
  14.1 6.1 %copy-start.16 = (s32[128,4]{0,1:T(4,128)S(1)}, s32[128,4]{0,1:T(4,128)}, u32[]{:S(2)}) copy-start(s32[128,4]{0,1:T(4,128)} %param.14) | copy-start | bytes 6148
  14.1 6.4 %copy-start.17 = (f32[128,4]{0,1:T(4,128)S(1)}, f32[128,4]{0,1:T(4,128)}, u32[]{:S(2)}) copy-start(f32[128,4]{0,1:T(4,128)} %param.15) | copy-start | bytes 6148
  14.1 90.6 %all-to-all-start = ((bf16[1,16,8,10,2880]{4,1,3,0,2:T(8,128)(2,1)}), bf16[1,16,8,10,2880]{4,1,3,0,2:T(8,128)(2,1)}, u32[]{:S(2)}, u32[]{:S(2)}) async-start(bf16[1,16,8,10,2880]{4,1,3,0,2:T(8,128)(2,1)} %copy.96), calls=%async_computation | async-start | bytes 15073280 | tf_op jit(solution)/shard_map/all_to_all | solution.py:75
  19.1 138.5 %all-gather.6.cloned.1.call-start = ((), (), s32[]{:S(2)}) async-start(), calls=%async_computation.3 | async-start | bytes 7603200 | tf_op jit(solution)/shard_map/all_gather | solution.py:96
  20.1 181.9 %all-gather.4.cloned.1.call-start = ((), (), s32[]{:S(2)}) async-start(), calls=%async_computation.2 | async-start | bytes 6635520 | tf_op jit(solution)/shard_map/all_gather | solution.py:92
  150.7 2.2 copy-start.2
  152.9 0.8 copy-start.11
  152.9 3.2 copy-start.9
  152.9 3.2 copy-start.14
  155.1 128.9 %all-gather.8.cloned.1.call-start = ((), (), s32[]{:S(2)}) async-start(), calls=%async_computation.4 | async-start | bytes 3108864 | tf_op jit(solution)/shard_map/all_gather | solution.py:97
  155.8 185.8 %reduce-scatter.4.cloned.1.call-start = ((), (), s32[]{:S(2)}) async-start(), calls=%async_computation.5 | async-start | bytes 6782976
  210.6 4.6 %copy-start.10 = (bf16[1024,1,640]{0,2,1:T(8,128)(2,1)}, bf16[1024,1,640]{0,2,1:T(8,128)(2,1)S(1)}, u32[]{:S(2)}) copy-start(bf16[1024,1,640]{0,2,1:T(8,128)(2,1)S(1)} %get-tuple-element.27) | copy-start | bytes 3932164
  211.3 8.0 %copy-start = (bf16[1024,1,32]{0,2,1:T(8,128)(2,1)}, bf16[1024,1,32]{0,2,1:T(8,128)(2,1)S(1)}, u32[]{:S(2)}) copy-start(bf16[1024,1,32]{0,2,1:T(8,128)(2,1)S(1)} %get-tuple-element.10) | copy-start | bytes 196612
  211.3 7.9 %collective-permute-start = (bf16[128,1,128]{0,2,1:T(8,128)(2,1)S(1)}, bf16[128,1,128]{0,2,1:T(8,128)(2,1)S(1)}, u32[]{:S(2)}, u32[]{:S(2)}) collective-permute-start(bf16[128,1,128]{0,2,1:T(8,128)(2,1)S(1)} %pad_maximum_fusion.8), channel_id=1, source_target_pairs={{0,8},{8,16},{16,24},{24,32},{32,40},{40,48},{48,56},{56,64},{64,7... | collective-permute-start | bytes 98312 | tf_op jit(solution)/shard_map/ppermute | solution.py:19
  216.9 4.1 %copy-start.13 = (f32[1,8]{1,0:T(1,128)S(1)}, f32[1,8]{1,0:T(1,128)}, u32[]{:S(2)}) copy-start(f32[1,8]{1,0:T(1,128)} %param.21) | copy-start | bytes 100
  219.2 1.8 copy-start.6
  226.5 4.3 %copy-start.4 = (f32[8,512]{1,0:T(8,128)S(1)}, f32[8,512]{1,0:T(8,128)}, u32[]{:S(2)}) copy-start(f32[8,512]{1,0:T(8,128)} %get-tuple-element.26) | copy-start | bytes 49156
  230.9 4.3 %copy-start.1 = (bf16[1024,1,32]{0,2,1:T(8,128)(2,1)S(1)}, bf16[1024,1,32]{0,2,1:T(8,128)(2,1)}, u32[]{:S(2)}) copy-start(bf16[1024,1,32]{0,2,1:T(8,128)(2,1)} %copy-done) | copy-start | bytes 196612
  230.9 4.3 %copy-start.5 = (f32[8,512]{1,0:T(8,128)S(1)}, f32[8,512]{1,0:T(8,128)}, u32[]{:S(2)}) copy-start(f32[8,512]{1,0:T(8,128)} %broadcast_maximum_fusion.1) | copy-start | bytes 49156
  230.9 4.3 %copy-start.7 = (bf16[128,1,128]{0,2,1:T(8,128)(2,1)S(1)}, bf16[128,1,128]{0,2,1:T(8,128)(2,1)}, u32[]{:S(2)}) copy-start(bf16[128,1,128]{0,2,1:T(8,128)(2,1)} %copy-done.6) | copy-start | bytes 98308
  230.9 4.3 %copy-start.8 = (f32[8,512]{1,0:T(8,128)S(1)}, f32[8,512]{1,0:T(8,128)}, u32[]{:S(2)}) copy-start(f32[8,512]{1,0:T(8,128)} %get-tuple-element.25) | copy-start | bytes 49156
  299.6 43.6 %copy-start.12 = (f32[2880]{0:T(1024)S(1)}, f32[2880]{0:T(1024)}, u32[]{:S(2)}) copy-start(f32[2880]{0:T(1024)} %param.23) | copy-start | bytes 34564
Sparse Core Ops, SparseCore 0:
  22.6 95.4 all-gather.5
  155.2 46.7 all-gather.3
  204.6 79.3 all-gather.7
  299.7 41.8 reduce-scatter.3
where the time goes:
time: 352 us; the launch traced here: 351 us
  waiting for transfers between devices  219 us (62%)
  local copies, waits for them, and re-layouts  65 us (18%)
  matrix products  26.4 us (8%)
  other arithmetic  17.9 us (5%)
  between operations  13.6 us (4%)
  starting transfers between devices  8.87 us (3%)
    all_to_all x1, waiting for transfers between devices, shards(): lax.all_to_all(expert_rows, 'expert', split_axis=2, concat_axis=1, tiled=...  84.2 us
    all_gather x1, waiting for transfers between devices, shards(): lax.all_gather(output_weight, 'fsdp', axis=1, tiled=True)  45.6 us
    all_gather x1, waiting for transfers between devices, shards(): gathered = lax.all_gather(normalized_rows, 'expert', axis=0, tiled=True)  44.4 us
    unnamed x5, waiting for transfers between devices  42.8 us
    gather x3, local copies, waits for them, and re-layouts, shards(): jnp.take(slot_table, flat_index, axis=0)  19.7 us
    unnamed x40, local copies, waits for them, and re-layouts  18.5 us
    reshape x1, local copies, waits for them, and re-layouts, shards(): slot_table = returned.reshape(-1, model_width)  14.4 us
    all_to_all x1, local copies, waits for them, and re-layouts, shards(): lax.all_to_all(expert_rows, 'expert', split_axis=2, concat_axis=1, tiled=...  12.1 us
  transfers between devices with their start and end apart: 6, of which 5 were waited for; matrix products, arithmetic and copies ran while one was open for 24% of the time, Pallas kernels for 0%

commit v1 on v0

--- a/solution.py
+++ b/solution.py
@@ -73,15 +73,19 @@
     own_rows = residual.shape[0]
     model_width = residual.shape[1]
     returned = lax.all_to_all(expert_rows, "expert", split_axis=2, concat_axis=1, tiled=True)
+    all_experts = returned.shape[1]
     capacity = returned.shape[3]
-    slot_table = returned.reshape(-1, model_width)
-    flat_index = (route_ids * capacity + route_slots).reshape(-1)
-    picked = jnp.take(slot_table, flat_index, axis=0).reshape(own_rows, TOPK, model_width)
-    combined = route_weights[:, 0:1] * picked[:, 0].astype(jnp.float32)
-    for route_number in range(1, TOPK):
-        combined = combined + route_weights[:, route_number : route_number + 1] * picked[
-            :, route_number
-        ].astype(jnp.float32)
+    hit_expert = route_ids[..., None] == jnp.arange(all_experts, dtype=jnp.int32)
+    hit_slot = route_slots[..., None] == jnp.arange(capacity, dtype=jnp.int32)
+    hits = hit_expert[..., :, None] & hit_slot[..., None, :]
+    select = jnp.sum(jnp.where(hits, route_weights[..., None, None], 0.0), axis=1)
+    high = select.astype(jnp.bfloat16)
+    low = (select - high.astype(jnp.float32)).astype(jnp.bfloat16)
+    both = jnp.concatenate([high, low], axis=0)
+    picked = jnp.einsum(
+        "txs,xsm->tm", both, returned[0, :, 0], preferred_element_type=jnp.float32
+    )
+    combined = picked[:own_rows] + picked[own_rows:]
     hidden = (residual.astype(jnp.float32) + combined).astype(jnp.bfloat16)
     widened = hidden.astype(jnp.float32)
     normalized_rows = (

time: 352 us -> 314 us (0.89)
  local copies, waits for them, and re-layouts: 65 us -> 22.6 us
    gather x3 -> x0, local copies, waits for them, and re-layouts: 19.7 us -> none  [shards(): jnp.take(slot_table, flat_index, axis=0)]
    reshape x2 -> x0, local copies, waits for them, and re-layouts: 14.5 us -> none  [the longest x1 14.4 us: shards(): slot_table = returned.reshape(-1, model_width)]
    all_to_all x1, local copies, waits for them, and re-layouts: 12.1 us -> 3.87 us  [shards(): lax.all_to_all(expert_rows, 'expert', split_axis=2, concat_axis=1, tiled=...]
  transfers between devices with their start and end apart: 6 -> 6, of which waited for: 5 -> 6; matrix products, arithmetic and copies ran while one was open for 24% -> 14% of each run, Pallas kernels for 0% -> 0%
where the time goes in v1:
time: 314 us; the launch traced here: 313 us
  waiting for transfers between devices  222 us (71%)
  matrix products  29.6 us (9%)
  local copies, waits for them, and re-layouts  22.6 us (7%)
  other arithmetic  16.7 us (5%)
  between operations  13.6 us (4%)
  starting transfers between devices  8.81 us (3%)
    all_to_all x1, waiting for transfers between devices, shards(): lax.all_to_all(expert_rows, 'expert', split_axis=2, concat_axis=1, tiled=...  83 us
    all_gather x1, waiting for transfers between devices, shards(): gathered = lax.all_gather(normalized_rows, 'expert', axis=0, tiled=True)  46.1 us
    all_gather x1, waiting for transfers between devices, shards(): lax.all_gather(output_weight, 'fsdp', axis=1, tiled=True)  45.6 us
    unnamed x5, waiting for transfers between devices  42.8 us
    unnamed x40, local copies, waits for them, and re-layouts  18.5 us
    dot_general x1, matrix products, shards(): jnp.dot(gathered, qkv_full.reshape(model_width, -1), preferred_element_ty...  8.51 us
    dot_general x2, matrix products, attend_block(): jnp.einsum('jgqk,kjd->qjgd', weights_soft, values_only, preferred_element...  7.33 us
    dot_general x1, matrix products, shards(): jnp.dot(attention_result, output_weights, preferred_element_type=jnp.floa...  7 us
  transfers between devices with their start and end apart: 6, of which 6 were waited for; matrix products, arithmetic and copies ran while one was open for 14% of the time, Pallas kernels for 0%

profile of v1, /device:TPU:2, one launch (start us, length us, event | category | flops | bytes accessed | tf_op | source)
XLA Modules:
  0.0 313.1 jit_solution(7532244793137862492)
XLA Ops:
  6.5 7.6 %copy.53 = bf16[1,16,8,10,2880]{4,1,3,0,2:T(8,128)(2,1)} copy(bf16[1,16,8,10,2880]{4,2,3,1,0:T(8,128)(2,1)} %param.12) | data formatting | bytes 14745600 | tf_op args[0]
  14.2 5.0 %all-to-all-start = ((bf16[1,16,8,10,2880]{4,1,3,0,2:T(8,128)(2,1)}), bf16[1,16,8,10,2880]{4,1,3,0,2:T(8,128)(2,1)}, u32[]{:S(2)}, u32[]{:S(2)}) async-start(bf16[1,16,8,10,2880]{4,1,3,0,2:T(8,128)(2,1)} %copy.53), calls=%async_computation | async-start | bytes 15073280 | tf_op jit(solution)/shard_map/all_to_all | solution.py:75
  19.2 0.0 all-gather.6.cloned.1.call-start
  19.2 0.0 copy-done.3
  19.2 0.9 copy.56
  20.1 0.0 all-gather.6.cloned.1.call-update
  20.1 0.0 all-gather.4.cloned.1.call-start
  20.2 0.0 copy-done.16
  20.2 0.0 copy-done.17
  20.2 0.1 iota_compare_fusion
  20.4 0.0 copy-done.15
  20.4 1.1 select_reduce_fusion
  21.5 0.1 subtract_convert_fusion.1
  21.6 83.0 %all-to-all-done = bf16[1,16,8,10,2880]{4,1,3,0,2:T(8,128)(2,1)} async-done(((bf16[1,16,8,10,2880]{4,1,3,0,2:T(8,128)(2,1)}), bf16[1,16,8,10,2880]{4,1,3,0,2:T(8,128)(2,1)}, u32[]{:S(2)}, u32[]{:S(2)}) %all-to-all-start) | async-done | bytes 7372832 | tf_op jit(solution)/shard_map/all_to_all | solution.py:75
  104.7 3.9 %copy.54 = bf16[1,8,16,1,10,2880]{5,2,1,4,3,0:T(8,128)(2,1)S(1)} copy(bf16[1,8,16,1,10,2880]{5,2,4,1,3,0:T(8,128)(2,1)} %bitcast.1) | data formatting | bytes 14745600 | tf_op jit(solution)/shard_map/all_to_all | solution.py:75
  108.5 0.0 copy-start.2
  108.6 0.0 copy-start.11
  108.6 3.2 %convolution_bitcast_fusion = f32[256,2880]{0,1:T(8,128)S(1)} fusion(bf16[128,10,2880]{2,0,1:T(8,128)(2,1)S(1)} %bitcast.112, bf16[128,128,10]{1,0,2:T(8,128)(2,1)S(1)} %get-tuple-element.7, bf16[128,128,10]{1,0,2:T(8,128)(2,1)S(1)} %get-tuple-element.8), kind=kOutput, calls=%fused_computation.15 | convolution fusion | flops 1888747520 | bytes 10977280 | tf_op jit(solution)/shard_map/txs,xsm->tm/dot_general | solution.py:85
  111.8 0.0 copy-done.2
  111.8 0.0 copy-start.9
  111.8 0.0 copy-start.14
  111.8 0.4 fusion.14
  112.2 1.3 fusion.16
  113.6 0.0 all-gather.4.cloned.1.call-update
  113.6 0.0 all-gather.8.cloned.1.call-start
  113.6 0.7 all-gather.8.cloned.1.call-update
  114.3 0.0 reduce-scatter.4.cloned.1.call-start
  114.5 0.5 multiply_cosine_fusion
  115.0 0.4 compare_and_fusion
  115.4 0.4 compare_and_fusion.1
  115.9 2.2 all-gather.6.cloned.1.call-done
  118.1 46.1 %all-gather.4.cloned.1.call-done = bf16[1024,2880]{0,1:T(8,128)(2,1)} async-done(((bf16[128,2880]{0,1:T(8,128)(2,1)}), bf16[1024,2880]{0,1:T(8,128)(2,1)}) %all-gather.4.cloned.1.call-update) | async-done | bytes 5898256 | tf_op jit(solution)/shard_map/all_gather | solution.py:96
  164.2 8.5 %fusion.75 = (bf16[1024,1,640]{0,2,1:T(8,128)(2,1)S(1)}, f32[1024,1,640]{0,2,1:T(8,128)S(1)}) fusion(f32[640]{0:T(1024)S(1)} %reduce.4, bf16[1024,2880]{0,1:T(8,128)(2,1)} %all-gather.4.cloned.1.call-done, bf16[2880,1,640]{2,1,0:T(2,128)(2,1)} %all-gather.6.cloned.1.call-done), kind=kOutput, calls=%fused_computation.109 | convolution fusion | flops 3776184320 | bytes 13519360 | tf_op jit(solution)/shard_map/dot_general | solution.py:103
  172.7 0.0 copy-start.10
  172.7 0.1 slice.94
  172.8 0.6 fusion.49
  173.4 0.0 copy-start
  173.4 3.6 %collective-permute-start = (bf16[128,1,128]{0,2,1:T(8,128)(2,1)S(1)}, bf16[128,1,128]{0,2,1:T(8,128)(2,1)S(1)}, u32[]{:S(2)}, u32[]{:S(2)}) collective-permute-start(bf16[128,1,128]{0,2,1:T(8,128)(2,1)S(1)} %pad_maximum_fusion.8), channel_id=1, source_target_pairs={{0,8},{8,16},{16,24},{24,32},{32,40},{40,48},{48,56},{56,64},{64,7... | collective-permute-start | bytes 98312 | tf_op jit(solution)/shard_map/ppermute | solution.py:19
  177.1 0.3 subtract_convert_fusion
  177.4 1.7 fusion.3
  179.2 0.0 copy-start.13
  179.2 2.2 collective-permute-done
  181.4 0.0 copy-done
  181.4 1.8 fusion.2
  183.2 0.7 broadcast_maximum_fusion.1
  183.8 3.5 %fusion = f32[8,512]{1,0:T(8,128)} fusion(f32[640,512,8]{1,0,2:T(8,128)S(1)} %get-tuple-element.26, f32[8,512]{1,0:T(8,128)} %broadcast_maximum_fusion.1, pred[512,640]{0,1:T(8,128)(4,1)S(1)} %compare_and_fusion.1), kind=kLoop, calls=%fused_computation.6 | loop fusion | flops 10481664 | bytes 10846208 | tf_op jit(solution)/shard_map/reduce_sum | solution.py:52
  187.3 1.4 exponential_add_fusion.1
  188.7 3.5 %fusion.1 = f32[8,512]{1,0:T(8,128)} fusion(f32[640,512,8]{1,0,2:T(8,128)S(1)} %get-tuple-element.28, f32[8,512]{1,0:T(8,128)} %get-tuple-element.22, pred[512,640]{0,1:T(8,128)(4,1)S(1)} %compare_and_fusion), kind=kLoop, calls=%fused_computation.7 | loop fusion | flops 10481664 | bytes 10846208 | tf_op jit(solution)/shard_map/reduce_sum | solution.py:52
  192.2 0.8 exponential_add_fusion
  193.0 0.0 copy-start.1
  193.0 0.0 copy-start.5
  193.0 0.0 copy-start.7
  193.0 0.0 copy-start.8
  193.0 4.2 %fusion.27 = bf16[512,1,8,64]{0,3,2,1:T(8,128)(2,1)S(1)} fusion(f32[8,512]{1,0:T(8,128)S(1)} %exponential_add_fusion, f32[8,512]{1,0:T(8,128)S(1)} %copy-done.4, f32[640,512,8]{1,0,2:T(8,128)S(1)} %get-tuple-element.28, pred[512,640]{0,1:T(8,128)(4,1)S(1)} %compare_and_fusion, bf16[1024,1,640]{0,2,1:T(8,128)(2,1)} %copy-done.10), kind=kOutput, calls=%fused_computation.37 | convolution fusion | flops 348913664 | bytes 11452416 | tf_op jit(solution)/shard_map/jgqk,kjd->qjgd/dot_general | solution.py:54
  197.3 3.1 fusion.30
  200.4 0.1 pad_maximum_fusion
  200.6 45.6 %all-gather.8.cloned.1.call-done = bf16[1,512,2880]{2,1,0:T(8,128)(2,1)} async-done(((bf16[1,16,2880]{2,1,0:T(8,128)(2,1)}), bf16[1,512,2880]{2,1,0:T(8,128)(2,1)}) %all-gather.8.cloned.1.call-update) | async-done | bytes 2949136 | tf_op jit(solution)/shard_map/all_gather | solution.py:101
  246.2 7.0 %convolution_convert_fusion = bf16[1024,2880]{0,1:T(8,128)(2,1)} fusion(bf16[1024,512]{0,1:T(8,128)(2,1)S(1)} %bitcast.113, bf16[1,512,2880]{2,1,0:T(8,128)(2,1)} %all-gather.8.cloned.1.call-done), kind=kOutput, calls=%fused_computation.10 | convolution fusion | flops 3022848000 | bytes 9895936 | tf_op jit(solution)/shard_map/dot_general | solution.py:148
  253.2 8.5 %copy.62 = bf16[1024,2880]{1,0:T(8,128)(2,1)} copy(bf16[1024,2880]{0,1:T(8,128)(2,1)} %convolution_convert_fusion) | data formatting | bytes 11796480
  261.6 0.0 reduce-scatter.4.cloned.1.call-update
  261.7 42.1 %reduce-scatter.4.cloned.1.call-done = bf16[128,2880]{1,0:T(8,128)(2,1)} async-done(((bf16[1024,2880]{1,0:T(8,128)(2,1)}), bf16[128,2880]{1,0:T(8,128)(2,1)}) %reduce-scatter.4.cloned.1.call-update) | async-done | bytes 737296
  303.7 1.5 copy.63
  305.2 0.0 copy-done.12
  305.2 1.3 fusion.18
  (29 shorter events, 0.1 us)
Async XLA Ops:
  14.2 5.1 %copy-start.3 = (bf16[90,1,640]{2,0,1:T(8,128)(2,1)S(1)}, bf16[90,1,640]{2,0,1:T(8,128)(2,1)}, u32[]{:S(2)}) copy-start(bf16[90,1,640]{2,0,1:T(8,128)(2,1)} %param.19) | copy-start | bytes 345604
  14.2 6.0 %copy-start.16 = (s32[128,4]{0,1:T(4,128)S(1)}, s32[128,4]{0,1:T(4,128)}, u32[]{:S(2)}) copy-start(s32[128,4]{0,1:T(4,128)} %param.16) | copy-start | bytes 6148
  14.2 6.1 %copy-start.17 = (s32[128,4]{0,1:T(4,128)S(1)}, s32[128,4]{0,1:T(4,128)}, u32[]{:S(2)}) copy-start(s32[128,4]{0,1:T(4,128)} %param.14) | copy-start | bytes 6148
  14.2 6.2 %copy-start.15 = (f32[128,4]{0,1:T(4,128)S(1)}, f32[128,4]{0,1:T(4,128)}, u32[]{:S(2)}) copy-start(f32[128,4]{0,1:T(4,128)} %param.15) | copy-start | bytes 6148
  14.2 90.5 %all-to-all-start = ((bf16[1,16,8,10,2880]{4,1,3,0,2:T(8,128)(2,1)}), bf16[1,16,8,10,2880]{4,1,3,0,2:T(8,128)(2,1)}, u32[]{:S(2)}, u32[]{:S(2)}) async-start(bf16[1,16,8,10,2880]{4,1,3,0,2:T(8,128)(2,1)} %copy.53), calls=%async_computation | async-start | bytes 15073280 | tf_op jit(solution)/shard_map/all_to_all | solution.py:75
  19.2 98.9 %all-gather.6.cloned.1.call-start = ((), (), s32[]{:S(2)}) async-start(), calls=%async_computation.3 | async-start | bytes 7603200 | tf_op jit(solution)/shard_map/all_gather | solution.py:100
  20.1 144.0 %all-gather.4.cloned.1.call-start = ((), (), s32[]{:S(2)}) async-start(), calls=%async_computation.2 | async-start | bytes 6635520 | tf_op jit(solution)/shard_map/all_gather | solution.py:96
  108.5 3.3 %copy-start.2 = (bf16[128,2880]{0,1:T(8,128)(2,1)S(1)}, bf16[128,2880]{0,1:T(8,128)(2,1)}, u32[]{:S(2)}) copy-start(bf16[128,2880]{0,1:T(8,128)(2,1)} %param.13) | copy-start | bytes 2211844
  108.6 3.7 %copy-start.11 = (f32[2880]{0:T(1024)S(1)}, f32[2880]{0:T(1024)}, u32[]{:S(2)}) copy-start(f32[2880]{0:T(1024)} %param.18) | copy-start | bytes 34564
  111.8 2.6 copy-start.9
  111.8 2.7 copy-start.14
  113.6 132.6 %all-gather.8.cloned.1.call-start = ((), (), s32[]{:S(2)}) async-start(), calls=%async_computation.4 | async-start | bytes 3108864 | tf_op jit(solution)/shard_map/all_gather | solution.py:101
  114.3 189.4 %reduce-scatter.4.cloned.1.call-start = ((), (), s32[]{:S(2)}) async-start(), calls=%async_computation.5 | async-start | bytes 6782976
  172.7 4.8 %copy-start.10 = (bf16[1024,1,640]{0,2,1:T(8,128)(2,1)}, bf16[1024,1,640]{0,2,1:T(8,128)(2,1)S(1)}, u32[]{:S(2)}) copy-start(bf16[1024,1,640]{0,2,1:T(8,128)(2,1)S(1)} %get-tuple-element.23) | copy-start | bytes 3932164
  173.4 8.0 %copy-start = (bf16[1024,1,32]{0,2,1:T(8,128)(2,1)}, bf16[1024,1,32]{0,2,1:T(8,128)(2,1)S(1)}, u32[]{:S(2)}) copy-start(bf16[1024,1,32]{0,2,1:T(8,128)(2,1)S(1)} %get-tuple-element.10) | copy-start | bytes 196612
  173.4 7.9 %collective-permute-start = (bf16[128,1,128]{0,2,1:T(8,128)(2,1)S(1)}, bf16[128,1,128]{0,2,1:T(8,128)(2,1)S(1)}, u32[]{:S(2)}, u32[]{:S(2)}) collective-permute-start(bf16[128,1,128]{0,2,1:T(8,128)(2,1)S(1)} %pad_maximum_fusion.8), channel_id=1, source_target_pairs={{0,8},{8,16},{16,24},{24,32},{32,40},{40,48},{48,56},{56,64},{64,7... | collective-permute-start | bytes 98312 | tf_op jit(solution)/shard_map/ppermute | solution.py:19
  179.2 4.0 %copy-start.13 = (f32[1,8]{1,0:T(1,128)S(1)}, f32[1,8]{1,0:T(1,128)}, u32[]{:S(2)}) copy-start(f32[1,8]{1,0:T(1,128)} %param.21) | copy-start | bytes 100
  181.4 1.8 copy-start.6
  188.7 4.3 %copy-start.4 = (f32[8,512]{1,0:T(8,128)S(1)}, f32[8,512]{1,0:T(8,128)}, u32[]{:S(2)}) copy-start(f32[8,512]{1,0:T(8,128)} %get-tuple-element.22) | copy-start | bytes 49156
  193.0 4.3 %copy-start.1 = (bf16[1024,1,32]{0,2,1:T(8,128)(2,1)S(1)}, bf16[1024,1,32]{0,2,1:T(8,128)(2,1)}, u32[]{:S(2)}) copy-start(bf16[1024,1,32]{0,2,1:T(8,128)(2,1)} %copy-done) | copy-start | bytes 196612
  193.0 4.3 %copy-start.5 = (f32[8,512]{1,0:T(8,128)S(1)}, f32[8,512]{1,0:T(8,128)}, u32[]{:S(2)}) copy-start(f32[8,512]{1,0:T(8,128)} %broadcast_maximum_fusion.1) | copy-start | bytes 49156
  193.0 4.3 %copy-start.7 = (bf16[128,1,128]{0,2,1:T(8,128)(2,1)S(1)}, bf16[128,1,128]{0,2,1:T(8,128)(2,1)}, u32[]{:S(2)}) copy-start(bf16[128,1,128]{0,2,1:T(8,128)(2,1)} %copy-done.6) | copy-start | bytes 98308
  193.0 4.3 %copy-start.8 = (f32[8,512]{1,0:T(8,128)S(1)}, f32[8,512]{1,0:T(8,128)}, u32[]{:S(2)}) copy-start(f32[8,512]{1,0:T(8,128)} %get-tuple-element.21) | copy-start | bytes 49156
  261.6 43.6 %copy-start.12 = (f32[2880]{0:T(1024)S(1)}, f32[2880]{0:T(1024)}, u32[]{:S(2)}) copy-start(f32[2880]{0:T(1024)} %param.23) | copy-start | bytes 34564
Sparse Core Ops, SparseCore 0:
  22.6 95.4 all-gather.5
  119.9 44.1 all-gather.3
  166.8 79.3 all-gather.7
  261.8 41.8 reduce-scatter.3

commit v2 on v1

--- a/solution.py
+++ b/solution.py
@@ -56,6 +56,12 @@
     ).astype(jnp.bfloat16)
 
 
+def gather_fsdp(block):
+    count = lax.axis_size("fsdp")
+    spread = jnp.broadcast_to(block[None], (count,) + block.shape)
+    return lax.all_to_all(spread, "fsdp", split_axis=0, concat_axis=0, tiled=True)
+
+
 def shards(
     expert_rows,
     residual,
@@ -73,6 +79,8 @@
     own_rows = residual.shape[0]
     model_width = residual.shape[1]
     returned = lax.all_to_all(expert_rows, "expert", split_axis=2, concat_axis=1, tiled=True)
+    qkv_full = lax.all_gather(projection_weight, "fsdp", axis=0, tiled=True)
+    qkv_full, returned = lax.optimization_barrier((qkv_full, returned))
     all_experts = returned.shape[1]
     capacity = returned.shape[3]
     hit_expert = route_ids[..., None] == jnp.arange(all_experts, dtype=jnp.int32)
@@ -94,12 +102,10 @@
         * norm_gain
     ).astype(jnp.bfloat16)
     gathered = lax.all_gather(normalized_rows, "expert", axis=0, tiled=True)
+    out_full = gather_fsdp(output_weight[0])
+    out_full, gathered = lax.optimization_barrier((out_full, gathered))
     block_rows = gathered.shape[0]
     local_heads = projection_weight.shape[1]
-    qkv_full, out_full = (
-        lax.all_gather(projection_weight, "fsdp", axis=0, tiled=True),
-        lax.all_gather(output_weight, "fsdp", axis=1, tiled=True),
-    )
     projected_rows = jnp.dot(
         gathered, qkv_full.reshape(model_width, -1), preferred_element_type=jnp.float32
     )

time: 314 us -> 306 us (0.975)
  waiting for transfers between devices: 222 us -> 194 us
  starting transfers between devices: 8.81 us -> 19.4 us
  local copies, waits for them, and re-layouts: 22.6 us -> 28.3 us
    all_to_all x0 -> x1, waiting for transfers between devices: none -> 67.5 us  [gather_fsdp(): lax.all_to_all(spread, 'fsdp', split_axis=0, concat_axis=0, tiled=True)]
    all_gather x2 -> x1, waiting for transfers between devices: 47.8 us -> 0.01 us  [shards(): qkv_full = lax.all_gather(projection_weight, 'fsdp', axis=0, tiled=True)]
    all_gather x1, waiting for transfers between devices: 46.1 us -> 0.01 us  [shards(): gathered = lax.all_gather(normalized_rows, 'expert', axis=0, tiled=True)]
    all_to_all x0 -> x1, starting transfers between devices: none -> 11.7 us  [gather_fsdp(): lax.all_to_all(spread, 'fsdp', split_axis=0, concat_axis=0, tiled=True)]
    unnamed x5 -> x4, waiting for transfers between devices: 42.8 us -> 39.3 us
  transfers between devices with their start and end apart: 6 -> 6, of which waited for: 6 -> 4; matrix products, arithmetic and copies ran while one was open for 14% -> 7% of each run, Pallas kernels for 0% -> 0%
where the time goes in v2:
time: 306 us; the launch traced here: 305 us
  waiting for transfers between devices  194 us (63%)
  matrix products  32.7 us (11%)
  local copies, waits for them, and re-layouts  28.3 us (9%)
  starting transfers between devices  19.4 us (6%)
  other arithmetic  16.7 us (5%)
  between operations  13.5 us (4%)
    all_to_all x1, waiting for transfers between devices, shards(): lax.all_to_all(expert_rows, 'expert', split_axis=2, concat_axis=1, tiled=...  84 us
    all_to_all x1, waiting for transfers between devices, gather_fsdp(): lax.all_to_all(spread, 'fsdp', split_axis=0, concat_axis=0, tiled=True)  67.5 us
    unnamed x4, waiting for transfers between devices  39.3 us
    unnamed x40, local copies, waits for them, and re-layouts  19.5 us
    all_to_all x1, starting transfers between devices, gather_fsdp(): lax.all_to_all(spread, 'fsdp', split_axis=0, concat_axis=0, tiled=True)  11.7 us
    dot_general x1, matrix products, shards(): jnp.dot(gathered, qkv_full.reshape(model_width, -1), preferred_element_ty...  8.51 us
    dot_general x2, matrix products, attend_block(): jnp.einsum('jgqk,kjd->qjgd', weights_soft, values_only, preferred_element...  7.33 us
    dot_general x1, matrix products, shards(): jnp.dot(attention_result, output_weights, preferred_element_type=jnp.floa...  7.03 us
  transfers between devices with their start and end apart: 6, of which 4 were waited for; matrix products, arithmetic and copies ran while one was open for 7% of the time, Pallas kernels for 0%

profile of v2, /device:TPU:2, one launch (start us, length us, event | category | flops | bytes accessed | tf_op | source)
XLA Modules:
  0.0 304.9 jit_solution(17909378280636249586)
XLA Ops:
  6.5 0.0 all-gather.3.cloned.1.call-start
  6.5 1.8 copy.52
  8.3 0.0 all-gather.3.cloned.1.call-update
  8.3 7.6 %copy.53 = bf16[1,16,8,10,2880]{4,1,3,0,2:T(8,128)(2,1)} copy(bf16[1,16,8,10,2880]{4,2,3,1,0:T(8,128)(2,1)} %param.12) | data formatting | bytes 14745600 | tf_op args[0]
  15.9 5.0 %all-to-all-start = ((bf16[1,16,8,10,2880]{4,1,3,0,2:T(8,128)(2,1)}), bf16[1,16,8,10,2880]{4,1,3,0,2:T(8,128)(2,1)}, u32[]{:S(2)}, u32[]{:S(2)}) async-start(bf16[1,16,8,10,2880]{4,1,3,0,2:T(8,128)(2,1)} %copy.53), calls=%async_computation | async-start | bytes 15073280 | tf_op jit(solution)/shard_map/all_to_all | solution.py:81
  21.0 0.0 all-gather.5.cloned.1.call-start
  21.0 0.0 copy-done.16
  21.0 0.0 copy-done.17
  21.1 0.1 iota_compare_fusion
  21.2 0.0 copy-done.15
  21.2 1.1 select_reduce_fusion
  22.3 0.1 subtract_convert_fusion.1
  22.5 84.0 %all-to-all-done = bf16[1,16,8,10,2880]{4,1,3,0,2:T(8,128)(2,1)} async-done(((bf16[1,16,8,10,2880]{4,1,3,0,2:T(8,128)(2,1)}), bf16[1,16,8,10,2880]{4,1,3,0,2:T(8,128)(2,1)}, u32[]{:S(2)}, u32[]{:S(2)}) %all-to-all-start) | async-done | bytes 7372832 | tf_op jit(solution)/shard_map/all_to_all | solution.py:81
  106.5 6.9 %copy.54 = bf16[1,8,16,1,10,2880]{5,2,1,4,3,0:T(8,128)(2,1)} copy(bf16[1,8,16,1,10,2880]{5,2,4,1,3,0:T(8,128)(2,1)} %bitcast.1) | data formatting | bytes 14745600 | tf_op jit(solution)/shard_map/all_to_all | solution.py:81
  113.3 6.3 %fusion.10 = f32[256,2880]{0,1:T(8,128)S(1)} fusion(bf16[1,128,1,10,2880]{4,1,3,2,0:T(8,128)(2,1)} %bitcast.116, bf16[128,128,10]{1,0,2:T(8,128)(2,1)S(1)} %get-tuple-element.15, bf16[128,128,10]{1,0,2:T(8,128)(2,1)S(1)} %get-tuple-element.16), kind=kOutput, calls=%fused_computation.17 | convolution fusion | flops 1888747520 | bytes 10977280 | tf_op jit(solution)/shard_map/txs,xsm->tm/dot_general | solution.py:93
  119.7 0.0 copy-done.2
  119.7 0.0 copy-start.3
  119.7 0.4 fusion.18
  120.1 0.0 copy-start.9
  120.1 0.0 copy-done.11
  120.1 1.3 fusion.20
  121.4 0.0 all-gather.5.cloned.1.call-update
  121.5 0.0 copy-done.3
  121.5 1.9 broadcast_in_dim.33
  123.3 11.7 %all-to-all-start.1 = ((bf16[32,16,2880]{2,1,0:T(8,128)(2,1)}), bf16[32,16,2880]{2,1,0:T(8,128)(2,1)}, u32[]{:S(2)}, u32[]{:S(2)}) async-start(bf16[32,16,2880]{2,1,0:T(8,128)(2,1)} %broadcast_in_dim.33), calls=%async_computation.1 | async-start | bytes 6029312 | tf_op jit(solution)/shard_map/all_to_all | solution.py:62
  135.0 0.2 reduce-scatter.4.cloned.1.call-start
  135.3 0.0 copy-done.14
  135.3 0.0 copy-done.9
  135.4 0.5 multiply_cosine_fusion
  135.9 0.4 compare_and_fusion
  136.3 0.4 compare_and_fusion.1
  136.7 67.5 %all-to-all-done.1 = bf16[32,16,2880]{2,1,0:T(8,128)(2,1)} async-done(((bf16[32,16,2880]{2,1,0:T(8,128)(2,1)}), bf16[32,16,2880]{2,1,0:T(8,128)(2,1)}, u32[]{:S(2)}, u32[]{:S(2)}) %all-to-all-start.1) | async-done | bytes 2949152 | tf_op jit(solution)/shard_map/all_to_all | solution.py:62
  204.3 8.5 %fusion.79 = (bf16[1024,1,640]{0,2,1:T(8,128)(2,1)S(1)}, f32[1024,1,640]{0,2,1:T(8,128)S(1)}) fusion(f32[640]{0:T(1024)S(1)} %reduce.4, bf16[1024,2880]{0,1:T(8,128)(2,1)} %all-gather.5.cloned.1.call-done, bf16[2880,1,640]{2,1,0:T(2,128)(2,1)} %all-gather.3.cloned.1.call-done), kind=kOutput, calls=%fused_computation.110 | convolution fusion | flops 3776184320 | bytes 13519360 | tf_op jit(solution)/shard_map/dot_general | solution.py:109
  212.8 0.0 copy-start.10
  212.8 0.1 slice.94
  213.0 0.6 fusion.53
  213.5 0.0 copy-start
  213.6 2.5 collective-permute-start
  216.1 0.3 subtract_convert_fusion
  216.4 0.0 copy-done.10
  216.4 1.7 fusion.3
  218.2 0.0 copy-start.13
  218.2 3.3 %collective-permute-done = bf16[128,1,128]{0,2,1:T(8,128)(2,1)S(1)} collective-permute-done((bf16[128,1,128]{0,2,1:T(8,128)(2,1)S(1)}, bf16[128,1,128]{0,2,1:T(8,128)(2,1)S(1)}, u32[]{:S(2)}, u32[]{:S(2)}) %collective-permute-start) | collective-permute-done | bytes 32800 | tf_op jit(solution)/shard_map/ppermute | solution.py:19
  221.5 0.0 copy-done
  221.5 1.8 fusion.2
  223.3 0.0 copy-done.6
  223.3 0.0 copy-done.13
  223.3 0.7 broadcast_maximum_fusion.1
  224.0 3.5 %fusion = f32[8,512]{1,0:T(8,128)} fusion(f32[640,512,8]{1,0,2:T(8,128)S(1)} %get-tuple-element.34, f32[8,512]{1,0:T(8,128)} %broadcast_maximum_fusion.1, pred[512,640]{0,1:T(8,128)(4,1)S(1)} %compare_and_fusion.1), kind=kLoop, calls=%fused_computation.6 | loop fusion | flops 10481664 | bytes 10846208 | tf_op jit(solution)/shard_map/reduce_sum | solution.py:52
  227.4 1.4 exponential_add_fusion.1
  228.8 3.5 %fusion.1 = f32[8,512]{1,0:T(8,128)} fusion(f32[640,512,8]{1,0,2:T(8,128)S(1)} %get-tuple-element.36, f32[8,512]{1,0:T(8,128)} %get-tuple-element.30, pred[512,640]{0,1:T(8,128)(4,1)S(1)} %compare_and_fusion), kind=kLoop, calls=%fused_computation.7 | loop fusion | flops 10481664 | bytes 10846208 | tf_op jit(solution)/shard_map/reduce_sum | solution.py:52
  232.3 0.8 exponential_add_fusion
  233.1 0.0 copy-done.4
  233.1 0.0 copy-start.1
  233.2 4.2 %fusion.31 = bf16[512,1,8,64]{0,3,2,1:T(8,128)(2,1)S(1)} fusion(f32[8,512]{1,0:T(8,128)S(1)} %exponential_add_fusion, f32[8,512]{1,0:T(8,128)S(1)} %copy-done.4, f32[640,512,8]{1,0,2:T(8,128)S(1)} %get-tuple-element.36, pred[512,640]{0,1:T(8,128)(4,1)S(1)} %compare_and_fusion, bf16[1024,1,640]{0,2,1:T(8,128)(2,1)} %copy-done.10), kind=kOutput, calls=%fused_computation.38 | convolution fusion | flops 348913664 | bytes 11452416 | tf_op jit(solution)/shard_map/jgqk,kjd->qjgd/dot_general | solution.py:54
  237.4 3.1 %fusion.34 = bf16[512,1,8,64]{0,3,2,1:T(8,128)(2,1)S(1)} fusion(f32[8,512]{1,0:T(8,128)S(1)} %copy-done.8, f32[8,512]{1,0:T(8,128)S(1)} %copy-done.5, f32[640,512,8]{1,0,2:T(8,128)S(1)} %get-tuple-element.34, pred[512,640]{0,1:T(8,128)(4,1)S(1)} %compare_and_fusion.1, bf16[128,1,128]{0,2,1:T(8,128)(2,1)S(1)} %copy-done.7, ...), kind=kOutput, calls=%fused_computation.39 | convolution fusion | flops 349241344 | bytes 11665408 | tf_op jit(solution)/shard_map/jgqk,kjd->qjgd/dot_general | solution.py:54
  240.6 0.1 pad_maximum_fusion
  240.7 7.0 %convolution_convert_fusion = bf16[1024,2880]{0,1:T(8,128)(2,1)} fusion(bf16[1024,512]{0,1:T(8,128)(2,1)S(1)} %bitcast.117, bf16[512,2880]{1,0:T(8,128)(2,1)} %bitcast.30), kind=kOutput, calls=%fused_computation.12 | convolution fusion | flops 3022848000 | bytes 9895936 | tf_op jit(solution)/shard_map/dot_general | solution.py:154
  247.7 8.5 %copy.61 = bf16[1024,2880]{1,0:T(8,128)(2,1)} copy(bf16[1024,2880]{0,1:T(8,128)(2,1)} %convolution_convert_fusion) | data formatting | bytes 11796480
  256.2 0.0 reduce-scatter.4.cloned.1.call-update
  256.2 39.3 %reduce-scatter.4.cloned.1.call-done = bf16[128,2880]{1,0:T(8,128)(2,1)} async-done(((bf16[1024,2880]{1,0:T(8,128)(2,1)}), bf16[128,2880]{1,0:T(8,128)(2,1)}) %reduce-scatter.4.cloned.1.call-update) | async-done | bytes 737296
  295.5 1.5 copy.62
  297.0 0.0 copy-done.12
  297.0 1.3 fusion.22
  (29 shorter events, 0.1 us)
Async XLA Ops:
  6.5 106.8 %all-gather.3.cloned.1.call-start = ((), (), s32[]{:S(2)}) async-start(), calls=%async_computation.3 | async-start | bytes 7603200 | tf_op jit(solution)/shard_map/all_gather | solution.py:82
  15.9 5.1 %copy-start.16 = (s32[128,4]{0,1:T(4,128)S(1)}, s32[128,4]{0,1:T(4,128)}, u32[]{:S(2)}) copy-start(s32[128,4]{0,1:T(4,128)} %param.16) | copy-start | bytes 6148
  15.9 5.1 %copy-start.17 = (s32[128,4]{0,1:T(4,128)S(1)}, s32[128,4]{0,1:T(4,128)}, u32[]{:S(2)}) copy-start(s32[128,4]{0,1:T(4,128)} %param.14) | copy-start | bytes 6148
  15.9 5.2 %copy-start.15 = (f32[128,4]{0,1:T(4,128)S(1)}, f32[128,4]{0,1:T(4,128)}, u32[]{:S(2)}) copy-start(f32[128,4]{0,1:T(4,128)} %param.15) | copy-start | bytes 6148
  15.9 90.5 %all-to-all-start = ((bf16[1,16,8,10,2880]{4,1,3,0,2:T(8,128)(2,1)}), bf16[1,16,8,10,2880]{4,1,3,0,2:T(8,128)(2,1)}, u32[]{:S(2)}, u32[]{:S(2)}) async-start(bf16[1,16,8,10,2880]{4,1,3,0,2:T(8,128)(2,1)} %copy.53), calls=%async_computation | async-start | bytes 15073280 | tf_op jit(solution)/shard_map/all_to_all | solution.py:81
  21.0 183.3 %all-gather.5.cloned.1.call-start = ((), (), s32[]{:S(2)}) async-start(), calls=%async_computation.4 | async-start | bytes 6635520 | tf_op jit(solution)/shard_map/all_gather | solution.py:104
  113.3 6.4 %copy-start.2 = (bf16[128,2880]{0,1:T(8,128)(2,1)S(1)}, bf16[128,2880]{0,1:T(8,128)(2,1)}, u32[]{:S(2)}) copy-start(bf16[128,2880]{0,1:T(8,128)(2,1)} %param.13) | copy-start | bytes 2211844
  113.3 6.8 %copy-start.11 = (f32[2880]{0:T(1024)S(1)}, f32[2880]{0:T(1024)}, u32[]{:S(2)}) copy-start(f32[2880]{0:T(1024)} %param.18) | copy-start | bytes 34564
  119.7 1.8 copy-start.3
  120.1 15.2 %copy-start.14 = (f32[1,640]{1,0:T(1,128)S(1)}, f32[1,640]{1,0:T(1,128)}, u32[]{:S(2)}) copy-start(f32[1,640]{1,0:T(1,128)} %param.20) | copy-start | bytes 7684
  120.1 15.2 %copy-start.9 = (s32[1024]{0:T(1024)S(1)}, s32[1024]{0:T(1024)}, u32[]{:S(2)}) copy-start(s32[1024]{0:T(1024)} %param.17) | copy-start | bytes 12292
  123.3 80.9 %all-to-all-start.1 = ((bf16[32,16,2880]{2,1,0:T(8,128)(2,1)}), bf16[32,16,2880]{2,1,0:T(8,128)(2,1)}, u32[]{:S(2)}, u32[]{:S(2)}) async-start(bf16[32,16,2880]{2,1,0:T(8,128)(2,1)} %broadcast_in_dim.33), calls=%async_computation.1 | async-start | bytes 6029312 | tf_op jit(solution)/shard_map/all_to_all | solution.py:62
  135.0 160.5 %reduce-scatter.4.cloned.1.call-start = ((), (), s32[]{:S(2)}) async-start(), calls=%async_computation.5 | async-start | bytes 6782976
  212.8 3.6 %copy-start.10 = (bf16[1024,1,640]{0,2,1:T(8,128)(2,1)}, bf16[1024,1,640]{0,2,1:T(8,128)(2,1)S(1)}, u32[]{:S(2)}) copy-start(bf16[1024,1,640]{0,2,1:T(8,128)(2,1)S(1)} %get-tuple-element.31) | copy-start | bytes 3932164
  213.5 8.0 %copy-start = (bf16[1024,1,32]{0,2,1:T(8,128)(2,1)}, bf16[1024,1,32]{0,2,1:T(8,128)(2,1)S(1)}, u32[]{:S(2)}) copy-start(bf16[1024,1,32]{0,2,1:T(8,128)(2,1)S(1)} %get-tuple-element.18) | copy-start | bytes 196612
  213.6 7.9 %collective-permute-start = (bf16[128,1,128]{0,2,1:T(8,128)(2,1)S(1)}, bf16[128,1,128]{0,2,1:T(8,128)(2,1)S(1)}, u32[]{:S(2)}, u32[]{:S(2)}) collective-permute-start(bf16[128,1,128]{0,2,1:T(8,128)(2,1)S(1)} %pad_maximum_fusion.8), channel_id=1, source_target_pairs={{0,8},{8,16},{16,24},{24,32},{32,40},{40,48},{48,56},{56,64},{64,7... | collective-permute-start | bytes 98312 | tf_op jit(solution)/shard_map/ppermute | solution.py:19
  218.2 5.1 %copy-start.13 = (f32[1,8]{1,0:T(1,128)S(1)}, f32[1,8]{1,0:T(1,128)}, u32[]{:S(2)}) copy-start(f32[1,8]{1,0:T(1,128)} %param.21) | copy-start | bytes 100
  221.5 1.8 copy-start.6
  228.8 4.3 %copy-start.4 = (f32[8,512]{1,0:T(8,128)S(1)}, f32[8,512]{1,0:T(8,128)}, u32[]{:S(2)}) copy-start(f32[8,512]{1,0:T(8,128)} %get-tuple-element.30) | copy-start | bytes 49156
  233.1 4.3 %copy-start.1 = (bf16[1024,1,32]{0,2,1:T(8,128)(2,1)S(1)}, bf16[1024,1,32]{0,2,1:T(8,128)(2,1)}, u32[]{:S(2)}) copy-start(bf16[1024,1,32]{0,2,1:T(8,128)(2,1)} %copy-done) | copy-start | bytes 196612
  233.1 4.3 %copy-start.5 = (f32[8,512]{1,0:T(8,128)S(1)}, f32[8,512]{1,0:T(8,128)}, u32[]{:S(2)}) copy-start(f32[8,512]{1,0:T(8,128)} %broadcast_maximum_fusion.1) | copy-start | bytes 49156
  233.1 4.3 %copy-start.7 = (bf16[128,1,128]{0,2,1:T(8,128)(2,1)S(1)}, bf16[128,1,128]{0,2,1:T(8,128)(2,1)}, u32[]{:S(2)}) copy-start(bf16[128,1,128]{0,2,1:T(8,128)(2,1)} %copy-done.6) | copy-start | bytes 98308
  233.2 4.3 %copy-start.8 = (f32[8,512]{1,0:T(8,128)S(1)}, f32[8,512]{1,0:T(8,128)}, u32[]{:S(2)}) copy-start(f32[8,512]{1,0:T(8,128)} %get-tuple-element.29) | copy-start | bytes 49156
  256.2 40.8 %copy-start.12 = (f32[2880]{0:T(1024)S(1)}, f32[2880]{0:T(1024)}, u32[]{:S(2)}) copy-start(f32[2880]{0:T(1024)} %param.23) | copy-start | bytes 34564
Sparse Core Ops, SparseCore 0:
  9.9 95.1 all-gather.2
  121.6 46.7 all-gather.4
  256.4 39.1 reduce-scatter.3

commit v3 on v2

--- a/solution.py
+++ b/solution.py
@@ -103,7 +103,6 @@
     ).astype(jnp.bfloat16)
     gathered = lax.all_gather(normalized_rows, "expert", axis=0, tiled=True)
     out_full = gather_fsdp(output_weight[0])
-    out_full, gathered = lax.optimization_barrier((out_full, gathered))
     block_rows = gathered.shape[0]
     local_heads = projection_weight.shape[1]
     projected_rows = jnp.dot(
@@ -149,6 +148,7 @@
             )
         )
     attention_result = jnp.concatenate(outputs_list, axis=0).reshape(block_rows, -1)
+    out_full, attention_result = lax.optimization_barrier((out_full, attention_result))
     output_weights = out_full.reshape(-1, model_width)
     projection_step = lax.psum_scatter(
         jnp.dot(attention_result, output_weights, preferred_element_type=jnp.float32).astype(

time: 306 us -> 289 us (0.944)
  waiting for transfers between devices: 194 us -> 177 us
    all_to_all x1, waiting for transfers between devices: 67.5 us -> 0.01 us  [gather_fsdp(): lax.all_to_all(spread, 'fsdp', split_axis=0, concat_axis=0, tiled=True)]
    all_gather x1, waiting for transfers between devices: 0.01 us -> 31.7 us  [shards(): gathered = lax.all_gather(normalized_rows, 'expert', axis=0, tiled=True)]
    ppermute x1, waiting for transfers between devices: 3.32 us -> 18.9 us  [passed_along(): return lax.ppermute(block, axis, route)]
  transfers between devices with their start and end apart: 6 -> 6, of which waited for: 4 -> 4; matrix products, arithmetic and copies ran while one was open for 7% -> 17% of each run, Pallas kernels for 0% -> 0%
where the time goes in v3:
time: 289 us; the launch traced here: 288 us
  waiting for transfers between devices  177 us (61%)
  matrix products  32.7 us (11%)
  local copies, waits for them, and re-layouts  28.3 us (10%)
  starting transfers between devices  20.4 us (7%)
  other arithmetic  16.7 us (6%)
  between operations  13.6 us (5%)
    all_to_all x1, waiting for transfers between devices, shards(): lax.all_to_all(expert_rows, 'expert', split_axis=2, concat_axis=1, tiled=...  84 us
    unnamed x4, waiting for transfers between devices  42.1 us
    all_gather x1, waiting for transfers between devices, shards(): gathered = lax.all_gather(normalized_rows, 'expert', axis=0, tiled=True)  31.7 us
    unnamed x40, local copies, waits for them, and re-layouts  19.5 us
    ppermute x1, waiting for transfers between devices, passed_along(): return lax.ppermute(block, axis, route)  18.9 us
    all_to_all x1, starting transfers between devices, gather_fsdp(): lax.all_to_all(spread, 'fsdp', split_axis=0, concat_axis=0, tiled=True)  11.7 us
    dot_general x1, matrix products, shards(): jnp.dot(gathered, qkv_full.reshape(model_width, -1), preferred_element_ty...  8.51 us
    dot_general x2, matrix products, attend_block(): jnp.einsum('jgqk,kjd->qjgd', weights_soft, values_only, preferred_element...  7.33 us
  transfers between devices with their start and end apart: 6, of which 4 were waited for; matrix products, arithmetic and copies ran while one was open for 17% of the time, Pallas kernels for 0%

profile of v3, /device:TPU:2, one launch (start us, length us, event | category | flops | bytes accessed | tf_op | source)
XLA Modules:
  0.0 288.4 jit_solution(8379033605320299008)
XLA Ops:
  6.5 0.0 all-gather.3.cloned.1.call-start
  6.5 1.8 copy.52
  8.3 0.0 all-gather.3.cloned.1.call-update
  8.3 7.6 %copy.53 = bf16[1,16,8,10,2880]{4,1,3,0,2:T(8,128)(2,1)} copy(bf16[1,16,8,10,2880]{4,2,3,1,0:T(8,128)(2,1)} %param.12) | data formatting | bytes 14745600 | tf_op args[0]
  16.0 5.0 %all-to-all-start = ((bf16[1,16,8,10,2880]{4,1,3,0,2:T(8,128)(2,1)}), bf16[1,16,8,10,2880]{4,1,3,0,2:T(8,128)(2,1)}, u32[]{:S(2)}, u32[]{:S(2)}) async-start(bf16[1,16,8,10,2880]{4,1,3,0,2:T(8,128)(2,1)} %copy.53), calls=%async_computation | async-start | bytes 15073280 | tf_op jit(solution)/shard_map/all_to_all | solution.py:81
  21.0 0.0 all-gather.5.cloned.1.call-start
  21.0 0.0 copy-done.16
  21.0 0.0 copy-done.17
  21.1 0.1 iota_compare_fusion
  21.2 0.0 copy-done.15
  21.2 1.1 select_reduce_fusion
  22.3 0.1 subtract_convert_fusion.1
  22.5 84.0 %all-to-all-done = bf16[1,16,8,10,2880]{4,1,3,0,2:T(8,128)(2,1)} async-done(((bf16[1,16,8,10,2880]{4,1,3,0,2:T(8,128)(2,1)}), bf16[1,16,8,10,2880]{4,1,3,0,2:T(8,128)(2,1)}, u32[]{:S(2)}, u32[]{:S(2)}) %all-to-all-start) | async-done | bytes 7372832 | tf_op jit(solution)/shard_map/all_to_all | solution.py:81
  106.5 6.9 %copy.54 = bf16[1,8,16,1,10,2880]{5,2,1,4,3,0:T(8,128)(2,1)} copy(bf16[1,8,16,1,10,2880]{5,2,4,1,3,0:T(8,128)(2,1)} %bitcast.1) | data formatting | bytes 14745600 | tf_op jit(solution)/shard_map/all_to_all | solution.py:81
  113.3 6.3 %fusion.10 = f32[256,2880]{0,1:T(8,128)S(1)} fusion(bf16[1,128,1,10,2880]{4,1,3,2,0:T(8,128)(2,1)} %bitcast.116, bf16[128,128,10]{1,0,2:T(8,128)(2,1)S(1)} %get-tuple-element.15, bf16[128,128,10]{1,0,2:T(8,128)(2,1)S(1)} %get-tuple-element.16), kind=kOutput, calls=%fused_computation.17 | convolution fusion | flops 1888747520 | bytes 10977280 | tf_op jit(solution)/shard_map/txs,xsm->tm/dot_general | solution.py:93
  119.7 0.0 copy-done.2
  119.7 0.0 copy-start.3
  119.7 0.4 fusion.18
  120.1 0.0 copy-start.9
  120.1 0.0 copy-done.11
  120.1 1.3 fusion.20
  121.5 0.0 all-gather.5.cloned.1.call-update
  121.5 0.0 copy-done.3
  121.5 1.9 broadcast_in_dim.33
  123.4 11.7 %all-to-all-start.1 = ((bf16[32,16,2880]{2,1,0:T(8,128)(2,1)}), bf16[32,16,2880]{2,1,0:T(8,128)(2,1)}, u32[]{:S(2)}, u32[]{:S(2)}) async-start(bf16[32,16,2880]{2,1,0:T(8,128)(2,1)} %broadcast_in_dim.33), calls=%async_computation.1 | async-start | bytes 6029312 | tf_op jit(solution)/shard_map/all_to_all | solution.py:62
  135.0 0.2 reduce-scatter.4.cloned.1.call-start
  135.3 0.0 copy-done.14
  135.3 0.0 copy-done.9
  135.4 0.5 multiply_cosine_fusion
  135.9 0.4 compare_and_fusion.1
  136.3 0.4 compare_and_fusion
  136.7 31.7 %all-gather.5.cloned.1.call-done = bf16[1024,2880]{0,1:T(8,128)(2,1)} async-done(((bf16[128,2880]{0,1:T(8,128)(2,1)}), bf16[1024,2880]{0,1:T(8,128)(2,1)}) %all-gather.5.cloned.1.call-update) | async-done | bytes 5898256 | tf_op jit(solution)/shard_map/all_gather | solution.py:104
  168.4 8.5 %fusion.79 = (bf16[1024,1,640]{0,2,1:T(8,128)(2,1)S(1)}, f32[1024,1,640]{0,2,1:T(8,128)S(1)}) fusion(f32[640]{0:T(1024)S(1)} %reduce.4, bf16[1024,2880]{0,1:T(8,128)(2,1)} %all-gather.5.cloned.1.call-done, bf16[2880,1,640]{2,1,0:T(2,128)(2,1)} %all-gather.3.cloned.1.call-done), kind=kOutput, calls=%fused_computation.110 | convolution fusion | flops 3776184320 | bytes 13519360 | tf_op jit(solution)/shard_map/dot_general | solution.py:108
  176.9 0.0 copy-start.10
  176.9 0.6 fusion.53
  177.5 0.0 copy-start
  177.5 0.1 slice.94
  177.7 3.5 %collective-permute-start = (bf16[128,1,128]{0,2,1:T(8,128)(2,1)S(1)}, bf16[128,1,128]{0,2,1:T(8,128)(2,1)S(1)}, u32[]{:S(2)}, u32[]{:S(2)}) collective-permute-start(bf16[128,1,128]{0,2,1:T(8,128)(2,1)S(1)} %pad_maximum_fusion.8), channel_id=1, source_target_pairs={{0,8},{8,16},{16,24},{24,32},{32,40},{40,48},{48,56},{56,64},{64,7... | collective-permute-start | bytes 98312 | tf_op jit(solution)/shard_map/ppermute | solution.py:19
  181.2 0.3 subtract_convert_fusion
  181.5 1.7 fusion.3
  183.3 0.0 copy-start.13
  183.3 18.9 %collective-permute-done = bf16[128,1,128]{0,2,1:T(8,128)(2,1)S(1)} collective-permute-done((bf16[128,1,128]{0,2,1:T(8,128)(2,1)S(1)}, bf16[128,1,128]{0,2,1:T(8,128)(2,1)S(1)}, u32[]{:S(2)}, u32[]{:S(2)}) %collective-permute-start) | collective-permute-done | bytes 32800 | tf_op jit(solution)/shard_map/ppermute | solution.py:19
  202.2 1.8 fusion.2
  204.0 0.7 broadcast_maximum_fusion.1
  204.7 3.5 %fusion = f32[8,512]{1,0:T(8,128)} fusion(f32[640,512,8]{1,0,2:T(8,128)S(1)} %get-tuple-element.34, f32[8,512]{1,0:T(8,128)} %broadcast_maximum_fusion.1, pred[512,640]{0,1:T(8,128)(4,1)S(1)} %compare_and_fusion.1), kind=kLoop, calls=%fused_computation.6 | loop fusion | flops 10481664 | bytes 10846208 | tf_op jit(solution)/shard_map/reduce_sum | solution.py:52
  208.1 1.4 exponential_add_fusion.1
  209.5 3.5 %fusion.1 = f32[8,512]{1,0:T(8,128)} fusion(f32[640,512,8]{1,0,2:T(8,128)S(1)} %get-tuple-element.36, f32[8,512]{1,0:T(8,128)} %get-tuple-element.30, pred[512,640]{0,1:T(8,128)(4,1)S(1)} %compare_and_fusion), kind=kLoop, calls=%fused_computation.7 | loop fusion | flops 10481664 | bytes 10846208 | tf_op jit(solution)/shard_map/reduce_sum | solution.py:52
  213.0 0.8 exponential_add_fusion
  213.8 0.0 copy-done.4
  213.8 0.0 copy-start.1
  213.9 4.2 %fusion.31 = bf16[512,1,8,64]{0,3,2,1:T(8,128)(2,1)S(1)} fusion(f32[8,512]{1,0:T(8,128)S(1)} %exponential_add_fusion, f32[8,512]{1,0:T(8,128)S(1)} %copy-done.4, f32[640,512,8]{1,0,2:T(8,128)S(1)} %get-tuple-element.36, pred[512,640]{0,1:T(8,128)(4,1)S(1)} %compare_and_fusion, bf16[1024,1,640]{0,2,1:T(8,128)(2,1)} %copy-done.10), kind=kOutput, calls=%fused_computation.38 | convolution fusion | flops 348913664 | bytes 11452416 | tf_op jit(solution)/shard_map/jgqk,kjd->qjgd/dot_general | solution.py:54
  218.1 0.0 copy-done.1
  218.1 0.0 copy-done.5
  218.1 0.0 copy-done.7
  218.2 0.0 copy-done.8
  218.2 3.1 %fusion.34 = bf16[512,1,8,64]{0,3,2,1:T(8,128)(2,1)S(1)} fusion(f32[8,512]{1,0:T(8,128)S(1)} %copy-done.8, f32[8,512]{1,0:T(8,128)S(1)} %copy-done.5, f32[640,512,8]{1,0,2:T(8,128)S(1)} %get-tuple-element.34, pred[512,640]{0,1:T(8,128)(4,1)S(1)} %compare_and_fusion.1, bf16[128,1,128]{0,2,1:T(8,128)(2,1)S(1)} %copy-done.7, ...), kind=kOutput, calls=%fused_computation.39 | convolution fusion | flops 349241344 | bytes 11665408 | tf_op jit(solution)/shard_map/jgqk,kjd->qjgd/dot_general | solution.py:54
  221.3 0.1 pad_maximum_fusion
  221.4 0.0 all-to-all-done.1
  221.4 7.0 %convolution_convert_fusion = bf16[1024,2880]{0,1:T(8,128)(2,1)} fusion(bf16[1024,512]{0,1:T(8,128)(2,1)S(1)} %bitcast.117, bf16[512,2880]{1,0:T(8,128)(2,1)} %bitcast.30), kind=kOutput, calls=%fused_computation.12 | convolution fusion | flops 3022848000 | bytes 9895936 | tf_op jit(solution)/shard_map/dot_general | solution.py:154
  228.4 8.5 %copy.61 = bf16[1024,2880]{1,0:T(8,128)(2,1)} copy(bf16[1024,2880]{0,1:T(8,128)(2,1)} %convolution_convert_fusion) | data formatting | bytes 11796480
  237.0 0.0 reduce-scatter.4.cloned.1.call-update
  237.0 42.0 %reduce-scatter.4.cloned.1.call-done = bf16[128,2880]{1,0:T(8,128)(2,1)} async-done(((bf16[1024,2880]{1,0:T(8,128)(2,1)}), bf16[128,2880]{1,0:T(8,128)(2,1)}) %reduce-scatter.4.cloned.1.call-update) | async-done | bytes 737296
  279.0 1.5 copy.62
  280.5 1.3 fusion.22
  (29 shorter events, 0.1 us)
Async XLA Ops:
  6.5 106.8 %all-gather.3.cloned.1.call-start = ((), (), s32[]{:S(2)}) async-start(), calls=%async_computation.3 | async-start | bytes 7603200 | tf_op jit(solution)/shard_map/all_gather | solution.py:82
  16.0 5.1 %copy-start.16 = (s32[128,4]{0,1:T(4,128)S(1)}, s32[128,4]{0,1:T(4,128)}, u32[]{:S(2)}) copy-start(s32[128,4]{0,1:T(4,128)} %param.16) | copy-start | bytes 6148
  16.0 5.1 %copy-start.17 = (s32[128,4]{0,1:T(4,128)S(1)}, s32[128,4]{0,1:T(4,128)}, u32[]{:S(2)}) copy-start(s32[128,4]{0,1:T(4,128)} %param.14) | copy-start | bytes 6148
  16.0 5.2 %copy-start.15 = (f32[128,4]{0,1:T(4,128)S(1)}, f32[128,4]{0,1:T(4,128)}, u32[]{:S(2)}) copy-start(f32[128,4]{0,1:T(4,128)} %param.15) | copy-start | bytes 6148
  16.0 90.5 %all-to-all-start = ((bf16[1,16,8,10,2880]{4,1,3,0,2:T(8,128)(2,1)}), bf16[1,16,8,10,2880]{4,1,3,0,2:T(8,128)(2,1)}, u32[]{:S(2)}, u32[]{:S(2)}) async-start(bf16[1,16,8,10,2880]{4,1,3,0,2:T(8,128)(2,1)} %copy.53), calls=%async_computation | async-start | bytes 15073280 | tf_op jit(solution)/shard_map/all_to_all | solution.py:81
  21.0 147.4 %all-gather.5.cloned.1.call-start = ((), (), s32[]{:S(2)}) async-start(), calls=%async_computation.4 | async-start | bytes 6635520 | tf_op jit(solution)/shard_map/all_gather | solution.py:104
  113.3 6.4 %copy-start.2 = (bf16[128,2880]{0,1:T(8,128)(2,1)S(1)}, bf16[128,2880]{0,1:T(8,128)(2,1)}, u32[]{:S(2)}) copy-start(bf16[128,2880]{0,1:T(8,128)(2,1)} %param.13) | copy-start | bytes 2211844
  113.3 6.8 %copy-start.11 = (f32[2880]{0:T(1024)S(1)}, f32[2880]{0:T(1024)}, u32[]{:S(2)}) copy-start(f32[2880]{0:T(1024)} %param.18) | copy-start | bytes 34564
  119.7 1.8 copy-start.3
  120.1 15.2 %copy-start.14 = (f32[1,640]{1,0:T(1,128)S(1)}, f32[1,640]{1,0:T(1,128)}, u32[]{:S(2)}) copy-start(f32[1,640]{1,0:T(1,128)} %param.20) | copy-start | bytes 7684
  120.1 15.2 %copy-start.9 = (s32[1024]{0:T(1024)S(1)}, s32[1024]{0:T(1024)}, u32[]{:S(2)}) copy-start(s32[1024]{0:T(1024)} %param.17) | copy-start | bytes 12292
  123.4 98.1 %all-to-all-start.1 = ((bf16[32,16,2880]{2,1,0:T(8,128)(2,1)}), bf16[32,16,2880]{2,1,0:T(8,128)(2,1)}, u32[]{:S(2)}, u32[]{:S(2)}) async-start(bf16[32,16,2880]{2,1,0:T(8,128)(2,1)} %broadcast_in_dim.33), calls=%async_computation.1 | async-start | bytes 6029312 | tf_op jit(solution)/shard_map/all_to_all | solution.py:62
  135.0 144.0 %reduce-scatter.4.cloned.1.call-start = ((), (), s32[]{:S(2)}) async-start(), calls=%async_computation.5 | async-start | bytes 6782976
  176.9 4.6 %copy-start.10 = (bf16[1024,1,640]{0,2,1:T(8,128)(2,1)}, bf16[1024,1,640]{0,2,1:T(8,128)(2,1)S(1)}, u32[]{:S(2)}) copy-start(bf16[1024,1,640]{0,2,1:T(8,128)(2,1)S(1)} %get-tuple-element.31) | copy-start | bytes 3932164
  177.5 24.7 %copy-start = (bf16[1024,1,32]{0,2,1:T(8,128)(2,1)}, bf16[1024,1,32]{0,2,1:T(8,128)(2,1)S(1)}, u32[]{:S(2)}) copy-start(bf16[1024,1,32]{0,2,1:T(8,128)(2,1)S(1)} %get-tuple-element.18) | copy-start | bytes 196612
  177.7 24.5 %collective-permute-start = (bf16[128,1,128]{0,2,1:T(8,128)(2,1)S(1)}, bf16[128,1,128]{0,2,1:T(8,128)(2,1)S(1)}, u32[]{:S(2)}, u32[]{:S(2)}) collective-permute-start(bf16[128,1,128]{0,2,1:T(8,128)(2,1)S(1)} %pad_maximum_fusion.8), channel_id=1, source_target_pairs={{0,8},{8,16},{16,24},{24,32},{32,40},{40,48},{48,56},{56,64},{64,7... | collective-permute-start | bytes 98312 | tf_op jit(solution)/shard_map/ppermute | solution.py:19
  183.3 20.7 %copy-start.13 = (f32[1,8]{1,0:T(1,128)S(1)}, f32[1,8]{1,0:T(1,128)}, u32[]{:S(2)}) copy-start(f32[1,8]{1,0:T(1,128)} %param.21) | copy-start | bytes 100
  202.2 1.8 copy-start.6
  209.5 4.3 %copy-start.4 = (f32[8,512]{1,0:T(8,128)S(1)}, f32[8,512]{1,0:T(8,128)}, u32[]{:S(2)}) copy-start(f32[8,512]{1,0:T(8,128)} %get-tuple-element.30) | copy-start | bytes 49156
  213.8 4.3 %copy-start.1 = (bf16[1024,1,32]{0,2,1:T(8,128)(2,1)S(1)}, bf16[1024,1,32]{0,2,1:T(8,128)(2,1)}, u32[]{:S(2)}) copy-start(bf16[1024,1,32]{0,2,1:T(8,128)(2,1)} %copy-done) | copy-start | bytes 196612
  213.9 4.3 %copy-start.5 = (f32[8,512]{1,0:T(8,128)S(1)}, f32[8,512]{1,0:T(8,128)}, u32[]{:S(2)}) copy-start(f32[8,512]{1,0:T(8,128)} %broadcast_maximum_fusion.1) | copy-start | bytes 49156
  213.9 4.3 %copy-start.7 = (bf16[128,1,128]{0,2,1:T(8,128)(2,1)S(1)}, bf16[128,1,128]{0,2,1:T(8,128)(2,1)}, u32[]{:S(2)}) copy-start(bf16[128,1,128]{0,2,1:T(8,128)(2,1)} %copy-done.6) | copy-start | bytes 98308
  213.9 4.3 %copy-start.8 = (f32[8,512]{1,0:T(8,128)S(1)}, f32[8,512]{1,0:T(8,128)}, u32[]{:S(2)}) copy-start(f32[8,512]{1,0:T(8,128)} %get-tuple-element.29) | copy-start | bytes 49156
  236.9 43.6 %copy-start.12 = (f32[2880]{0:T(1024)S(1)}, f32[2880]{0:T(1024)}, u32[]{:S(2)}) copy-start(f32[2880]{0:T(1024)} %param.23) | copy-start | bytes 34564
Sparse Core Ops, SparseCore 0:
  9.9 95.1 all-gather.2
  121.6 46.7 all-gather.4
  237.1 41.8 reduce-scatter.3

commit v4 on v3

--- a/solution.py
+++ b/solution.py
@@ -78,22 +78,35 @@
 ):
     own_rows = residual.shape[0]
     model_width = residual.shape[1]
-    returned = lax.all_to_all(expert_rows, "expert", split_axis=2, concat_axis=1, tiled=True)
     qkv_full = lax.all_gather(projection_weight, "fsdp", axis=0, tiled=True)
-    qkv_full, returned = lax.optimization_barrier((qkv_full, returned))
-    all_experts = returned.shape[1]
-    capacity = returned.shape[3]
-    hit_expert = route_ids[..., None] == jnp.arange(all_experts, dtype=jnp.int32)
+    local_experts = expert_rows.shape[1]
+    half = local_experts // 2
+    capacity = expert_rows.shape[3]
+    n_exp = lax.axis_size("expert")
+    hit_expert = route_ids[..., None] == jnp.arange(n_exp * local_experts, dtype=jnp.int32)
     hit_slot = route_slots[..., None] == jnp.arange(capacity, dtype=jnp.int32)
     hits = hit_expert[..., :, None] & hit_slot[..., None, :]
     select = jnp.sum(jnp.where(hits, route_weights[..., None, None], 0.0), axis=1)
     high = select.astype(jnp.bfloat16)
     low = (select - high.astype(jnp.float32)).astype(jnp.bfloat16)
-    both = jnp.concatenate([high, low], axis=0)
-    picked = jnp.einsum(
-        "txs,xsm->tm", both, returned[0, :, 0], preferred_element_type=jnp.float32
+    both = jnp.concatenate([high, low], axis=0).reshape(
+        2 * own_rows, n_exp, local_experts, capacity
     )
-    combined = picked[:own_rows] + picked[own_rows:]
+    combined = None
+    for first in (0, half):
+        returned = lax.all_to_all(
+            expert_rows[:, first : first + half], "expert", split_axis=2, concat_axis=1, tiled=True
+        )
+        if first == 0:
+            qkv_full, returned = lax.optimization_barrier((qkv_full, returned))
+        picked = jnp.einsum(
+            "tkxs,kxsm->tm",
+            both[:, :, first : first + half],
+            returned[0, :, 0].reshape(n_exp, half, capacity, model_width),
+            preferred_element_type=jnp.float32,
+        )
+        picked = picked[:own_rows] + picked[own_rows:]
+        combined = picked if combined is None else combined + picked
     hidden = (residual.astype(jnp.float32) + combined).astype(jnp.bfloat16)
     widened = hidden.astype(jnp.float32)
     normalized_rows = (

time: 289 us -> 297 us (1.028)
  matrix products: 32.7 us -> 38.3 us
  waiting for transfers between devices: 177 us -> 172 us
  starting transfers between devices: 20.4 us -> 24.6 us
    dot_general x1 -> x2, matrix products: 6.34 us -> 11.9 us  [shards(): jnp.einsum('tkxs,kxsm->tm', both[:, :, first:first + half], returned[0, :...]
    all_to_all x1 -> x2, waiting for transfers between devices: 84 us -> 79.1 us  [shards(): lax.all_to_all(expert_rows[:, first:first + half], 'expert', split_axis=2...]
    slice x0 -> x1, local copies, waits for them, and re-layouts: none -> 4.76 us  [shards(): expert_rows[:, first:first + half]]
    all_to_all x1 -> x2, starting transfers between devices: 5 us -> 9.03 us  [shards(): lax.all_to_all(expert_rows[:, first:first + half], 'expert', split_axis=2...]
    unnamed x40 -> x43, local copies, waits for them, and re-layouts: 19.5 us -> 19.2 us
  transfers between devices with their start and end apart: 6 -> 7, of which waited for: 4 -> 5; matrix products, arithmetic and copies ran while one was open for 17% -> 20% of each run, Pallas kernels for 0% -> 0%
where the time goes in v4:
time: 297 us; the launch traced here: 296 us
  waiting for transfers between devices  172 us (58%)
  matrix products  38.3 us (13%)
  local copies, waits for them, and re-layouts  31 us (10%)
  starting transfers between devices  24.6 us (8%)
  other arithmetic  16.7 us (6%)
  between operations  13.6 us (5%)
    all_to_all x2, waiting for transfers between devices, shards(): lax.all_to_all(expert_rows[:, first:first + half], 'expert', split_axis=2...  79.1 us
    unnamed x4, waiting for transfers between devices  42.1 us
    all_gather x1, waiting for transfers between devices, shards(): gathered = lax.all_gather(normalized_rows, 'expert', axis=0, tiled=True)  31.6 us
    unnamed x43, local copies, waits for them, and re-layouts  19.2 us
    ppermute x1, waiting for transfers between devices, passed_along(): return lax.ppermute(block, axis, route)  19 us
    dot_general x2, matrix products, shards(): jnp.einsum('tkxs,kxsm->tm', both[:, :, first:first + half], returned[0, :...  11.9 us
    all_to_all x1, starting transfers between devices, gather_fsdp(): lax.all_to_all(spread, 'fsdp', split_axis=0, concat_axis=0, tiled=True)  11.8 us
    all_to_all x2, starting transfers between devices, shards(): lax.all_to_all(expert_rows[:, first:first + half], 'expert', split_axis=2...  9.03 us
  transfers between devices with their start and end apart: 7, of which 5 were waited for; matrix products, arithmetic and copies ran while one was open for 20% of the time, Pallas kernels for 0%

profile of v4, /device:TPU:2, one launch (start us, length us, event | category | flops | bytes accessed | tf_op | source)
XLA Modules:
  0.0 295.9 jit_solution(3841369724568175458)
XLA Ops:
  6.5 0.0 all-gather.3.cloned.1.call-start
  6.5 1.8 copy.50
  8.3 0.0 all-gather.3.cloned.1.call-update
  8.3 4.8 %fusion.82 = (bf16[1,8,8,10,2880]{4,2,3,1,0:T(8,128)(2,1)S(1)}, bf16[1,8,8,10,2880]{4,2,3,1,0:T(8,128)(2,1)}) fusion(bf16[1,16,8,10,2880]{4,2,3,1,0:T(8,128)(2,1)} %param.12), kind=kLoop, calls=%fused_computation.114 | loop fusion | bytes 14745600 | tf_op jit(solution)/shard_map/slice | solution.py:98
  13.1 2.5 copy.65
  15.6 4.5 %all-to-all-start = ((bf16[1,8,8,10,2880]{4,1,3,0,2:T(8,128)(2,1)}), bf16[1,8,8,10,2880]{4,1,3,0,2:T(8,128)(2,1)}, u32[]{:S(2)}, u32[]{:S(2)}) async-start(bf16[1,8,8,10,2880]{4,1,3,0,2:T(8,128)(2,1)} %copy.65), calls=%async_computation | async-start | bytes 7536640 | tf_op jit(solution)/shard_map/all_to_all | solution.py:97
  20.1 4.6 %copy.66 = bf16[1,8,8,10,2880]{4,1,3,0,2:T(8,128)(2,1)} copy(bf16[1,8,8,10,2880]{4,2,3,1,0:T(8,128)(2,1)} %get-tuple-element.16) | data formatting | bytes 7372800
  24.7 40.5 %all-to-all-done = bf16[1,8,8,10,2880]{4,1,3,0,2:T(8,128)(2,1)} async-done(((bf16[1,8,8,10,2880]{4,1,3,0,2:T(8,128)(2,1)}), bf16[1,8,8,10,2880]{4,1,3,0,2:T(8,128)(2,1)}, u32[]{:S(2)}, u32[]{:S(2)}) %all-to-all-start) | async-done | bytes 3686432 | tf_op jit(solution)/shard_map/all_to_all | solution.py:97
  65.3 4.5 %all-to-all-start.1 = ((bf16[1,8,8,10,2880]{4,1,3,0,2:T(8,128)(2,1)}), bf16[1,8,8,10,2880]{4,1,3,0,2:T(8,128)(2,1)}, u32[]{:S(2)}, u32[]{:S(2)}) async-start(bf16[1,8,8,10,2880]{4,1,3,0,2:T(8,128)(2,1)} %copy.66), calls=%async_computation.1 | async-start | bytes 7536640 | tf_op jit(solution)/shard_map/all_to_all | solution.py:97
  69.8 0.0 all-gather.5.cloned.1.call-start
  69.9 0.0 copy-done.17
  69.9 0.1 iota_compare_fusion
  70.1 1.1 select_reduce_fusion
  71.2 0.5 copy.49
  71.7 0.1 convert_element_type.81
  71.8 0.1 subtract_convert_fusion.1
  71.9 4.5 %copy.86 = bf16[1,8,8,10,2880]{4,1,2,3,0:T(8,128)(2,1)} copy(bf16[1,8,8,10,2880]{4,1,3,0,2:T(8,128)(2,1)} %all-to-all-done) | data formatting | bytes 7372800 | tf_op jit(solution)/shard_map/all_to_all | solution.py:97
  76.4 38.6 %all-to-all-done.1 = bf16[1,8,8,10,2880]{4,1,3,0,2:T(8,128)(2,1)} async-done(((bf16[1,8,8,10,2880]{4,1,3,0,2:T(8,128)(2,1)}), bf16[1,8,8,10,2880]{4,1,3,0,2:T(8,128)(2,1)}, u32[]{:S(2)}, u32[]{:S(2)}) %all-to-all-start.1) | async-done | bytes 3686432 | tf_op jit(solution)/shard_map/all_to_all | solution.py:97
  114.9 6.2 %fusion.16 = f32[256,2880]{0,1:T(8,128)} fusion(bf16[1,8,8,10,2880]{4,1,3,0,2:T(8,128)(2,1)} %all-to-all-done.1, bf16[128,8,16,10]{0,3,2,1:T(8,128)(2,1)S(1)} %subtract_convert_fusion.1, bf16[128,8,16,10]{0,3,2,1:T(8,128)(2,1)S(1)} %convert_element_type.81), kind=kOutput, calls=%fused_computation.21 | convolution fusion | flops 945029120 | bytes 7290880 | tf_op jit(solution)/shard_map/tkxs,kxsm->tm/dot_general | solution.py:102
  121.1 5.7 %fusion.13 = f32[256,2880]{0,1:T(8,128)S(1)} fusion(bf16[8,8,10,2880]{3,1,0,2:T(8,128)(2,1)} %bitcast.133, bf16[128,8,16,10]{0,3,2,1:T(8,128)(2,1)S(1)} %subtract_convert_fusion.1, bf16[128,8,16,10]{0,3,2,1:T(8,128)(2,1)S(1)} %convert_element_type.81), kind=kOutput, calls=%fused_computation.20 | convolution fusion | flops 945029120 | bytes 7290880 | tf_op jit(solution)/shard_map/tkxs,kxsm->tm/dot_general | solution.py:102
  126.9 0.0 copy-start.12
  126.9 0.0 copy-start.4
  126.9 0.4 fusion.24
  127.3 0.3 copy-done.12
  127.6 1.3 fusion.26
  128.9 0.0 all-gather.5.cloned.1.call-update
  128.9 0.0 copy-done.4
  128.9 1.8 broadcast_in_dim.33
  130.8 11.8 %all-to-all-start.2 = ((bf16[32,16,2880]{2,1,0:T(8,128)(2,1)}), bf16[32,16,2880]{2,1,0:T(8,128)(2,1)}, u32[]{:S(2)}, u32[]{:S(2)}) async-start(bf16[32,16,2880]{2,1,0:T(8,128)(2,1)} %broadcast_in_dim.33), calls=%async_computation.2 | async-start | bytes 6029312 | tf_op jit(solution)/shard_map/all_to_all | solution.py:62
  142.6 0.2 reduce-scatter.4.cloned.1.call-start
  142.9 0.5 multiply_cosine_fusion
  143.5 0.4 compare_and_fusion.1
  143.9 0.4 compare_and_fusion
  144.3 31.6 %all-gather.5.cloned.1.call-done = bf16[1024,2880]{0,1:T(8,128)(2,1)} async-done(((bf16[128,2880]{0,1:T(8,128)(2,1)}), bf16[1024,2880]{0,1:T(8,128)(2,1)}) %all-gather.5.cloned.1.call-update) | async-done | bytes 5898256 | tf_op jit(solution)/shard_map/all_gather | solution.py:117
  175.9 8.5 %fusion.85 = (bf16[1024,1,640]{0,2,1:T(8,128)(2,1)S(1)}, f32[1024,1,640]{0,2,1:T(8,128)S(1)}) fusion(f32[640]{0:T(1024)S(1)} %reduce.4, bf16[1024,2880]{0,1:T(8,128)(2,1)} %all-gather.5.cloned.1.call-done, bf16[2880,1,640]{2,1,0:T(2,128)(2,1)} %all-gather.3.cloned.1.call-done), kind=kOutput, calls=%fused_computation.117 | convolution fusion | flops 3776184320 | bytes 13519360 | tf_op jit(solution)/shard_map/dot_general | solution.py:121
  184.4 0.6 fusion.57
  185.0 0.0 copy-start.1
  185.0 0.1 slice.120
  185.2 3.5 %collective-permute-start = (bf16[128,1,128]{0,2,1:T(8,128)(2,1)S(1)}, bf16[128,1,128]{0,2,1:T(8,128)(2,1)S(1)}, u32[]{:S(2)}, u32[]{:S(2)}) collective-permute-start(bf16[128,1,128]{0,2,1:T(8,128)(2,1)S(1)} %pad_maximum_fusion.11), channel_id=1, source_target_pairs={{0,8},{8,16},{16,24},{24,32},{32,40},{40,48},{48,56},{56,64},{64,7... | collective-permute-start | bytes 98312 | tf_op jit(solution)/shard_map/ppermute | solution.py:19
  188.6 0.3 subtract_convert_fusion
  189.0 1.7 fusion.3
  190.7 0.0 copy-start.14
  190.7 19.0 %collective-permute-done = bf16[128,1,128]{0,2,1:T(8,128)(2,1)S(1)} collective-permute-done((bf16[128,1,128]{0,2,1:T(8,128)(2,1)S(1)}, bf16[128,1,128]{0,2,1:T(8,128)(2,1)S(1)}, u32[]{:S(2)}, u32[]{:S(2)}) %collective-permute-start) | collective-permute-done | bytes 32800 | tf_op jit(solution)/shard_map/ppermute | solution.py:19
  209.8 1.8 fusion.2
  211.5 0.0 copy-done.7
  211.5 0.0 copy-done.14
  211.6 0.7 broadcast_maximum_fusion.1
  212.2 3.4 %fusion = f32[8,512]{1,0:T(8,128)} fusion(f32[640,512,8]{1,0,2:T(8,128)S(1)} %get-tuple-element.34, f32[8,512]{1,0:T(8,128)} %broadcast_maximum_fusion.1, pred[512,640]{0,1:T(8,128)(4,1)S(1)} %compare_and_fusion.1), kind=kLoop, calls=%fused_computation.6 | loop fusion | flops 10481664 | bytes 10846208 | tf_op jit(solution)/shard_map/reduce_sum | solution.py:52
  215.7 1.4 exponential_add_fusion.1
  217.1 3.5 %fusion.1 = f32[8,512]{1,0:T(8,128)} fusion(f32[640,512,8]{1,0,2:T(8,128)S(1)} %get-tuple-element.36, f32[8,512]{1,0:T(8,128)} %get-tuple-element.30, pred[512,640]{0,1:T(8,128)(4,1)S(1)} %compare_and_fusion), kind=kLoop, calls=%fused_computation.7 | loop fusion | flops 10481664 | bytes 10846208 | tf_op jit(solution)/shard_map/reduce_sum | solution.py:52
  220.6 0.8 exponential_add_fusion
  221.4 0.0 copy-done.5
  221.4 0.0 copy-start.2
  221.4 4.2 %fusion.38 = bf16[512,1,8,64]{0,3,2,1:T(8,128)(2,1)S(1)} fusion(f32[8,512]{1,0:T(8,128)S(1)} %exponential_add_fusion, f32[8,512]{1,0:T(8,128)S(1)} %copy-done.5, f32[640,512,8]{1,0,2:T(8,128)S(1)} %get-tuple-element.36, pred[512,640]{0,1:T(8,128)(4,1)S(1)} %compare_and_fusion, bf16[1024,1,640]{0,2,1:T(8,128)(2,1)} %copy-done.11), kind=kOutput, calls=%fused_computation.45 | convolution fusion | flops 348913664 | bytes 11452416 | tf_op jit(solution)/shard_map/jgqk,kjd->qjgd/dot_general | solution.py:54
  225.7 3.1 %fusion.41 = bf16[512,1,8,64]{0,3,2,1:T(8,128)(2,1)S(1)} fusion(f32[8,512]{1,0:T(8,128)S(1)} %copy-done.9, f32[8,512]{1,0:T(8,128)S(1)} %copy-done.6, f32[640,512,8]{1,0,2:T(8,128)S(1)} %get-tuple-element.34, pred[512,640]{0,1:T(8,128)(4,1)S(1)} %compare_and_fusion.1, bf16[128,1,128]{0,2,1:T(8,128)(2,1)S(1)} %copy-done.8, ...), kind=kOutput, calls=%fused_computation.46 | convolution fusion | flops 349241344 | bytes 11665408 | tf_op jit(solution)/shard_map/jgqk,kjd->qjgd/dot_general | solution.py:54
  228.8 0.1 pad_maximum_fusion.1
  229.0 0.0 all-to-all-done.2
  229.0 7.0 %convolution_convert_fusion = bf16[1024,2880]{0,1:T(8,128)(2,1)} fusion(bf16[1024,512]{0,1:T(8,128)(2,1)S(1)} %bitcast.134, bf16[512,2880]{1,0:T(8,128)(2,1)} %bitcast.39), kind=kOutput, calls=%fused_computation.15 | convolution fusion | flops 3022848000 | bytes 9895936 | tf_op jit(solution)/shard_map/dot_general | solution.py:167
  236.0 8.5 %copy.62 = bf16[1024,2880]{1,0:T(8,128)(2,1)} copy(bf16[1024,2880]{0,1:T(8,128)(2,1)} %convolution_convert_fusion) | data formatting | bytes 11796480
  244.5 0.0 reduce-scatter.4.cloned.1.call-update
  244.5 42.0 %reduce-scatter.4.cloned.1.call-done = bf16[128,2880]{1,0:T(8,128)(2,1)} async-done(((bf16[1024,2880]{1,0:T(8,128)(2,1)}), bf16[128,2880]{1,0:T(8,128)(2,1)}) %reduce-scatter.4.cloned.1.call-update) | async-done | bytes 737296
  286.6 1.5 copy.63
  288.0 0.0 copy-done.13
  288.1 1.3 fusion.28
  (38 shorter events, 0.1 us)
Async XLA Ops:
  6.5 114.6 %all-gather.3.cloned.1.call-start = ((), (), s32[]{:S(2)}) async-start(), calls=%async_computation.4 | async-start | bytes 7603200 | tf_op jit(solution)/shard_map/all_gather | solution.py:81
  15.6 49.7 %all-to-all-start = ((bf16[1,8,8,10,2880]{4,1,3,0,2:T(8,128)(2,1)}), bf16[1,8,8,10,2880]{4,1,3,0,2:T(8,128)(2,1)}, u32[]{:S(2)}, u32[]{:S(2)}) async-start(bf16[1,8,8,10,2880]{4,1,3,0,2:T(8,128)(2,1)} %copy.65), calls=%async_computation | async-start | bytes 7536640 | tf_op jit(solution)/shard_map/all_to_all | solution.py:97
  24.7 45.1 %copy-start.17 = (s32[128,4]{0,1:T(4,128)S(1)}, s32[128,4]{0,1:T(4,128)}, u32[]{:S(2)}) copy-start(s32[128,4]{0,1:T(4,128)} %param.16) | copy-start | bytes 6148
  24.7 45.2 %copy-start.18 = (s32[128,4]{0,1:T(4,128)S(1)}, s32[128,4]{0,1:T(4,128)}, u32[]{:S(2)}) copy-start(s32[128,4]{0,1:T(4,128)} %param.14) | copy-start | bytes 6148
  24.7 45.3 %copy-start.16 = (f32[128,4]{0,1:T(4,128)S(1)}, f32[128,4]{0,1:T(4,128)}, u32[]{:S(2)}) copy-start(f32[128,4]{0,1:T(4,128)} %param.15) | copy-start | bytes 6148
  65.3 49.6 %all-to-all-start.1 = ((bf16[1,8,8,10,2880]{4,1,3,0,2:T(8,128)(2,1)}), bf16[1,8,8,10,2880]{4,1,3,0,2:T(8,128)(2,1)}, u32[]{:S(2)}, u32[]{:S(2)}) async-start(bf16[1,8,8,10,2880]{4,1,3,0,2:T(8,128)(2,1)} %copy.66), calls=%async_computation.1 | async-start | bytes 7536640 | tf_op jit(solution)/shard_map/all_to_all | solution.py:97
  69.8 106.1 %all-gather.5.cloned.1.call-start = ((), (), s32[]{:S(2)}) async-start(), calls=%async_computation.5 | async-start | bytes 6635520 | tf_op jit(solution)/shard_map/all_gather | solution.py:117
  121.1 5.7 %copy-start = (f32[256,2880]{0,1:T(8,128)S(1)}, f32[256,2880]{0,1:T(8,128)}, u32[]{:S(2)}) copy-start(f32[256,2880]{0,1:T(8,128)} %fusion.16) | copy-start | bytes 8847364
  121.1 5.8 %copy-start.3 = (bf16[128,2880]{0,1:T(8,128)(2,1)S(1)}, bf16[128,2880]{0,1:T(8,128)(2,1)}, u32[]{:S(2)}) copy-start(bf16[128,2880]{0,1:T(8,128)(2,1)} %param.13) | copy-start | bytes 2211844
  126.9 0.7 copy-start.12
  126.9 2.0 copy-start.4
  130.8 12.1 %copy-start.15 = (f32[1,640]{1,0:T(1,128)S(1)}, f32[1,640]{1,0:T(1,128)}, u32[]{:S(2)}) copy-start(f32[1,640]{1,0:T(1,128)} %param.20) | copy-start | bytes 7684
  130.8 12.1 %copy-start.10 = (s32[1024]{0:T(1024)S(1)}, s32[1024]{0:T(1024)}, u32[]{:S(2)}) copy-start(s32[1024]{0:T(1024)} %param.17) | copy-start | bytes 12292
  130.8 98.2 %all-to-all-start.2 = ((bf16[32,16,2880]{2,1,0:T(8,128)(2,1)}), bf16[32,16,2880]{2,1,0:T(8,128)(2,1)}, u32[]{:S(2)}, u32[]{:S(2)}) async-start(bf16[32,16,2880]{2,1,0:T(8,128)(2,1)} %broadcast_in_dim.33), calls=%async_computation.2 | async-start | bytes 6029312 | tf_op jit(solution)/shard_map/all_to_all | solution.py:62
  142.6 144.0 %reduce-scatter.4.cloned.1.call-start = ((), (), s32[]{:S(2)}) async-start(), calls=%async_computation.6 | async-start | bytes 6782976
  184.4 4.6 %copy-start.11 = (bf16[1024,1,640]{0,2,1:T(8,128)(2,1)}, bf16[1024,1,640]{0,2,1:T(8,128)(2,1)S(1)}, u32[]{:S(2)}) copy-start(bf16[1024,1,640]{0,2,1:T(8,128)(2,1)S(1)} %get-tuple-element.31) | copy-start | bytes 3932164
  185.0 24.8 %copy-start.1 = (bf16[1024,1,32]{0,2,1:T(8,128)(2,1)}, bf16[1024,1,32]{0,2,1:T(8,128)(2,1)S(1)}, u32[]{:S(2)}) copy-start(bf16[1024,1,32]{0,2,1:T(8,128)(2,1)S(1)} %get-tuple-element.18) | copy-start | bytes 196612
  185.2 24.6 %collective-permute-start = (bf16[128,1,128]{0,2,1:T(8,128)(2,1)S(1)}, bf16[128,1,128]{0,2,1:T(8,128)(2,1)S(1)}, u32[]{:S(2)}, u32[]{:S(2)}) collective-permute-start(bf16[128,1,128]{0,2,1:T(8,128)(2,1)S(1)} %pad_maximum_fusion.11), channel_id=1, source_target_pairs={{0,8},{8,16},{16,24},{24,32},{32,40},{40,48},{48,56},{56,64},{64,7... | collective-permute-start | bytes 98312 | tf_op jit(solution)/shard_map/ppermute | solution.py:19
  190.7 20.8 %copy-start.14 = (f32[1,8]{1,0:T(1,128)S(1)}, f32[1,8]{1,0:T(1,128)}, u32[]{:S(2)}) copy-start(f32[1,8]{1,0:T(1,128)} %param.21) | copy-start | bytes 100
  209.8 1.8 copy-start.7
  217.1 4.3 %copy-start.5 = (f32[8,512]{1,0:T(8,128)S(1)}, f32[8,512]{1,0:T(8,128)}, u32[]{:S(2)}) copy-start(f32[8,512]{1,0:T(8,128)} %get-tuple-element.30) | copy-start | bytes 49156
  221.4 4.3 %copy-start.2 = (bf16[1024,1,32]{0,2,1:T(8,128)(2,1)S(1)}, bf16[1024,1,32]{0,2,1:T(8,128)(2,1)}, u32[]{:S(2)}) copy-start(bf16[1024,1,32]{0,2,1:T(8,128)(2,1)} %copy-done.1) | copy-start | bytes 196612
  221.4 4.3 %copy-start.6 = (f32[8,512]{1,0:T(8,128)S(1)}, f32[8,512]{1,0:T(8,128)}, u32[]{:S(2)}) copy-start(f32[8,512]{1,0:T(8,128)} %broadcast_maximum_fusion.1) | copy-start | bytes 49156
  221.4 4.3 %copy-start.8 = (bf16[128,1,128]{0,2,1:T(8,128)(2,1)S(1)}, bf16[128,1,128]{0,2,1:T(8,128)(2,1)}, u32[]{:S(2)}) copy-start(bf16[128,1,128]{0,2,1:T(8,128)(2,1)} %copy-done.7) | copy-start | bytes 98308
  221.4 4.3 %copy-start.9 = (f32[8,512]{1,0:T(8,128)S(1)}, f32[8,512]{1,0:T(8,128)}, u32[]{:S(2)}) copy-start(f32[8,512]{1,0:T(8,128)} %get-tuple-element.29) | copy-start | bytes 49156
  244.5 43.6 %copy-start.13 = (f32[2880]{0:T(1024)S(1)}, f32[2880]{0:T(1024)}, u32[]{:S(2)}) copy-start(f32[2880]{0:T(1024)} %param.23) | copy-start | bytes 34564
Sparse Core Ops, SparseCore 0:
  9.9 95.2 all-gather.2
  129.0 46.7 all-gather.4
  244.6 41.8 reduce-scatter.3

commit v5 on v3

--- a/solution.py
+++ b/solution.py
@@ -126,27 +126,31 @@
         [key_part, projected_rows[..., (QUERY_PER_KV + 1) * HEAD_SIZE :]], axis=-1
     ).astype(jnp.bfloat16)
     before = passed_along(keys_values[block_rows - KEYS_VISIBLE :], "fsdp", 1)
-    extended = jnp.concatenate([before, keys_values], axis=0)
     query_block = min(512, block_rows)
-    outputs_list = []
-    for first_row in range(0, block_rows, query_block):
-        key_rows = extended[first_row : first_row + query_block + KEYS_VISIBLE]
+
+    def one_query_block(first_row, key_rows):
         key_pos = (
             block_start
             - KEYS_VISIBLE
             + first_row
             + jnp.arange(query_block + KEYS_VISIBLE, dtype=jnp.int32)
         )
-        outputs_list.append(
-            attend_block(
-                query_rows[first_row : first_row + query_block],
-                key_rows,
-                positions[first_row : first_row + query_block],
-                key_pos,
-                doc_start[first_row : first_row + query_block],
-                sinks,
-            )
+        return attend_block(
+            query_rows[first_row : first_row + query_block],
+            key_rows,
+            positions[first_row : first_row + query_block],
+            key_pos,
+            doc_start[first_row : first_row + query_block],
+            sinks,
         )
+
+    later = [
+        one_query_block(first_row, keys_values[first_row - KEYS_VISIBLE : first_row + query_block])
+        for first_row in range(query_block, block_rows, query_block)
+    ]
+    before, later = lax.optimization_barrier((before, later))
+    extended = jnp.concatenate([before, keys_values[: query_block]], axis=0)
+    outputs_list = [one_query_block(0, extended)] + later
     attention_result = jnp.concatenate(outputs_list, axis=0).reshape(block_rows, -1)
     out_full, attention_result = lax.optimization_barrier((out_full, attention_result))
     output_weights = out_full.reshape(-1, model_width)

time: 289 us -> 277 us (0.958)
  waiting for transfers between devices: 177 us -> 171 us
  other arithmetic: 16.7 us -> 11.5 us
    ppermute x1, waiting for transfers between devices: 18.9 us -> 13.4 us  [passed_along(): return lax.ppermute(block, axis, route)]
    unnamed x40 -> x24, local copies, waits for them, and re-layouts: 19.5 us -> 19.4 us
  transfers between devices with their start and end apart: 6 -> 6, of which waited for: 4 -> 4; matrix products, arithmetic and copies ran while one was open for 17% -> 16% of each run, Pallas kernels for 0% -> 0%
where the time goes in v5:
time: 277 us; the launch traced here: 276 us
  waiting for transfers between devices  171 us (62%)
  matrix products  31.8 us (11%)
  local copies, waits for them, and re-layouts  28.3 us (10%)
  starting transfers between devices  20.3 us (7%)
  between operations  13.5 us (5%)
  other arithmetic  11.5 us (4%)
    all_to_all x1, waiting for transfers between devices, shards(): lax.all_to_all(expert_rows, 'expert', split_axis=2, concat_axis=1, tiled=...  84 us
    unnamed x4, waiting for transfers between devices  42.1 us
    all_gather x1, waiting for transfers between devices, shards(): gathered = lax.all_gather(normalized_rows, 'expert', axis=0, tiled=True)  31.7 us
    unnamed x24, local copies, waits for them, and re-layouts  19.4 us
    ppermute x1, waiting for transfers between devices, passed_along(): return lax.ppermute(block, axis, route)  13.4 us
    all_to_all x1, starting transfers between devices, gather_fsdp(): lax.all_to_all(spread, 'fsdp', split_axis=0, concat_axis=0, tiled=True)  11.7 us
    dot_general x1, matrix products, shards(): jnp.dot(gathered, qkv_full.reshape(model_width, -1), preferred_element_ty...  8.51 us
    dot_general x1, matrix products, shards(): jnp.dot(attention_result, output_weights, preferred_element_type=jnp.floa...  7.03 us
  transfers between devices with their start and end apart: 6, of which 4 were waited for; matrix products, arithmetic and copies ran while one was open for 16% of the time, Pallas kernels for 0%

profile of v5, /device:TPU:2, one launch (start us, length us, event | category | flops | bytes accessed | tf_op | source)
XLA Modules:
  0.0 276.4 jit_solution(4853821800912047730)
XLA Ops:
  6.5 0.0 all-gather.3.cloned.1.call-start
  6.5 1.8 copy.52
  8.3 0.0 all-gather.3.cloned.1.call-update
  8.3 7.6 %copy.53 = bf16[1,16,8,10,2880]{4,1,3,0,2:T(8,128)(2,1)} copy(bf16[1,16,8,10,2880]{4,2,3,1,0:T(8,128)(2,1)} %param.12) | data formatting | bytes 14745600 | tf_op args[0]
  15.9 0.0 copy-start.8
  15.9 0.0 copy-start.9
  15.9 0.0 copy-start.7
  15.9 5.0 %all-to-all-start = ((bf16[1,16,8,10,2880]{4,1,3,0,2:T(8,128)(2,1)}), bf16[1,16,8,10,2880]{4,1,3,0,2:T(8,128)(2,1)}, u32[]{:S(2)}, u32[]{:S(2)}) async-start(bf16[1,16,8,10,2880]{4,1,3,0,2:T(8,128)(2,1)} %copy.53), calls=%async_computation | async-start | bytes 15073280 | tf_op jit(solution)/shard_map/all_to_all | solution.py:81
  20.9 0.0 all-gather.5.cloned.1.call-start
  21.0 0.0 copy-done.8
  21.0 0.0 copy-done.9
  21.0 0.1 iota_compare_fusion
  21.2 0.0 copy-done.7
  21.2 1.1 select_reduce_fusion
  22.3 0.1 subtract_convert_fusion.1
  22.4 84.0 %all-to-all-done = bf16[1,16,8,10,2880]{4,1,3,0,2:T(8,128)(2,1)} async-done(((bf16[1,16,8,10,2880]{4,1,3,0,2:T(8,128)(2,1)}), bf16[1,16,8,10,2880]{4,1,3,0,2:T(8,128)(2,1)}, u32[]{:S(2)}, u32[]{:S(2)}) %all-to-all-start) | async-done | bytes 7372832 | tf_op jit(solution)/shard_map/all_to_all | solution.py:81
  106.4 6.8 %copy.54 = bf16[1,8,16,1,10,2880]{5,2,1,4,3,0:T(8,128)(2,1)} copy(bf16[1,8,16,1,10,2880]{5,2,4,1,3,0:T(8,128)(2,1)} %bitcast.1) | data formatting | bytes 14745600 | tf_op jit(solution)/shard_map/all_to_all | solution.py:81
  113.3 0.0 all-gather.3.cloned.1.call-done
  113.3 0.0 copy-start
  113.3 6.3 %fusion.10 = f32[256,2880]{0,1:T(8,128)S(1)} fusion(bf16[1,128,1,10,2880]{4,1,3,2,0:T(8,128)(2,1)} %bitcast.116, bf16[128,128,10]{1,0,2:T(8,128)(2,1)S(1)} %get-tuple-element.19, bf16[128,128,10]{1,0,2:T(8,128)(2,1)S(1)} %get-tuple-element.20), kind=kOutput, calls=%fused_computation.17 | convolution fusion | flops 1888747520 | bytes 10977280 | tf_op jit(solution)/shard_map/txs,xsm->tm/dot_general | solution.py:93
  119.6 0.0 copy-done
  119.6 0.0 copy-start.1
  119.6 0.4 fusion.18
  120.0 0.0 copy-start.2
  120.1 0.0 copy-done.3
  120.1 1.3 fusion.20
  121.4 0.0 all-gather.5.cloned.1.call-update
  121.4 0.0 copy-done.1
  121.4 1.9 broadcast_in_dim.33
  123.3 11.7 %all-to-all-start.1 = ((bf16[32,16,2880]{2,1,0:T(8,128)(2,1)}), bf16[32,16,2880]{2,1,0:T(8,128)(2,1)}, u32[]{:S(2)}, u32[]{:S(2)}) async-start(bf16[32,16,2880]{2,1,0:T(8,128)(2,1)} %broadcast_in_dim.33), calls=%async_computation.1 | async-start | bytes 6029312 | tf_op jit(solution)/shard_map/all_to_all | solution.py:62
  135.0 0.2 reduce-scatter.4.cloned.1.call-start
  135.2 0.0 copy-done.6
  135.3 0.0 copy-done.2
  135.3 0.5 multiply_cosine_fusion
  135.9 0.4 compare_and_fusion.1
  136.3 0.4 compare_and_fusion
  136.7 31.7 %all-gather.5.cloned.1.call-done = bf16[1024,2880]{0,1:T(8,128)(2,1)} async-done(((bf16[128,2880]{0,1:T(8,128)(2,1)}), bf16[1024,2880]{0,1:T(8,128)(2,1)}) %all-gather.5.cloned.1.call-update) | async-done | bytes 5898256 | tf_op jit(solution)/shard_map/all_gather | solution.py:104
  168.4 8.5 %fusion.70 = (bf16[1024,1,640]{0,2,1:T(8,128)(2,1)S(1)}, f32[1024,1,640]{0,2,1:T(8,128)S(1)}) fusion(f32[640]{0:T(1024)S(1)} %reduce.4, bf16[1024,2880]{0,1:T(8,128)(2,1)} %all-gather.5.cloned.1.call-done, bf16[2880,1,640]{2,1,0:T(2,128)(2,1)} %all-gather.3.cloned.1.call-done), kind=kOutput, calls=%fused_computation.101 | convolution fusion | flops 3776184320 | bytes 13519360 | tf_op jit(solution)/shard_map/dot_general | solution.py:108
  176.9 0.1 slice.96
  177.1 0.6 fusion.54
  177.7 3.4 %collective-permute-start = (bf16[128,1,128]{0,2,1:T(8,128)(2,1)S(1)}, bf16[128,1,128]{0,2,1:T(8,128)(2,1)S(1)}, u32[]{:S(2)}, u32[]{:S(2)}) collective-permute-start(bf16[128,1,128]{0,2,1:T(8,128)(2,1)S(1)} %pad_maximum_fusion.5), channel_id=1, source_target_pairs={{0,8},{8,16},{16,24},{24,32},{32,40},{40,48},{48,56},{56,64},{64,7... | collective-permute-start | bytes 98312 | tf_op jit(solution)/shard_map/ppermute | solution.py:19
  181.1 0.3 add_convert_fusion
  181.4 0.0 copy-start.5
  181.4 1.7 fusion.2
  183.2 0.0 copy-done.5
  183.2 0.1 broadcast_maximum_fusion.1
  183.2 2.2 fusion
  185.4 0.1 exponential_add_fusion.1
  185.5 3.3 %fusion.34 = bf16[512,1,8,64]{0,3,2,1:T(8,128)(2,1)S(1)} fusion(f32[8,512]{1,0:T(8,128)S(1)} %exponential_add_fusion.1, f32[8,512]{1,0:T(8,128)S(1)} %broadcast_maximum_fusion.1, f32[640,512,8]{1,0,2:T(8,128)S(1)} %get-tuple-element.36, pred[512,640]{0,1:T(8,128)(4,1)S(1)} %compare_and_fusion.1, bf16[1024,1,640]{0,2,1:T(8,128)(2,1)S(1)} %get-tuple-element.33), kind=kOutput, calls=%fused_computation.39 | convolution fusion | flops 348913664 | bytes 11452416 | tf_op jit(solution)/shard_map/jgqk,kjd->qjgd/dot_general | solution.py:54
  188.8 13.4 %collective-permute-done = bf16[128,1,128]{0,2,1:T(8,128)(2,1)S(1)} collective-permute-done((bf16[128,1,128]{0,2,1:T(8,128)(2,1)S(1)}, bf16[128,1,128]{0,2,1:T(8,128)(2,1)S(1)}, u32[]{:S(2)}, u32[]{:S(2)}) %collective-permute-start) | collective-permute-done | bytes 32800 | tf_op jit(solution)/shard_map/ppermute | solution.py:19
  202.2 1.8 fusion.3
  204.0 0.1 broadcast_maximum_fusion
  204.0 2.2 fusion.1
  206.2 0.1 exponential_add_fusion
  206.3 3.1 %fusion.31 = bf16[512,1,8,64]{0,3,2,1:T(8,128)(2,1)S(1)} fusion(f32[8,512]{1,0:T(8,128)S(1)} %exponential_add_fusion, f32[8,512]{1,0:T(8,128)S(1)} %broadcast_maximum_fusion, f32[640,512,8]{1,0,2:T(8,128)S(1)} %get-tuple-element.38, pred[512,640]{0,1:T(8,128)(4,1)S(1)} %compare_and_fusion, bf16[640,1,128]{0,2,1:T(8,128)(2,1)S(1)} %fusion.52), kind=kOutput, calls=%fused_computation.38 | convolution fusion | flops 348913664 | bytes 11452416 | tf_op jit(solution)/shard_map/jgqk,kjd->qjgd/dot_general | solution.py:54
  209.4 0.1 pad_maximum_fusion
  209.5 0.0 all-to-all-done.1
  209.5 7.0 %convolution_convert_fusion = bf16[1024,2880]{0,1:T(8,128)(2,1)} fusion(bf16[1024,512]{0,1:T(8,128)(2,1)S(1)} %bitcast.117, bf16[512,2880]{1,0:T(8,128)(2,1)} %bitcast.30), kind=kOutput, calls=%fused_computation.12 | convolution fusion | flops 3022848000 | bytes 9895936 | tf_op jit(solution)/shard_map/dot_general | solution.py:158
  216.5 8.5 %copy.61 = bf16[1024,2880]{1,0:T(8,128)(2,1)} copy(bf16[1024,2880]{0,1:T(8,128)(2,1)} %convolution_convert_fusion) | data formatting | bytes 11796480
  225.0 0.0 reduce-scatter.4.cloned.1.call-update
  225.1 42.0 %reduce-scatter.4.cloned.1.call-done = bf16[128,2880]{1,0:T(8,128)(2,1)} async-done(((bf16[1024,2880]{1,0:T(8,128)(2,1)}), bf16[128,2880]{1,0:T(8,128)(2,1)}) %reduce-scatter.4.cloned.1.call-update) | async-done | bytes 737296
  267.1 1.5 copy.62
  268.6 0.0 copy-done.4
  268.6 1.3 fusion.22
  (15 shorter events, 0.1 us)
Async XLA Ops:
  6.5 106.7 %all-gather.3.cloned.1.call-start = ((), (), s32[]{:S(2)}) async-start(), calls=%async_computation.3 | async-start | bytes 7603200 | tf_op jit(solution)/shard_map/all_gather | solution.py:82
  15.9 5.1 %copy-start.8 = (s32[128,4]{0,1:T(4,128)S(1)}, s32[128,4]{0,1:T(4,128)}, u32[]{:S(2)}) copy-start(s32[128,4]{0,1:T(4,128)} %param.16) | copy-start | bytes 6148
  15.9 5.1 %copy-start.9 = (s32[128,4]{0,1:T(4,128)S(1)}, s32[128,4]{0,1:T(4,128)}, u32[]{:S(2)}) copy-start(s32[128,4]{0,1:T(4,128)} %param.14) | copy-start | bytes 6148
  15.9 5.2 %copy-start.7 = (f32[128,4]{0,1:T(4,128)S(1)}, f32[128,4]{0,1:T(4,128)}, u32[]{:S(2)}) copy-start(f32[128,4]{0,1:T(4,128)} %param.15) | copy-start | bytes 6148
  15.9 90.5 %all-to-all-start = ((bf16[1,16,8,10,2880]{4,1,3,0,2:T(8,128)(2,1)}), bf16[1,16,8,10,2880]{4,1,3,0,2:T(8,128)(2,1)}, u32[]{:S(2)}, u32[]{:S(2)}) async-start(bf16[1,16,8,10,2880]{4,1,3,0,2:T(8,128)(2,1)} %copy.53), calls=%async_computation | async-start | bytes 15073280 | tf_op jit(solution)/shard_map/all_to_all | solution.py:81
  20.9 147.5 %all-gather.5.cloned.1.call-start = ((), (), s32[]{:S(2)}) async-start(), calls=%async_computation.4 | async-start | bytes 6635520 | tf_op jit(solution)/shard_map/all_gather | solution.py:104
  113.3 6.4 %copy-start = (bf16[128,2880]{0,1:T(8,128)(2,1)S(1)}, bf16[128,2880]{0,1:T(8,128)(2,1)}, u32[]{:S(2)}) copy-start(bf16[128,2880]{0,1:T(8,128)(2,1)} %param.13) | copy-start | bytes 2211844
  113.3 6.8 %copy-start.3 = (f32[2880]{0:T(1024)S(1)}, f32[2880]{0:T(1024)}, u32[]{:S(2)}) copy-start(f32[2880]{0:T(1024)} %param.18) | copy-start | bytes 34564
  119.6 1.8 copy-start.1
  120.0 15.2 %copy-start.6 = (f32[1,640]{1,0:T(1,128)S(1)}, f32[1,640]{1,0:T(1,128)}, u32[]{:S(2)}) copy-start(f32[1,640]{1,0:T(1,128)} %param.20) | copy-start | bytes 7684
  120.0 15.3 %copy-start.2 = (s32[1024]{0:T(1024)S(1)}, s32[1024]{0:T(1024)}, u32[]{:S(2)}) copy-start(s32[1024]{0:T(1024)} %param.17) | copy-start | bytes 12292
  123.3 86.2 %all-to-all-start.1 = ((bf16[32,16,2880]{2,1,0:T(8,128)(2,1)}), bf16[32,16,2880]{2,1,0:T(8,128)(2,1)}, u32[]{:S(2)}, u32[]{:S(2)}) async-start(bf16[32,16,2880]{2,1,0:T(8,128)(2,1)} %broadcast_in_dim.33), calls=%async_computation.1 | async-start | bytes 6029312 | tf_op jit(solution)/shard_map/all_to_all | solution.py:62
  135.0 132.1 %reduce-scatter.4.cloned.1.call-start = ((), (), s32[]{:S(2)}) async-start(), calls=%async_computation.5 | async-start | bytes 6782976
  177.7 24.5 %collective-permute-start = (bf16[128,1,128]{0,2,1:T(8,128)(2,1)S(1)}, bf16[128,1,128]{0,2,1:T(8,128)(2,1)S(1)}, u32[]{:S(2)}, u32[]{:S(2)}) collective-permute-start(bf16[128,1,128]{0,2,1:T(8,128)(2,1)S(1)} %pad_maximum_fusion.5), channel_id=1, source_target_pairs={{0,8},{8,16},{16,24},{24,32},{32,40},{40,48},{48,56},{56,64},{64,7... | collective-permute-start | bytes 98312 | tf_op jit(solution)/shard_map/ppermute | solution.py:19
  181.4 1.8 copy-start.5
  225.0 43.6 %copy-start.4 = (f32[2880]{0:T(1024)S(1)}, f32[2880]{0:T(1024)}, u32[]{:S(2)}) copy-start(f32[2880]{0:T(1024)} %param.23) | copy-start | bytes 34564
Sparse Core Ops, SparseCore 0:
  9.9 95.1 all-gather.2
  121.5 46.8 all-gather.4
  225.2 41.8 reduce-scatter.3

commit v6 on v5

--- a/solution.py
+++ b/solution.py
@@ -1,6 +1,7 @@
 import jax
 import jax.numpy as jnp
 from jax import lax
+from jax.experimental.layout import Layout, with_layout_constraint
 from jax.sharding import PartitionSpec as P
 
 HEAD_SIZE = 64
@@ -154,10 +155,14 @@
     attention_result = jnp.concatenate(outputs_list, axis=0).reshape(block_rows, -1)
     out_full, attention_result = lax.optimization_barrier((out_full, attention_result))
     output_weights = out_full.reshape(-1, model_width)
-    projection_step = lax.psum_scatter(
+    projection_step = with_layout_constraint(
         jnp.dot(attention_result, output_weights, preferred_element_type=jnp.float32).astype(
             jnp.bfloat16
         ),
+        Layout((0, 1)),
+    )
+    projection_step = lax.psum_scatter(
+        projection_step,
         "expert",
         scatter_dimension=0,
         tiled=True,

time: 277 us -> 266 us (0.960)
  local copies, waits for them, and re-layouts: 28.3 us -> 19.8 us
    reduce_scatter x0 -> x1, waiting for transfers between devices: none -> 42.1 us  [shards(): lax.psum_scatter(projection_step, 'expert', scatter_dimension=0, tiled=True)]
    unnamed x4 -> x3, waiting for transfers between devices: 42.1 us -> 0.05 us
    unnamed x24 -> x23, local copies, waits for them, and re-layouts: 19.4 us -> 9.76 us
    ppermute x1, waiting for transfers between devices: 13.4 us -> 16.7 us  [passed_along(): return lax.ppermute(block, axis, route)]
    all_gather x1, waiting for transfers between devices: 31.7 us -> 28.4 us  [shards(): gathered = lax.all_gather(normalized_rows, 'expert', axis=0, tiled=True)]
where the time goes in v6:
time: 266 us
  waiting for transfers between devices  171 us (64%)
  matrix products  29.9 us (11%)
  starting transfers between devices  20.4 us (8%)
  local copies, waits for them, and re-layouts  19.8 us (7%)
  between operations  13.5 us (5%)
  other arithmetic  11.3 us (4%)
    all_to_all x1, waiting for transfers between devices, shards(): lax.all_to_all(expert_rows, 'expert', split_axis=2, concat_axis=1, tiled=...  83.6 us
    reduce_scatter x1, waiting for transfers between devices, shards(): lax.psum_scatter(projection_step, 'expert', scatter_dimension=0, tiled=True)  42.1 us
    all_gather x1, waiting for transfers between devices, shards(): gathered = lax.all_gather(normalized_rows, 'expert', axis=0, tiled=True)  28.4 us
    ppermute x1, waiting for transfers between devices, passed_along(): return lax.ppermute(block, axis, route)  16.7 us
    all_to_all x1, starting transfers between devices, gather_fsdp(): lax.all_to_all(spread, 'fsdp', split_axis=0, concat_axis=0, tiled=True)  11.7 us
    unnamed x23, local copies, waits for them, and re-layouts  9.76 us
    dot_general x1, matrix products, shards(): jnp.dot(gathered, qkv_full.reshape(model_width, -1), preferred_element_ty...  8.53 us
    dot_general x1, matrix products, shards(): jnp.dot(attention_result, output_weights, preferred_element_type=jnp.floa...  7.19 us
  transfers between devices with their start and end apart: 6, of which 4 were waited for; matrix products, arithmetic and copies ran while one was open for 16% of the time, Pallas kernels for 0%

profile of v6, /device:TPU:2, one launch (start us, length us, event | category | flops | bytes accessed | tf_op | source)
XLA Modules:
  0.0 265.7 jit_solution(4478010216262861890)
XLA Ops:
  6.5 0.0 all-gather.3.cloned.1.call-start
  6.5 1.8 copy.73
  8.3 0.0 all-gather.3.cloned.1.call-update
  8.3 7.6 %copy.74 = bf16[1,16,8,10,2880]{4,1,3,0,2:T(8,128)(2,1)} copy(bf16[1,16,8,10,2880]{4,2,3,1,0:T(8,128)(2,1)} %param.12) | data formatting | bytes 14745600 | tf_op args[0]
  15.9 0.0 copy-start
  15.9 0.0 copy-start.8
  15.9 0.0 copy-start.9
  15.9 0.0 copy-start.7
  15.9 5.0 %all-to-all-start = ((bf16[1,16,8,10,2880]{4,1,3,0,2:T(8,128)(2,1)}), bf16[1,16,8,10,2880]{4,1,3,0,2:T(8,128)(2,1)}, u32[]{:S(2)}, u32[]{:S(2)}) async-start(bf16[1,16,8,10,2880]{4,1,3,0,2:T(8,128)(2,1)} %copy.74), calls=%async_computation | async-start | bytes 15073280 | tf_op jit(solution)/shard_map/all_to_all | solution.py:82
  20.9 0.0 all-gather.5.cloned.1.call-start
  21.0 0.0 copy-done
  21.0 0.3 copy.72
  21.4 0.0 copy-done.8
  21.4 0.0 copy-done.9
  21.4 0.1 iota_compare_fusion
  21.5 0.0 copy-done.7
  21.5 1.1 select_reduce_fusion
  22.7 0.1 subtract_convert_fusion.1
  22.8 83.6 %all-to-all-done = bf16[1,16,8,10,2880]{4,1,3,0,2:T(8,128)(2,1)} async-done(((bf16[1,16,8,10,2880]{4,1,3,0,2:T(8,128)(2,1)}), bf16[1,16,8,10,2880]{4,1,3,0,2:T(8,128)(2,1)}, u32[]{:S(2)}, u32[]{:S(2)}) %all-to-all-start) | async-done | bytes 7372832 | tf_op jit(solution)/shard_map/all_to_all | solution.py:82
  106.4 6.8 %copy.75 = bf16[1,8,16,1,10,2880]{5,2,1,4,3,0:T(8,128)(2,1)} copy(bf16[1,8,16,1,10,2880]{5,2,4,1,3,0:T(8,128)(2,1)} %bitcast.1) | data formatting | bytes 14745600 | tf_op jit(solution)/shard_map/all_to_all | solution.py:82
  113.3 4.5 %fusion.10 = f32[256,2880]{1,0:T(8,128)S(1)} fusion(bf16[1,128,1,10,2880]{4,1,3,2,0:T(8,128)(2,1)} %bitcast.117, bf16[128,128,10]{1,0,2:T(8,128)(2,1)S(1)} %get-tuple-element.19, bf16[128,128,10]{1,0,2:T(8,128)(2,1)S(1)} %get-tuple-element.20), kind=kOutput, calls=%fused_computation.17 | convolution fusion | flops 1888747520 | bytes 10977280 | tf_op jit(solution)/shard_map/txs,xsm->tm/dot_general | solution.py:94
  117.8 0.0 copy-start.1
  117.8 0.4 fusion.18
  118.2 0.0 copy-start.6
  118.2 0.0 copy-start.2
  118.3 0.0 copy-done.3
  118.3 1.1 fusion.20
  119.4 0.0 all-gather.5.cloned.1.call-update
  119.4 0.0 copy-done.1
  119.4 1.8 broadcast_in_dim.33
  121.2 11.7 %all-to-all-start.1 = ((bf16[32,16,2880]{2,1,0:T(8,128)(2,1)}), bf16[32,16,2880]{2,1,0:T(8,128)(2,1)}, u32[]{:S(2)}, u32[]{:S(2)}) async-start(bf16[32,16,2880]{2,1,0:T(8,128)(2,1)} %broadcast_in_dim.33), calls=%async_computation.1 | async-start | bytes 6029312 | tf_op jit(solution)/shard_map/all_to_all | solution.py:63
  132.9 0.0 reduce-scatter.2.cloned.1.call-start
  133.0 0.0 copy-done.6
  133.0 0.0 copy-done.2
  133.1 0.5 multiply_cosine_fusion
  133.6 0.4 compare_and_fusion.1
  134.0 0.4 compare_and_fusion
  134.4 28.4 %all-gather.5.cloned.1.call-done = bf16[1024,2880]{1,0:T(8,128)(2,1)} async-done(((bf16[128,2880]{1,0:T(8,128)(2,1)}), bf16[1024,2880]{1,0:T(8,128)(2,1)}) %all-gather.5.cloned.1.call-update) | async-done | bytes 5898256 | tf_op jit(solution)/shard_map/all_gather | solution.py:105
  162.9 8.5 %fusion.70 = (bf16[1024,1,640]{0,2,1:T(8,128)(2,1)S(1)}, f32[1024,1,640]{0,2,1:T(8,128)S(1)}) fusion(f32[640]{0:T(1024)S(1)} %reduce.4, bf16[1024,2880]{1,0:T(8,128)(2,1)} %all-gather.5.cloned.1.call-done, bf16[2880,1,640]{2,1,0:T(2,128)(2,1)} %all-gather.3.cloned.1.call-done), kind=kOutput, calls=%fused_computation.101 | convolution fusion | flops 3776184320 | bytes 13519360 | tf_op jit(solution)/shard_map/dot_general | solution.py:109
  171.4 0.2 slice.96
  171.7 0.6 fusion.54
  172.3 3.6 %collective-permute-start = (bf16[128,1,128]{0,2,1:T(8,128)(2,1)S(1)}, bf16[128,1,128]{0,2,1:T(8,128)(2,1)S(1)}, u32[]{:S(2)}, u32[]{:S(2)}) collective-permute-start(bf16[128,1,128]{0,2,1:T(8,128)(2,1)S(1)} %pad_maximum_fusion.5), channel_id=1, source_target_pairs={{0,8},{8,16},{16,24},{24,32},{32,40},{40,48},{48,56},{56,64},{64,7... | collective-permute-start | bytes 98312 | tf_op jit(solution)/shard_map/ppermute | solution.py:20
  175.9 0.3 add_convert_fusion
  176.3 0.0 copy-start.5
  176.3 1.7 fusion.2
  178.0 0.0 copy-done.5
  178.0 0.1 broadcast_maximum_fusion.1
  178.1 2.2 fusion
  180.2 0.1 exponential_add_fusion.1
  180.3 3.1 %fusion.34 = bf16[512,1,8,64]{0,3,2,1:T(8,128)(2,1)S(1)} fusion(f32[8,512]{1,0:T(8,128)S(1)} %exponential_add_fusion.1, f32[8,512]{1,0:T(8,128)S(1)} %broadcast_maximum_fusion.1, f32[640,512,8]{1,0,2:T(8,128)S(1)} %get-tuple-element.36, pred[512,640]{0,1:T(8,128)(4,1)S(1)} %compare_and_fusion.1, bf16[1024,1,640]{0,2,1:T(8,128)(2,1)S(1)} %get-tuple-element.33), kind=kOutput, calls=%fused_computation.39 | convolution fusion | flops 348913664 | bytes 11452416 | tf_op jit(solution)/shard_map/jgqk,kjd->qjgd/dot_general | solution.py:55
  183.4 16.7 %collective-permute-done = bf16[128,1,128]{0,2,1:T(8,128)(2,1)S(1)} collective-permute-done((bf16[128,1,128]{0,2,1:T(8,128)(2,1)S(1)}, bf16[128,1,128]{0,2,1:T(8,128)(2,1)S(1)}, u32[]{:S(2)}, u32[]{:S(2)}) %collective-permute-start) | collective-permute-done | bytes 32800 | tf_op jit(solution)/shard_map/ppermute | solution.py:20
  200.1 1.8 fusion.3
  201.9 0.1 broadcast_maximum_fusion
  201.9 2.2 fusion.1
  204.1 0.1 exponential_add_fusion
  204.2 3.1 %fusion.31 = bf16[512,1,8,64]{0,3,2,1:T(8,128)(2,1)S(1)} fusion(f32[8,512]{1,0:T(8,128)S(1)} %exponential_add_fusion, f32[8,512]{1,0:T(8,128)S(1)} %broadcast_maximum_fusion, f32[640,512,8]{1,0,2:T(8,128)S(1)} %get-tuple-element.38, pred[512,640]{0,1:T(8,128)(4,1)S(1)} %compare_and_fusion, bf16[640,1,128]{0,2,1:T(8,128)(2,1)S(1)} %fusion.52), kind=kOutput, calls=%fused_computation.38 | convolution fusion | flops 348913664 | bytes 11452416 | tf_op jit(solution)/shard_map/jgqk,kjd->qjgd/dot_general | solution.py:55
  207.3 0.1 pad_maximum_fusion
  207.4 0.0 all-to-all-done.1
  207.4 7.2 %convolution_convert_fusion = bf16[1024,2880]{1,0:T(8,128)(2,1)} fusion(bf16[1024,512]{0,1:T(8,128)(2,1)S(1)} %bitcast.118, bf16[512,2880]{1,0:T(8,128)(2,1)} %bitcast.32), kind=kOutput, calls=%fused_computation.12 | convolution fusion | flops 3022848000 | bytes 9895936 | tf_op jit(solution)/shard_map/dot_general | solution.py:159
  214.6 0.0 reduce-scatter.2.cloned.1.call-update
  214.6 42.1 %reduce-scatter.2.cloned.1.call-done = bf16[128,2880]{1,0:T(8,128)(2,1)} async-done(((bf16[1024,2880]{1,0:T(8,128)(2,1)}), bf16[128,2880]{1,0:T(8,128)(2,1)}) %reduce-scatter.2.cloned.1.call-update) | async-done | bytes 737296 | tf_op jit(solution)/shard_map/reduce_scatter | solution.py:164
  256.7 0.0 copy-done.4
  256.7 1.3 fusion.22
  258.0 1.1 copy.81
  (15 shorter events, 0.1 us)
Async XLA Ops:
  6.5 106.7 %all-gather.3.cloned.1.call-start = ((), (), s32[]{:S(2)}) async-start(), calls=%async_computation.3 | async-start | bytes 7603200 | tf_op jit(solution)/shard_map/all_gather | solution.py:83
  15.9 5.1 %copy-start = (bf16[128,2880]{0,1:T(8,128)(2,1)S(1)}, bf16[128,2880]{0,1:T(8,128)(2,1)}, u32[]{:S(2)}) copy-start(bf16[128,2880]{0,1:T(8,128)(2,1)} %param.13) | copy-start | bytes 2211844
  15.9 5.4 %copy-start.8 = (s32[128,4]{0,1:T(4,128)S(1)}, s32[128,4]{0,1:T(4,128)}, u32[]{:S(2)}) copy-start(s32[128,4]{0,1:T(4,128)} %param.16) | copy-start | bytes 6148
  15.9 5.5 %copy-start.9 = (s32[128,4]{0,1:T(4,128)S(1)}, s32[128,4]{0,1:T(4,128)}, u32[]{:S(2)}) copy-start(s32[128,4]{0,1:T(4,128)} %param.14) | copy-start | bytes 6148
  15.9 5.6 %copy-start.7 = (f32[128,4]{0,1:T(4,128)S(1)}, f32[128,4]{0,1:T(4,128)}, u32[]{:S(2)}) copy-start(f32[128,4]{0,1:T(4,128)} %param.15) | copy-start | bytes 6148
  15.9 90.5 %all-to-all-start = ((bf16[1,16,8,10,2880]{4,1,3,0,2:T(8,128)(2,1)}), bf16[1,16,8,10,2880]{4,1,3,0,2:T(8,128)(2,1)}, u32[]{:S(2)}, u32[]{:S(2)}) async-start(bf16[1,16,8,10,2880]{4,1,3,0,2:T(8,128)(2,1)} %copy.74), calls=%async_computation | async-start | bytes 15073280 | tf_op jit(solution)/shard_map/all_to_all | solution.py:82
  20.9 141.9 %all-gather.5.cloned.1.call-start = ((), (), s32[]{:S(2)}) async-start(), calls=%async_computation.4 | async-start | bytes 6782976 | tf_op jit(solution)/shard_map/all_gather | solution.py:105
  113.3 5.0 %copy-start.3 = (f32[2880]{0:T(1024)S(1)}, f32[2880]{0:T(1024)}, u32[]{:S(2)}) copy-start(f32[2880]{0:T(1024)} %param.18) | copy-start | bytes 34564
  117.8 1.6 copy-start.1
  118.2 14.7 %copy-start.6 = (f32[1,640]{1,0:T(1,128)S(1)}, f32[1,640]{1,0:T(1,128)}, u32[]{:S(2)}) copy-start(f32[1,640]{1,0:T(1,128)} %param.20) | copy-start | bytes 7684
  118.2 14.8 %copy-start.2 = (s32[1024]{0:T(1024)S(1)}, s32[1024]{0:T(1024)}, u32[]{:S(2)}) copy-start(s32[1024]{0:T(1024)} %param.17) | copy-start | bytes 12292
  121.2 86.2 %all-to-all-start.1 = ((bf16[32,16,2880]{2,1,0:T(8,128)(2,1)}), bf16[32,16,2880]{2,1,0:T(8,128)(2,1)}, u32[]{:S(2)}, u32[]{:S(2)}) async-start(bf16[32,16,2880]{2,1,0:T(8,128)(2,1)} %broadcast_in_dim.33), calls=%async_computation.1 | async-start | bytes 6029312 | tf_op jit(solution)/shard_map/all_to_all | solution.py:63
  132.9 123.8 %reduce-scatter.2.cloned.1.call-start = ((), (), s32[]{:S(2)}) async-start(), calls=%async_computation.5 | async-start | bytes 6782976 | tf_op jit(solution)/shard_map/reduce_scatter | solution.py:164
  172.3 27.8 %collective-permute-start = (bf16[128,1,128]{0,2,1:T(8,128)(2,1)S(1)}, bf16[128,1,128]{0,2,1:T(8,128)(2,1)S(1)}, u32[]{:S(2)}, u32[]{:S(2)}) collective-permute-start(bf16[128,1,128]{0,2,1:T(8,128)(2,1)S(1)} %pad_maximum_fusion.5), channel_id=1, source_target_pairs={{0,8},{8,16},{16,24},{24,32},{32,40},{40,48},{48,56},{56,64},{64,7... | collective-permute-start | bytes 98312 | tf_op jit(solution)/shard_map/ppermute | solution.py:20
  176.3 1.8 copy-start.5
  214.6 42.1 %copy-start.4 = (f32[2880]{0:T(1024)S(1)}, f32[2880]{0:T(1024)}, u32[]{:S(2)}) copy-start(f32[2880]{0:T(1024)} %param.23) | copy-start | bytes 34564
Sparse Core Ops, SparseCore 0:
  9.9 95.1 all-gather.2
  119.5 43.2 all-gather.4
  214.7 41.8 reduce-scatter.1

commit v7 on v6

--- a/solution.py
+++ b/solution.py
@@ -127,31 +127,39 @@
         [key_part, projected_rows[..., (QUERY_PER_KV + 1) * HEAD_SIZE :]], axis=-1
     ).astype(jnp.bfloat16)
     before = passed_along(keys_values[block_rows - KEYS_VISIBLE :], "fsdp", 1)
-    query_block = min(512, block_rows)
+    head_rows = min(KEYS_VISIBLE, block_rows)
+    body_rows = (block_rows - head_rows) // 2
 
-    def one_query_block(first_row, key_rows):
+    def one_query_block(first_row, query_count, key_rows):
         key_pos = (
             block_start
             - KEYS_VISIBLE
             + first_row
-            + jnp.arange(query_block + KEYS_VISIBLE, dtype=jnp.int32)
+            + jnp.arange(query_count + KEYS_VISIBLE, dtype=jnp.int32)
         )
         return attend_block(
-            query_rows[first_row : first_row + query_block],
+            query_rows[first_row : first_row + query_count],
             key_rows,
-            positions[first_row : first_row + query_block],
+            positions[first_row : first_row + query_count],
             key_pos,
-            doc_start[first_row : first_row + query_block],
+            doc_start[first_row : first_row + query_count],
             sinks,
         )
 
     later = [
-        one_query_block(first_row, keys_values[first_row - KEYS_VISIBLE : first_row + query_block])
-        for first_row in range(query_block, block_rows, query_block)
+        one_query_block(
+            first_row,
+            query_count,
+            keys_values[first_row - KEYS_VISIBLE : first_row + query_count],
+        )
+        for first_row, query_count in (
+            (head_rows, body_rows),
+            (head_rows + body_rows, block_rows - head_rows - body_rows),
+        )
     ]
     before, later = lax.optimization_barrier((before, later))
-    extended = jnp.concatenate([before, keys_values[: query_block]], axis=0)
-    outputs_list = [one_query_block(0, extended)] + later
+    extended = jnp.concatenate([before, keys_values[:head_rows]], axis=0)
+    outputs_list = [one_query_block(0, head_rows, extended)] + later
     attention_result = jnp.concatenate(outputs_list, axis=0).reshape(block_rows, -1)
     out_full, attention_result = lax.optimization_barrier((out_full, attention_result))
     output_weights = out_full.reshape(-1, model_width)

time: 266 us -> 260 us (0.977)
  waiting for transfers between devices: 171 us -> 162 us
    ppermute x1, waiting for transfers between devices: 16.7 us -> 8.69 us  [passed_along(): return lax.ppermute(block, axis, route)]
    dot_general x2 -> x3, matrix products: 6.18 us -> 5.71 us  [attend_block(): jnp.einsum('jgqk,kjd->qjgd', weights_soft, values_only, preferred_element...]
  transfers between devices with their start and end apart: 6 -> 6, of which waited for: 4 -> 5; matrix products, arithmetic and copies ran while one was open for 16% -> 18% of each run, Pallas kernels for 0% -> 0%
where the time goes in v7:
time: 260 us
  waiting for transfers between devices  162 us (62%)
  matrix products  30.8 us (12%)
  starting transfers between devices  20.6 us (8%)
  local copies, waits for them, and re-layouts  19.9 us (8%)
  between operations  13.5 us (5%)
  other arithmetic  12.6 us (5%)
    all_to_all x1, waiting for transfers between devices, shards(): lax.all_to_all(expert_rows, 'expert', split_axis=2, concat_axis=1, tiled=...  83.6 us
    reduce_scatter x1, waiting for transfers between devices, shards(): lax.psum_scatter(projection_step, 'expert', scatter_dimension=0, tiled=True)  41.2 us
    all_gather x1, waiting for transfers between devices, shards(): gathered = lax.all_gather(normalized_rows, 'expert', axis=0, tiled=True)  28 us
    all_to_all x1, starting transfers between devices, gather_fsdp(): lax.all_to_all(spread, 'fsdp', split_axis=0, concat_axis=0, tiled=True)  11.7 us
    unnamed x23, local copies, waits for them, and re-layouts  9.77 us
    ppermute x1, waiting for transfers between devices, passed_along(): return lax.ppermute(block, axis, route)  8.69 us
    dot_general x1, matrix products, shards(): jnp.dot(gathered, qkv_full.reshape(model_width, -1), preferred_element_ty...  8.53 us
    dot_general x1, matrix products, shards(): jnp.dot(attention_result, output_weights, preferred_element_type=jnp.floa...  7.16 us
  transfers between devices with their start and end apart: 6, of which 5 were waited for; matrix products, arithmetic and copies ran while one was open for 18% of the time, Pallas kernels for 0%

profile of v7, /device:TPU:2, one launch (start us, length us, event | category | flops | bytes accessed | tf_op | source)
XLA Modules:
  0.0 259.7 jit_solution(12166041470518046386)
XLA Ops:
  6.5 0.0 all-gather.3.cloned.1.call-start
  6.5 1.8 copy.68
  8.3 0.0 all-gather.3.cloned.1.call-update
  8.3 7.6 %copy.69 = bf16[1,16,8,10,2880]{4,1,3,0,2:T(8,128)(2,1)} copy(bf16[1,16,8,10,2880]{4,2,3,1,0:T(8,128)(2,1)} %param.12) | data formatting | bytes 14745600 | tf_op args[0]
  15.9 5.0 %all-to-all-start = ((bf16[1,16,8,10,2880]{4,1,3,0,2:T(8,128)(2,1)}), bf16[1,16,8,10,2880]{4,1,3,0,2:T(8,128)(2,1)}, u32[]{:S(2)}, u32[]{:S(2)}) async-start(bf16[1,16,8,10,2880]{4,1,3,0,2:T(8,128)(2,1)} %copy.69), calls=%async_computation | async-start | bytes 15073280 | tf_op jit(solution)/shard_map/all_to_all | solution.py:82
  21.0 0.0 all-gather.5.cloned.1.call-start
  21.0 0.0 copy-done
  21.0 0.3 copy.67
  21.4 0.0 copy-done.8
  21.4 0.0 copy-done.9
  21.4 0.1 iota_compare_fusion
  21.5 0.0 copy-done.7
  21.5 1.1 select_reduce_fusion
  22.7 0.1 subtract_convert_fusion.1
  22.8 83.6 %all-to-all-done = bf16[1,16,8,10,2880]{4,1,3,0,2:T(8,128)(2,1)} async-done(((bf16[1,16,8,10,2880]{4,1,3,0,2:T(8,128)(2,1)}), bf16[1,16,8,10,2880]{4,1,3,0,2:T(8,128)(2,1)}, u32[]{:S(2)}, u32[]{:S(2)}) %all-to-all-start) | async-done | bytes 7372832 | tf_op jit(solution)/shard_map/all_to_all | solution.py:82
  106.4 6.8 %copy.70 = bf16[1,8,16,1,10,2880]{5,2,1,4,3,0:T(8,128)(2,1)} copy(bf16[1,8,16,1,10,2880]{5,2,4,1,3,0:T(8,128)(2,1)} %bitcast.1) | data formatting | bytes 14745600 | tf_op jit(solution)/shard_map/all_to_all | solution.py:82
  113.3 4.5 %fusion.10 = f32[256,2880]{1,0:T(8,128)S(1)} fusion(bf16[1,128,1,10,2880]{4,1,3,2,0:T(8,128)(2,1)} %bitcast.145, bf16[128,128,10]{1,0,2:T(8,128)(2,1)S(1)} %get-tuple-element.21, bf16[128,128,10]{1,0,2:T(8,128)(2,1)S(1)} %get-tuple-element.22), kind=kOutput, calls=%fused_computation.17 | convolution fusion | flops 1888747520 | bytes 10977280 | tf_op jit(solution)/shard_map/txs,xsm->tm/dot_general | solution.py:94
  117.8 0.0 copy-start.1
  117.8 0.4 fusion.18
  118.2 0.0 copy-done.3
  118.3 1.1 fusion.20
  119.4 0.0 all-gather.5.cloned.1.call-update
  119.4 0.0 copy-start.6
  119.4 0.0 copy-done.1
  119.4 0.0 copy-start.2
  119.4 0.0 slice-start
  119.5 1.8 broadcast_in_dim.45
  121.3 11.7 %all-to-all-start.1 = ((bf16[32,16,2880]{2,1,0:T(8,128)(2,1)}), bf16[32,16,2880]{2,1,0:T(8,128)(2,1)}, u32[]{:S(2)}, u32[]{:S(2)}) async-start(bf16[32,16,2880]{2,1,0:T(8,128)(2,1)} %broadcast_in_dim.45), calls=%async_computation.1 | async-start | bytes 6029312 | tf_op jit(solution)/shard_map/all_to_all | solution.py:63
  132.9 0.2 reduce-scatter.2.cloned.1.call-start
  133.2 0.0 copy-done.6
  133.3 0.0 copy-done.2
  133.3 0.1 fusion.82
  133.4 0.1 fusion.81
  133.4 0.1 compare_and_fusion.2
  133.5 0.5 multiply_cosine_fusion
  134.1 0.8 compare_and_fusion
  134.9 28.0 %all-gather.5.cloned.1.call-done = bf16[1024,2880]{1,0:T(8,128)(2,1)} async-done(((bf16[128,2880]{1,0:T(8,128)(2,1)}), bf16[1024,2880]{1,0:T(8,128)(2,1)}) %all-gather.5.cloned.1.call-update) | async-done | bytes 5898256 | tf_op jit(solution)/shard_map/all_gather | solution.py:105
  162.9 8.5 %fusion.83 = (bf16[1024,1,640]{0,2,1:T(8,128)(2,1)S(1)}, f32[1024,1,640]{0,2,1:T(8,128)S(1)}) fusion(f32[640]{0:T(1024)S(1)} %reduce.6, bf16[1024,2880]{1,0:T(8,128)(2,1)} %all-gather.5.cloned.1.call-done, bf16[2880,1,640]{2,1,0:T(2,128)(2,1)} %all-gather.3.cloned.1.call-done), kind=kOutput, calls=%fused_computation.126 | convolution fusion | flops 3776184320 | bytes 13519360 | tf_op jit(solution)/shard_map/dot_general | solution.py:109
  171.4 0.2 slice.124
  171.7 0.6 fusion.58
  172.2 0.3 add_convert_fusion
  172.6 2.2 fusion.4
  174.8 0.0 copy-start.5
  174.8 2.4 fusion.5
  177.2 3.6 %collective-permute-start = (bf16[128,1,128]{0,2,1:T(8,128)(2,1)S(1)}, bf16[128,1,128]{0,2,1:T(8,128)(2,1)S(1)}, u32[]{:S(2)}, u32[]{:S(2)}) collective-permute-start(bf16[128,1,128]{0,2,1:T(8,128)(2,1)S(1)} %pad_maximum_fusion.5), channel_id=1, source_target_pairs={{0,8},{8,16},{16,24},{24,32},{32,40},{40,48},{48,56},{56,64},{64,7... | collective-permute-start | bytes 98312 | tf_op jit(solution)/shard_map/ppermute | solution.py:20
  180.9 0.1 broadcast_maximum_fusion
  180.9 2.5 fusion
  183.4 2.5 fusion.1
  185.9 0.1 exponential_add_fusion
  186.0 2.7 %fusion.33 = bf16[448,1,8,64]{0,3,2,1:T(8,128)(2,1)S(1)} fusion(f32[8,448]{1,0:T(8,128)S(1)} %get-tuple-element.37, f32[8,448]{1,0:T(8,128)S(1)} %get-tuple-element.39, f32[576,448,8]{0,1,2:T(8,128)S(1)} %get-tuple-element.44, pred[448,576]{1,0:T(8,128)(4,1)S(1)} %get-tuple-element.49, bf16[1024,1,640]{0,2,1:T(8,128)(2,1)S(1)} %get-tuple-element.41), kind=kOutput, calls=%fused_computation.39 | convolution fusion | flops 274792448 | bytes 10035200 | tf_op jit(solution)/shard_map/jgqk,kjd->qjgd/dot_general | solution.py:55
  188.7 2.7 %fusion.36 = bf16[448,1,8,64]{0,3,2,1:T(8,128)(2,1)S(1)} fusion(f32[8,448]{1,0:T(8,128)S(1)} %get-tuple-element.38, f32[8,448]{1,0:T(8,128)S(1)} %get-tuple-element.40, f32[576,448,8]{0,1,2:T(8,128)S(1)} %get-tuple-element.46, pred[448,576]{1,0:T(8,128)(4,1)S(1)} %get-tuple-element.50, bf16[1024,1,640]{0,2,1:T(8,128)(2,1)S(1)} %get-tuple-element.41), kind=kOutput, calls=%fused_computation.40 | convolution fusion | flops 274792448 | bytes 10035200 | tf_op jit(solution)/shard_map/jgqk,kjd->qjgd/dot_general | solution.py:55
  191.4 8.7 %collective-permute-done = bf16[128,1,128]{0,2,1:T(8,128)(2,1)S(1)} collective-permute-done((bf16[128,1,128]{0,2,1:T(8,128)(2,1)S(1)}, bf16[128,1,128]{0,2,1:T(8,128)(2,1)S(1)}, u32[]{:S(2)}, u32[]{:S(2)}) %collective-permute-start) | collective-permute-done | bytes 32800 | tf_op jit(solution)/shard_map/ppermute | solution.py:20
  200.1 0.3 fusion.84
  200.5 0.1 broadcast_maximum_fusion.2
  200.5 0.2 fusion.40
  200.7 0.1 exponential_add_fusion.2
  200.8 0.3 fusion.39
  201.1 0.3 pad_maximum_fusion
  201.4 0.9 all-to-all-done.1
  202.3 7.2 %convolution_convert_fusion = bf16[1024,2880]{1,0:T(8,128)(2,1)} fusion(bf16[1024,512]{0,1:T(8,128)(2,1)S(1)} %bitcast.146, bf16[512,2880]{1,0:T(8,128)(2,1)} %bitcast.42), kind=kOutput, calls=%fused_computation.12 | convolution fusion | flops 3022848000 | bytes 9895936 | tf_op jit(solution)/shard_map/dot_general | solution.py:167
  209.5 0.0 reduce-scatter.2.cloned.1.call-update
  209.5 41.2 %reduce-scatter.2.cloned.1.call-done = bf16[128,2880]{1,0:T(8,128)(2,1)} async-done(((bf16[1024,2880]{1,0:T(8,128)(2,1)}), bf16[128,2880]{1,0:T(8,128)(2,1)}) %reduce-scatter.2.cloned.1.call-update) | async-done | bytes 737296 | tf_op jit(solution)/shard_map/reduce_scatter | solution.py:172
  250.7 1.3 fusion.22
  252.1 1.1 copy.75
  (23 shorter events, 0.1 us)
Async XLA Ops:
  6.5 106.7 %all-gather.3.cloned.1.call-start = ((), (), s32[]{:S(2)}) async-start(), calls=%async_computation.3 | async-start | bytes 7603200 | tf_op jit(solution)/shard_map/all_gather | solution.py:83
  15.9 5.1 %copy-start = (bf16[128,2880]{0,1:T(8,128)(2,1)S(1)}, bf16[128,2880]{0,1:T(8,128)(2,1)}, u32[]{:S(2)}) copy-start(bf16[128,2880]{0,1:T(8,128)(2,1)} %param.13) | copy-start | bytes 2211844
  15.9 5.4 %copy-start.8 = (s32[128,4]{0,1:T(4,128)S(1)}, s32[128,4]{0,1:T(4,128)}, u32[]{:S(2)}) copy-start(s32[128,4]{0,1:T(4,128)} %param.16) | copy-start | bytes 6148
  15.9 5.5 %copy-start.9 = (s32[128,4]{0,1:T(4,128)S(1)}, s32[128,4]{0,1:T(4,128)}, u32[]{:S(2)}) copy-start(s32[128,4]{0,1:T(4,128)} %param.14) | copy-start | bytes 6148
  15.9 5.6 %copy-start.7 = (f32[128,4]{0,1:T(4,128)S(1)}, f32[128,4]{0,1:T(4,128)}, u32[]{:S(2)}) copy-start(f32[128,4]{0,1:T(4,128)} %param.15) | copy-start | bytes 6148
  15.9 90.5 %all-to-all-start = ((bf16[1,16,8,10,2880]{4,1,3,0,2:T(8,128)(2,1)}), bf16[1,16,8,10,2880]{4,1,3,0,2:T(8,128)(2,1)}, u32[]{:S(2)}, u32[]{:S(2)}) async-start(bf16[1,16,8,10,2880]{4,1,3,0,2:T(8,128)(2,1)} %copy.69), calls=%async_computation | async-start | bytes 15073280 | tf_op jit(solution)/shard_map/all_to_all | solution.py:82
  21.0 141.9 %all-gather.5.cloned.1.call-start = ((), (), s32[]{:S(2)}) async-start(), calls=%async_computation.4 | async-start | bytes 6782976 | tf_op jit(solution)/shard_map/all_gather | solution.py:105
  113.3 5.0 %copy-start.3 = (f32[2880]{0:T(1024)S(1)}, f32[2880]{0:T(1024)}, u32[]{:S(2)}) copy-start(f32[2880]{0:T(1024)} %param.18) | copy-start | bytes 34564
  117.8 1.6 copy-start.1
  119.4 13.8 %copy-start.6 = (f32[1,640]{1,0:T(1,128)S(1)}, f32[1,640]{1,0:T(1,128)}, u32[]{:S(2)}) copy-start(f32[1,640]{1,0:T(1,128)} %param.20) | copy-start | bytes 7684
  119.4 13.8 %copy-start.2 = (s32[1024]{0:T(1024)S(1)}, s32[1024]{0:T(1024)}, u32[]{:S(2)}) copy-start(s32[1024]{0:T(1024)} %param.17) | copy-start | bytes 12292
  119.4 14.0 %slice-start = ((s32[1024]{0:T(1024)}), s32[128]{0:T(128)S(1)}, s32[]{:S(2)}) async-start(s32[1024]{0:T(1024)} %param.17), calls=%async_computation.6 | async-start | bytes 1024 | tf_op jit(solution)/shard_map/slice | solution.py:145
  121.3 81.1 %all-to-all-start.1 = ((bf16[32,16,2880]{2,1,0:T(8,128)(2,1)}), bf16[32,16,2880]{2,1,0:T(8,128)(2,1)}, u32[]{:S(2)}, u32[]{:S(2)}) async-start(bf16[32,16,2880]{2,1,0:T(8,128)(2,1)} %broadcast_in_dim.45), calls=%async_computation.1 | async-start | bytes 6029312 | tf_op jit(solution)/shard_map/all_to_all | solution.py:63
  132.9 117.8 %reduce-scatter.2.cloned.1.call-start = ((), (), s32[]{:S(2)}) async-start(), calls=%async_computation.5 | async-start | bytes 6782976 | tf_op jit(solution)/shard_map/reduce_scatter | solution.py:172
  174.8 6.1 %copy-start.5 = (f32[1,8]{1,0:T(1,128)S(1)}, f32[1,8]{1,0:T(1,128)}, u32[]{:S(2)}) copy-start(f32[1,8]{1,0:T(1,128)} %param.21) | copy-start | bytes 100
  177.2 22.9 %collective-permute-start = (bf16[128,1,128]{0,2,1:T(8,128)(2,1)S(1)}, bf16[128,1,128]{0,2,1:T(8,128)(2,1)S(1)}, u32[]{:S(2)}, u32[]{:S(2)}) collective-permute-start(bf16[128,1,128]{0,2,1:T(8,128)(2,1)S(1)} %pad_maximum_fusion.5), channel_id=1, source_target_pairs={{0,8},{8,16},{16,24},{24,32},{32,40},{40,48},{48,56},{56,64},{64,7... | collective-permute-start | bytes 98312 | tf_op jit(solution)/shard_map/ppermute | solution.py:20
  209.5 41.2 %copy-start.4 = (f32[2880]{0:T(1024)S(1)}, f32[2880]{0:T(1024)}, u32[]{:S(2)}) copy-start(f32[2880]{0:T(1024)} %param.23) | copy-start | bytes 34564
Sparse Core Ops, SparseCore 0:
  9.9 95.1 all-gather.2
  119.5 43.3 all-gather.4
  209.6 41.0 reduce-scatter.1

commit v8 on v7

--- a/solution.py
+++ b/solution.py
@@ -163,18 +163,25 @@
     attention_result = jnp.concatenate(outputs_list, axis=0).reshape(block_rows, -1)
     out_full, attention_result = lax.optimization_barrier((out_full, attention_result))
     output_weights = out_full.reshape(-1, model_width)
-    projection_step = with_layout_constraint(
-        jnp.dot(attention_result, output_weights, preferred_element_type=jnp.float32).astype(
-            jnp.bfloat16
-        ),
-        Layout((0, 1)),
-    )
-    projection_step = lax.psum_scatter(
-        projection_step,
-        "expert",
-        scatter_dimension=0,
-        tiled=True,
-    ).astype(jnp.float32)
+    n_exp = lax.axis_size("expert")
+    split_rows = own_rows // 2
+    by_owner = attention_result.reshape(n_exp, own_rows, -1)
+
+    def project(rows):
+        return with_layout_constraint(
+            jnp.dot(
+                rows.reshape(-1, rows.shape[-1]), output_weights, preferred_element_type=jnp.float32
+            ).astype(jnp.bfloat16),
+            Layout((0, 1)),
+        )
+
+    front = lax.psum_scatter(
+        project(by_owner[:, :split_rows]), "expert", scatter_dimension=0, tiled=True
+    )
+    back = project(by_owner[:, split_rows:]).reshape(n_exp, own_rows - split_rows, model_width)
+    back = lax.all_to_all(back, "expert", split_axis=0, concat_axis=0, tiled=True)
+    back = jnp.sum(back.astype(jnp.float32), axis=0)
+    projection_step = jnp.concatenate([front.astype(jnp.float32), back], axis=0)
     return (widened + projection_step + b_out).astype(jnp.bfloat16)
 
 

time: 260 us -> 278 us (1.069)
  blocking collectives: 0 us -> 52.9 us
  waiting for transfers between devices: 162 us -> 124 us
    all_to_all x0 -> x1, blocking collectives: none -> 52.9 us  [shards(): lax.all_to_all(back, 'expert', split_axis=0, concat_axis=0, tiled=True)]
    reduce_scatter x1, waiting for transfers between devices: 41.2 us -> 2.36 us  [shards(): lax.psum_scatter(project(by_owner[:, :split_rows]), 'expert', scatter_dim...]
    dot_general x1 -> x2, matrix products: 7.16 us -> 8.95 us  [project(): jnp.dot(rows.reshape(-1, rows.shape[-1]), output_weights, preferred_eleme...]
where the time goes in v8:
time: 278 us; the launch traced here: 277 us
  waiting for transfers between devices  124 us (45%)
  blocking collectives  52.9 us (19%)
  matrix products  32.6 us (12%)
  starting transfers between devices  20.7 us (7%)
  local copies, waits for them, and re-layouts  20.7 us (7%)
  between operations  13.5 us (5%)
  other arithmetic  12.9 us (5%)
    all_to_all x1, waiting for transfers between devices, shards(): lax.all_to_all(expert_rows, 'expert', split_axis=2, concat_axis=1, tiled=...  83.6 us
    all_to_all x1, blocking collectives, shards(): lax.all_to_all(back, 'expert', split_axis=0, concat_axis=0, tiled=True)  52.9 us
    all_gather x1, waiting for transfers between devices, shards(): gathered = lax.all_gather(normalized_rows, 'expert', axis=0, tiled=True)  27.9 us
    all_to_all x1, starting transfers between devices, gather_fsdp(): lax.all_to_all(spread, 'fsdp', split_axis=0, concat_axis=0, tiled=True)  11.8 us
    unnamed x23, local copies, waits for them, and re-layouts  10 us
    dot_general x2, matrix products, project(): jnp.dot(rows.reshape(-1, rows.shape[-1]), output_weights, preferred_eleme...  8.95 us
    ppermute x1, waiting for transfers between devices, passed_along(): return lax.ppermute(block, axis, route)  8.75 us
    dot_general x1, matrix products, shards(): jnp.dot(gathered, qkv_full.reshape(model_width, -1), preferred_element_ty...  8.53 us
  transfers between devices with their start and end apart: 6, of which 5 were waited for; matrix products, arithmetic and copies ran while one was open for 18% of the time, Pallas kernels for 0%

profile of v8, /device:TPU:2, one launch (start us, length us, event | category | flops | bytes accessed | tf_op | source)
XLA Modules:
  0.0 276.9 jit_solution(1977502048382732544)
XLA Ops:
  6.5 0.0 all-gather.3.cloned.1.call-start
  6.5 1.8 copy.72
  8.3 0.0 all-gather.3.cloned.1.call-update
  8.3 7.6 %copy.73 = bf16[1,16,8,10,2880]{4,1,3,0,2:T(8,128)(2,1)} copy(bf16[1,16,8,10,2880]{4,2,3,1,0:T(8,128)(2,1)} %param.12) | data formatting | bytes 14745600 | tf_op args[0]
  15.9 5.0 %all-to-all-start = ((bf16[1,16,8,10,2880]{4,1,3,0,2:T(8,128)(2,1)}), bf16[1,16,8,10,2880]{4,1,3,0,2:T(8,128)(2,1)}, u32[]{:S(2)}, u32[]{:S(2)}) async-start(bf16[1,16,8,10,2880]{4,1,3,0,2:T(8,128)(2,1)} %copy.73), calls=%async_computation | async-start | bytes 15073280 | tf_op jit(solution)/shard_map/all_to_all | solution.py:82
  20.9 0.0 all-gather.5.cloned.1.call-start
  21.0 0.3 copy.71
  21.4 0.0 copy-done.8
  21.4 0.1 iota_compare_fusion
  21.5 0.0 copy-done.7
  21.5 1.1 select_reduce_fusion
  22.7 0.1 subtract_convert_fusion.1
  22.8 83.6 %all-to-all-done = bf16[1,16,8,10,2880]{4,1,3,0,2:T(8,128)(2,1)} async-done(((bf16[1,16,8,10,2880]{4,1,3,0,2:T(8,128)(2,1)}), bf16[1,16,8,10,2880]{4,1,3,0,2:T(8,128)(2,1)}, u32[]{:S(2)}, u32[]{:S(2)}) %all-to-all-start) | async-done | bytes 7372832 | tf_op jit(solution)/shard_map/all_to_all | solution.py:82
  106.4 6.8 %copy.74 = bf16[1,8,16,1,10,2880]{5,2,1,4,3,0:T(8,128)(2,1)} copy(bf16[1,8,16,1,10,2880]{5,2,4,1,3,0:T(8,128)(2,1)} %bitcast.1) | data formatting | bytes 14745600 | tf_op jit(solution)/shard_map/all_to_all | solution.py:82
  113.3 4.5 %fusion.10 = f32[256,2880]{1,0:T(8,128)S(1)} fusion(bf16[1,128,1,10,2880]{4,1,3,2,0:T(8,128)(2,1)} %bitcast.151, bf16[128,128,10]{1,0,2:T(8,128)(2,1)S(1)} %get-tuple-element.21, bf16[128,128,10]{1,0,2:T(8,128)(2,1)S(1)} %get-tuple-element.22), kind=kOutput, calls=%fused_computation.19 | convolution fusion | flops 1888747520 | bytes 10977280 | tf_op jit(solution)/shard_map/txs,xsm->tm/dot_general | solution.py:94
  117.8 0.0 copy-start.3
  117.8 0.0 copy-start.1
  117.8 0.4 fusion.18
  118.2 0.3 copy-done.3
  118.5 1.1 fusion.20
  119.6 0.0 all-gather.5.cloned.1.call-update
  119.7 0.0 copy-done.1
  119.7 1.8 broadcast_in_dim.45
  121.5 11.8 %all-to-all-start.1 = ((bf16[32,16,2880]{2,1,0:T(8,128)(2,1)}), bf16[32,16,2880]{2,1,0:T(8,128)(2,1)}, u32[]{:S(2)}, u32[]{:S(2)}) async-start(bf16[32,16,2880]{2,1,0:T(8,128)(2,1)} %broadcast_in_dim.45), calls=%async_computation.1 | async-start | bytes 6029312 | tf_op jit(solution)/shard_map/all_to_all | solution.py:63
  133.3 0.2 reduce-scatter.2.cloned.1.call-start
  133.6 0.1 fusion.83
  133.7 0.1 fusion.82
  133.8 0.1 compare_and_fusion.2
  133.9 0.5 multiply_cosine_fusion
  134.4 0.8 compare_and_fusion
  135.3 27.9 %all-gather.5.cloned.1.call-done = bf16[1024,2880]{1,0:T(8,128)(2,1)} async-done(((bf16[128,2880]{1,0:T(8,128)(2,1)}), bf16[1024,2880]{1,0:T(8,128)(2,1)}) %all-gather.5.cloned.1.call-update) | async-done | bytes 5898256 | tf_op jit(solution)/shard_map/all_gather | solution.py:105
  163.2 8.5 %fusion.84 = (bf16[1024,1,640]{0,2,1:T(8,128)(2,1)S(1)}, f32[1024,1,640]{0,2,1:T(8,128)S(1)}) fusion(f32[640]{0:T(1024)S(1)} %reduce.6, bf16[1024,2880]{1,0:T(8,128)(2,1)} %all-gather.5.cloned.1.call-done, bf16[2880,1,640]{2,1,0:T(2,128)(2,1)} %all-gather.3.cloned.1.call-done), kind=kOutput, calls=%fused_computation.129 | convolution fusion | flops 3776184320 | bytes 13519360 | tf_op jit(solution)/shard_map/dot_general | solution.py:109
  171.7 0.2 slice.132
  172.0 0.6 fusion.58
  172.5 0.3 add_convert_fusion
  172.9 2.2 fusion.4
  175.0 0.0 copy-start.5
  175.0 2.4 fusion.5
  177.5 3.7 %collective-permute-start = (bf16[128,1,128]{0,2,1:T(8,128)(2,1)S(1)}, bf16[128,1,128]{0,2,1:T(8,128)(2,1)S(1)}, u32[]{:S(2)}, u32[]{:S(2)}) collective-permute-start(bf16[128,1,128]{0,2,1:T(8,128)(2,1)S(1)} %pad_maximum_fusion.5), channel_id=1, source_target_pairs={{0,8},{8,16},{16,24},{24,32},{32,40},{40,48},{48,56},{56,64},{64,7... | collective-permute-start | bytes 98312 | tf_op jit(solution)/shard_map/ppermute | solution.py:20
  181.2 0.1 broadcast_maximum_fusion
  181.2 2.5 fusion
  183.7 2.5 fusion.1
  186.2 0.1 exponential_add_fusion
  186.3 2.7 fusion.33
  189.0 2.7 fusion.36
  191.7 8.7 %collective-permute-done = bf16[128,1,128]{0,2,1:T(8,128)(2,1)S(1)} collective-permute-done((bf16[128,1,128]{0,2,1:T(8,128)(2,1)S(1)}, bf16[128,1,128]{0,2,1:T(8,128)(2,1)S(1)}, u32[]{:S(2)}, u32[]{:S(2)}) %collective-permute-start) | collective-permute-done | bytes 32800 | tf_op jit(solution)/shard_map/ppermute | solution.py:20
  200.5 0.3 fusion.85
  200.8 0.1 broadcast_maximum_fusion.2
  200.9 0.2 fusion.40
  201.0 0.1 exponential_add_fusion.2
  201.1 0.3 fusion.39
  201.4 0.3 pad_maximum_fusion
  201.8 0.9 all-to-all-done.1
  202.7 0.5 copy.79
  203.2 0.1 fusion.80
  203.3 5.3 %convolution_convert_fusion.1 = bf16[512,2880]{1,0:T(8,128)(2,1)} fusion(bf16[512,512]{1,0:T(8,128)(2,1)S(1)} %bitcast.156, bf16[512,2880]{1,0:T(8,128)(2,1)} %bitcast.44), kind=kOutput, calls=%fused_computation.18 | convolution fusion | flops 1511424000 | bytes 6422528 | tf_op jit(solution)/shard_map/dot_general | solution.py:172
  208.6 0.0 reduce-scatter.2.cloned.1.call-update
  208.6 3.6 %convolution_convert_fusion = bf16[512,2880]{1,0:T(8,128)(2,1)S(1)} fusion(bf16[512,512]{1,0:T(8,128)(2,1)S(1)} %bitcast.155, bf16[512,2880]{1,0:T(8,128)(2,1)} %bitcast.44), kind=kOutput, calls=%fused_computation.17 | convolution fusion | flops 1511424000 | bytes 6422528 | tf_op jit(solution)/shard_map/dot_general | solution.py:172
  212.3 52.9 %all_to_all.28 = bf16[8,64,2880]{2,1,0:T(8,128)(2,1)S(1)} all-to-all(bf16[8,64,2880]{2,1,0:T(8,128)(2,1)S(1)} %bitcast.154), channel_id=1, replica_groups=mesh['fsdp'=32,'expert'=8] {'expert'}, dimensions={0} | all-to-all | bytes 5898240 | tf_op jit(solution)/shard_map/all_to_all | solution.py:182
  265.2 0.4 convert_reduce_fusion
  265.7 2.4 reduce-scatter.2.cloned.1.call-done
  268.0 1.0 convert_element_type.115
  269.1 0.2 fusion.22
  269.3 1.1 copy.80
  (29 shorter events, 0.1 us)
Async XLA Ops:
  6.5 106.7 %all-gather.3.cloned.1.call-start = ((), (), s32[]{:S(2)}) async-start(), calls=%async_computation.4 | async-start | bytes 7603200 | tf_op jit(solution)/shard_map/all_gather | solution.py:83
  15.9 5.1 %copy-start = (bf16[128,2880]{0,1:T(8,128)(2,1)S(1)}, bf16[128,2880]{0,1:T(8,128)(2,1)}, u32[]{:S(2)}) copy-start(bf16[128,2880]{0,1:T(8,128)(2,1)} %param.13) | copy-start | bytes 2211844
  15.9 5.4 %copy-start.8 = (s32[128,4]{0,1:T(4,128)S(1)}, s32[128,4]{0,1:T(4,128)}, u32[]{:S(2)}) copy-start(s32[128,4]{0,1:T(4,128)} %param.16) | copy-start | bytes 6148
  15.9 5.5 %copy-start.9 = (s32[128,4]{0,1:T(4,128)S(1)}, s32[128,4]{0,1:T(4,128)}, u32[]{:S(2)}) copy-start(s32[128,4]{0,1:T(4,128)} %param.14) | copy-start | bytes 6148
  15.9 5.6 %copy-start.7 = (f32[128,4]{0,1:T(4,128)S(1)}, f32[128,4]{0,1:T(4,128)}, u32[]{:S(2)}) copy-start(f32[128,4]{0,1:T(4,128)} %param.15) | copy-start | bytes 6148
  15.9 90.5 %all-to-all-start = ((bf16[1,16,8,10,2880]{4,1,3,0,2:T(8,128)(2,1)}), bf16[1,16,8,10,2880]{4,1,3,0,2:T(8,128)(2,1)}, u32[]{:S(2)}, u32[]{:S(2)}) async-start(bf16[1,16,8,10,2880]{4,1,3,0,2:T(8,128)(2,1)} %copy.73), calls=%async_computation | async-start | bytes 15073280 | tf_op jit(solution)/shard_map/all_to_all | solution.py:82
  20.9 142.2 %all-gather.5.cloned.1.call-start = ((), (), s32[]{:S(2)}) async-start(), calls=%async_computation.5 | async-start | bytes 6782976 | tf_op jit(solution)/shard_map/all_gather | solution.py:105
  117.8 0.7 copy-start.3
  117.8 1.9 copy-start.1
  121.5 12.1 %copy-start.6 = (f32[1,640]{1,0:T(1,128)S(1)}, f32[1,640]{1,0:T(1,128)}, u32[]{:S(2)}) copy-start(f32[1,640]{1,0:T(1,128)} %param.20) | copy-start | bytes 7684
  121.5 12.2 %copy-start.2 = (s32[1024]{0:T(1024)S(1)}, s32[1024]{0:T(1024)}, u32[]{:S(2)}) copy-start(s32[1024]{0:T(1024)} %param.17) | copy-start | bytes 12292
  121.5 12.3 %slice-start = ((s32[1024]{0:T(1024)}), s32[128]{0:T(128)S(1)}, s32[]{:S(2)}) async-start(s32[1024]{0:T(1024)} %param.17), calls=%async_computation.7 | async-start | bytes 1024 | tf_op jit(solution)/shard_map/slice | solution.py:145
  121.5 81.2 %all-to-all-start.1 = ((bf16[32,16,2880]{2,1,0:T(8,128)(2,1)}), bf16[32,16,2880]{2,1,0:T(8,128)(2,1)}, u32[]{:S(2)}, u32[]{:S(2)}) async-start(bf16[32,16,2880]{2,1,0:T(8,128)(2,1)} %broadcast_in_dim.45), calls=%async_computation.1 | async-start | bytes 6029312 | tf_op jit(solution)/shard_map/all_to_all | solution.py:63
  133.3 134.7 %reduce-scatter.2.cloned.1.call-start = ((), (), s32[]{:S(2)}) async-start(), calls=%async_computation.6 | async-start | bytes 3391488 | tf_op jit(solution)/shard_map/reduce_scatter | solution.py:178
  175.0 6.1 %copy-start.5 = (f32[1,8]{1,0:T(1,128)S(1)}, f32[1,8]{1,0:T(1,128)}, u32[]{:S(2)}) copy-start(f32[1,8]{1,0:T(1,128)} %param.21) | copy-start | bytes 100
  177.5 23.0 %collective-permute-start = (bf16[128,1,128]{0,2,1:T(8,128)(2,1)S(1)}, bf16[128,1,128]{0,2,1:T(8,128)(2,1)S(1)}, u32[]{:S(2)}, u32[]{:S(2)}) collective-permute-start(bf16[128,1,128]{0,2,1:T(8,128)(2,1)S(1)} %pad_maximum_fusion.5), channel_id=1, source_target_pairs={{0,8},{8,16},{16,24},{24,32},{32,40},{40,48},{48,56},{56,64},{64,7... | collective-permute-start | bytes 98312 | tf_op jit(solution)/shard_map/ppermute | solution.py:20
  265.2 3.8 %copy-start.4 = (f32[2880]{0:T(1024)S(1)}, f32[2880]{0:T(1024)}, u32[]{:S(2)}) copy-start(f32[2880]{0:T(1024)} %param.23) | copy-start | bytes 34564
Sparse Core Ops, SparseCore 0:
  9.9 95.1 all-gather.2
  119.8 43.3 all-gather.4
  208.8 59.2 reduce-scatter.1

commit v9 on v7

--- a/solution.py
+++ b/solution.py
@@ -2,7 +2,7 @@
 import jax.numpy as jnp
 from jax import lax
 from jax.experimental.layout import Layout, with_layout_constraint
-from jax.sharding import PartitionSpec as P
+from jax.sharding import Mesh, PartitionSpec as P
 
 HEAD_SIZE = 64
 QUERY_PER_KV = 8
@@ -79,7 +79,7 @@
 ):
     own_rows = residual.shape[0]
     model_width = residual.shape[1]
-    returned = lax.all_to_all(expert_rows, "expert", split_axis=2, concat_axis=1, tiled=True)
+    returned = lax.all_to_all(expert_rows, ("ey", "ec"), split_axis=2, concat_axis=1, tiled=True)
     qkv_full = lax.all_gather(projection_weight, "fsdp", axis=0, tiled=True)
     qkv_full, returned = lax.optimization_barrier((qkv_full, returned))
     all_experts = returned.shape[1]
@@ -102,7 +102,16 @@
         * lax.rsqrt(jnp.mean(widened * widened, axis=-1, keepdims=True) + EPSILON)
         * norm_gain
     ).astype(jnp.bfloat16)
-    gathered = lax.all_gather(normalized_rows, "expert", axis=0, tiled=True)
+    own_parity = lax.all_gather(normalized_rows[None], "ey", axis=0, tiled=True)
+    other_parity = lax.ppermute(own_parity, "ec", [(0, 1), (1, 0)])
+    first_core = lax.axis_index("ec") == 0
+    gathered = jnp.stack(
+        [
+            jnp.where(first_core, own_parity, other_parity),
+            jnp.where(first_core, other_parity, own_parity),
+        ],
+        axis=1,
+    ).reshape(-1, model_width)
     out_full = gather_fsdp(output_weight[0])
     block_rows = gathered.shape[0]
     local_heads = projection_weight.shape[1]
@@ -171,7 +180,7 @@
     )
     projection_step = lax.psum_scatter(
         projection_step,
-        "expert",
+        ("ey", "ec"),
         scatter_dimension=0,
         tiled=True,
     ).astype(jnp.float32)
@@ -179,19 +188,22 @@
 
 
 def solution(mesh):
+    n_fsdp, n_expert = mesh.devices.shape
+    split_mesh = Mesh(mesh.devices.reshape(n_fsdp, n_expert // 2, 2), ("fsdp", "ey", "ec"))
+    expert = ("ey", "ec")
     in_specs = (
-        P("fsdp", "expert", None, None, None),
-        P(("fsdp", "expert"), None),
-        P(("fsdp", "expert"), None),
-        P(("fsdp", "expert"), None),
-        P(("fsdp", "expert"), None),
+        P("fsdp", expert, None, None, None),
+        P(("fsdp",) + expert, None),
+        P(("fsdp",) + expert, None),
+        P(("fsdp",) + expert, None),
+        P(("fsdp",) + expert, None),
         P("fsdp"),
         P(),
-        P("fsdp", "expert", None),
-        P("expert", None),
-        P("expert", None),
-        P("expert", "fsdp", None),
+        P("fsdp", expert, None),
+        P(expert, None),
+        P(expert, None),
+        P(expert, "fsdp", None),
         P(),
     )
-    out_specs = P(("fsdp", "expert"), None)
-    return jax.shard_map(shards, mesh=mesh, in_specs=in_specs, out_specs=out_specs, check_vma=False)
+    out_specs = P(("fsdp",) + expert, None)
+    return jax.shard_map(shards, mesh=split_mesh, in_specs=in_specs, out_specs=out_specs, check_vma=False)

time: 260 us -> 308 us (1.18)
  waiting for transfers between devices: 162 us -> 191 us
  local copies, waits for them, and re-layouts: 19.9 us -> 33.2 us
  other arithmetic: 12.6 us -> 19 us
    ppermute x1, waiting for transfers between devices: 8.69 us -> 22.9 us  [passed_along(): return lax.ppermute(block, axis, route)]
    all_gather x1, waiting for transfers between devices: 28 us -> 42.1 us  [shards(): own_parity = lax.all_gather(normalized_rows[None], 'ey', axis=0, tiled=True)]
    another operation x0 -> x1, local copies, waits for them, and re-layouts: none -> 8.43 us  [shards(): jnp.stack([jnp.where(first_core, own_parity, other_parity), jnp.where(fir...]
    another operation x2 -> x4, other arithmetic: 0.89 us -> 6.13 us  [the longest x2 5.24 us: shards(): jnp.stack([jnp.where(first_core, own_parity, other_parity), jnp.where(fir...]
    all_gather x0 -> x1, local copies, waits for them, and re-layouts: none -> 3.43 us  [shards(): own_parity = lax.all_gather(normalized_rows[None], 'ey', axis=0, tiled=True)]
    unnamed x23 -> x41, local copies, waits for them, and re-layouts: 9.77 us -> 11.1 us
  transfers between devices with their start and end apart: 6 -> 7, of which waited for: 5 -> 4; matrix products, arithmetic and copies ran while one was open for 18% -> 20% of each run, Pallas kernels for 0% -> 0%
where the time goes in v9:
time: 308 us; the launch traced here: 307 us
  waiting for transfers between devices  191 us (62%)
  local copies, waits for them, and re-layouts  33.2 us (11%)
  matrix products  30.9 us (10%)
  starting transfers between devices  19.3 us (6%)
  other arithmetic  19 us (6%)
  between operations  13.6 us (4%)
    all_to_all x1, waiting for transfers between devices, shards(): lax.all_to_all(expert_rows, ('ey', 'ec'), split_axis=2, concat_axis=1, ti...  83.6 us
    reduce_scatter x1, waiting for transfers between devices, shards(): lax.psum_scatter(projection_step, ('ey', 'ec'), scatter_dimension=0, tile...  42.5 us
    all_gather x1, waiting for transfers between devices, shards(): own_parity = lax.all_gather(normalized_rows[None], 'ey', axis=0, tiled=True)  42.1 us
    ppermute x1, waiting for transfers between devices, passed_along(): return lax.ppermute(block, axis, route)  22.9 us
    unnamed x41, local copies, waits for them, and re-layouts  11.1 us
    all_to_all x1, starting transfers between devices, gather_fsdp(): lax.all_to_all(spread, 'fsdp', split_axis=0, concat_axis=0, tiled=True)  10.3 us
    dot_general x1, matrix products, shards(): jnp.dot(gathered, qkv_full.reshape(model_width, -1), preferred_element_ty...  8.53 us
    another operation x1, local copies, waits for them, and re-layouts, shards(): jnp.stack([jnp.where(first_core, own_parity, other_parity), jnp.where(fir...  8.43 us
  transfers between devices with their start and end apart: 7, of which 4 were waited for; matrix products, arithmetic and copies ran while one was open for 20% of the time, Pallas kernels for 0%

profile of v9, /device:TPU:2, one launch (start us, length us, event | category | flops | bytes accessed | tf_op | source)
XLA Modules:
  0.0 307.0 jit_solution(5626157274746386398)
XLA Ops:
  6.5 0.0 all-gather.4.cloned.1.call-start
  6.5 1.8 copy.81
  8.3 0.0 all-gather.4.cloned.1.call-update
  8.3 7.6 %copy.82 = bf16[1,16,8,10,2880]{4,1,3,0,2:T(8,128)(2,1)} copy(bf16[1,16,8,10,2880]{4,2,3,1,0:T(8,128)(2,1)} %param.12) | data formatting | bytes 14745600 | tf_op args[0]
  15.9 5.0 %all-to-all-start = ((bf16[1,16,8,10,2880]{4,1,3,0,2:T(8,128)(2,1)}), bf16[1,16,8,10,2880]{4,1,3,0,2:T(8,128)(2,1)}, u32[]{:S(2)}, u32[]{:S(2)}) async-start(bf16[1,16,8,10,2880]{4,1,3,0,2:T(8,128)(2,1)} %copy.82), calls=%async_computation | async-start | bytes 15073280 | tf_op jit(solution)/shard_map/all_to_all | solution.py:82
  21.0 0.0 all-gather.6.cloned.1.call-start
  21.0 0.3 copy.80
  21.4 0.1 iota_compare_fusion
  21.6 1.1 select_reduce_fusion
  22.7 0.1 subtract_convert_fusion.1
  22.8 83.6 %all-to-all-done = bf16[1,16,8,10,2880]{4,1,3,0,2:T(8,128)(2,1)} async-done(((bf16[1,16,8,10,2880]{4,1,3,0,2:T(8,128)(2,1)}), bf16[1,16,8,10,2880]{4,1,3,0,2:T(8,128)(2,1)}, u32[]{:S(2)}, u32[]{:S(2)}) %all-to-all-start) | async-done | bytes 7372832 | tf_op jit(solution)/shard_map/all_to_all | solution.py:82
  106.5 6.8 %copy.83 = bf16[1,8,16,1,10,2880]{5,2,1,4,3,0:T(8,128)(2,1)} copy(bf16[1,8,16,1,10,2880]{5,2,4,1,3,0:T(8,128)(2,1)} %bitcast.1) | data formatting | bytes 14745600 | tf_op jit(solution)/shard_map/all_to_all | solution.py:82
  113.3 4.5 %fusion.10 = f32[256,2880]{1,0:T(8,128)S(1)} fusion(bf16[1,128,1,10,2880]{4,1,3,2,0:T(8,128)(2,1)} %bitcast.151, bf16[128,128,10]{1,0,2:T(8,128)(2,1)S(1)} %get-tuple-element.21, bf16[128,128,10]{1,0,2:T(8,128)(2,1)S(1)} %get-tuple-element.22), kind=kOutput, calls=%fused_computation.18 | convolution fusion | flops 1888747520 | bytes 10977280 | tf_op jit(solution)/shard_map/txs,xsm->tm/dot_general | solution.py:94
  117.8 0.0 copy-start.9
  117.8 0.4 fusion.18
  118.3 0.9 copy-done
  119.2 1.1 fusion.20
  120.3 0.0 all-gather.6.cloned.1.call-update
  120.3 42.1 %all-gather.6.cloned.1.call-done = bf16[512,2880]{1,0:T(8,128)(2,1)} async-done(((bf16[128,2880]{1,0:T(8,128)(2,1)}), bf16[512,2880]{1,0:T(8,128)(2,1)}) %all-gather.6.cloned.1.call-update) | async-done | bytes 2949136 | tf_op jit(solution)/shard_map/all_gather | solution.py:105
  162.4 3.4 %copy.88 = bf16[4,128,2880]{1,2,0:T(8,128)(2,1)S(1)} copy(bf16[4,128,2880]{2,1,0:T(8,128)(2,1)} %bitcast.153) | data formatting | bytes 5898240 | tf_op jit(solution)/shard_map/all_gather | solution.py:105
  165.9 0.1 collective-permute-start
  166.0 1.9 broadcast_in_dim.47
  167.9 10.3 %all-to-all-start.1 = ((bf16[32,16,2880]{2,1,0:T(8,128)(2,1)}), bf16[32,16,2880]{2,1,0:T(8,128)(2,1)}, u32[]{:S(2)}, u32[]{:S(2)}) async-start(bf16[32,16,2880]{2,1,0:T(8,128)(2,1)} %broadcast_in_dim.47), calls=%async_computation.1 | async-start | bytes 6029312 | tf_op jit(solution)/shard_map/all_to_all | solution.py:63
  178.2 0.2 reduce-scatter.2.cloned.1.call-start
  178.5 0.6 reduce.6
  179.1 0.1 fusion.82
  179.2 0.1 fusion.81
  179.3 0.1 compare_and_fusion.2
  179.4 1.2 multiply_cosine_fusion
  180.6 0.4 compare_and_fusion.1
  181.0 0.4 compare_and_fusion
  181.4 0.0 collective-permute-done
  181.4 2.2 select_bitcast_fusion.1
  183.6 3.0 pad_maximum_fusion
  186.7 8.4 %copy.90 = bf16[4,2,128,2880]{3,2,1,0:T(8,128)(2,1)} copy(bf16[4,2,128,2880]{2,3,0,1:T(8,128)(2,1)} %pad_maximum_fusion) | data formatting | bytes 11796480 | tf_op jit(solution)/shard_map/stack | solution.py:108
  195.1 8.5 %fusion.83 = (bf16[1024,1,640]{0,2,1:T(8,128)(2,1)S(1)}, f32[1024,1,640]{0,2,1:T(8,128)S(1)}) fusion(f32[640]{0:T(1024)S(1)} %copy-done.12, bf16[1024,2880]{1,0:T(8,128)(2,1)} %bitcast.152, bf16[2880,1,640]{2,1,0:T(2,128)(2,1)} %all-gather.4.cloned.1.call-done), kind=kOutput, calls=%fused_computation.129 | convolution fusion | flops 3776184320 | bytes 13519360 | tf_op jit(solution)/shard_map/dot_general | solution.py:118
  203.7 0.0 copy-start.3
  203.7 0.2 slice.124
  203.9 0.4 copy-done.7
  204.3 0.6 fusion.58
  204.9 0.3 add_convert_fusion
  205.3 2.2 fusion.4
  207.4 0.0 copy-start.11
  207.4 2.4 fusion.5
  209.9 3.6 %collective-permute-start.1 = (bf16[128,1,128]{0,2,1:T(8,128)(2,1)S(1)}, bf16[128,1,128]{0,2,1:T(8,128)(2,1)S(1)}, u32[]{:S(2)}, u32[]{:S(2)}) collective-permute-start(bf16[128,1,128]{0,2,1:T(8,128)(2,1)S(1)} %pad_maximum_fusion.6), channel_id=1, source_target_pairs={{0,8},{8,16},{16,24},{24,32},{32,40},{40,48},{48,56},{56,64},{64,7... | collective-permute-start | bytes 98312 | tf_op jit(solution)/shard_map/ppermute | solution.py:20
  213.5 0.1 broadcast_maximum_fusion
  213.5 2.5 fusion
  216.0 2.5 fusion.1
  218.5 0.1 exponential_add_fusion
  218.6 2.7 fusion.33
  221.4 2.7 fusion.36
  224.0 22.9 %collective-permute-done.1 = bf16[128,1,128]{0,2,1:T(8,128)(2,1)S(1)} collective-permute-done((bf16[128,1,128]{0,2,1:T(8,128)(2,1)S(1)}, bf16[128,1,128]{0,2,1:T(8,128)(2,1)S(1)}, u32[]{:S(2)}, u32[]{:S(2)}) %collective-permute-start.1) | collective-permute-done | bytes 32800 | tf_op jit(solution)/shard_map/ppermute | solution.py:20
  246.9 0.3 fusion.84
  247.3 0.1 broadcast_maximum_fusion.2
  247.3 0.2 fusion.40
  247.5 0.1 exponential_add_fusion.2
  247.6 0.3 fusion.39
  247.9 0.3 pad_maximum_fusion.1
  248.2 0.0 all-to-all-done.1
  248.2 7.2 %convolution_convert_fusion = bf16[1024,2880]{1,0:T(8,128)(2,1)} fusion(bf16[1024,512]{0,1:T(8,128)(2,1)S(1)} %bitcast.154, bf16[512,2880]{1,0:T(8,128)(2,1)} %bitcast.46), kind=kOutput, calls=%fused_computation.13 | convolution fusion | flops 3022848000 | bytes 9895936 | tf_op jit(solution)/shard_map/dot_general | solution.py:176
  255.4 0.0 reduce-scatter.2.cloned.1.call-update
  255.5 42.5 %reduce-scatter.2.cloned.1.call-done = bf16[128,2880]{1,0:T(8,128)(2,1)} async-done(((bf16[1024,2880]{1,0:T(8,128)(2,1)}), bf16[128,2880]{1,0:T(8,128)(2,1)}) %reduce-scatter.2.cloned.1.call-update) | async-done | bytes 737296 | tf_op jit(solution)/shard_map/reduce_scatter | solution.py:181
  298.0 1.3 fusion.22
  299.3 1.1 copy.92
  (47 shorter events, 0.2 us)
Async XLA Ops:
  6.5 106.8 %all-gather.4.cloned.1.call-start = ((), (), s32[]{:S(2)}) async-start(), calls=%async_computation.3 | async-start | bytes 7603200 | tf_op jit(solution)/shard_map/all_gather | solution.py:83
  15.9 5.1 %copy-start.2 = (bf16[128,2880]{0,1:T(8,128)(2,1)S(1)}, bf16[128,2880]{0,1:T(8,128)(2,1)}, u32[]{:S(2)}) copy-start(bf16[128,2880]{0,1:T(8,128)(2,1)} %param.13) | copy-start | bytes 2211844
  15.9 5.4 %copy-start.17 = (s32[128,4]{0,1:T(4,128)S(1)}, s32[128,4]{0,1:T(4,128)}, u32[]{:S(2)}) copy-start(s32[128,4]{0,1:T(4,128)} %param.16) | copy-start | bytes 6148
  15.9 5.5 %copy-start.18 = (s32[128,4]{0,1:T(4,128)S(1)}, s32[128,4]{0,1:T(4,128)}, u32[]{:S(2)}) copy-start(s32[128,4]{0,1:T(4,128)} %param.14) | copy-start | bytes 6148
  15.9 5.6 %copy-start.14 = (f32[128,4]{0,1:T(4,128)S(1)}, f32[128,4]{0,1:T(4,128)}, u32[]{:S(2)}) copy-start(f32[128,4]{0,1:T(4,128)} %param.15) | copy-start | bytes 6148
  15.9 90.5 %all-to-all-start = ((bf16[1,16,8,10,2880]{4,1,3,0,2:T(8,128)(2,1)}), bf16[1,16,8,10,2880]{4,1,3,0,2:T(8,128)(2,1)}, u32[]{:S(2)}, u32[]{:S(2)}) async-start(bf16[1,16,8,10,2880]{4,1,3,0,2:T(8,128)(2,1)} %copy.82), calls=%async_computation | async-start | bytes 15073280 | tf_op jit(solution)/shard_map/all_to_all | solution.py:82
  21.0 141.5 %all-gather.6.cloned.1.call-start = ((), (), s32[]{:S(2)}) async-start(), calls=%async_computation.5 | async-start | bytes 3768320 | tf_op jit(solution)/shard_map/all_gather | solution.py:105
  117.8 1.3 copy-start.9
  118.2 0.9 copy-start
  120.3 45.7 %copy-start.5 = (bf16[1,16,2880]{2,1,0:T(8,128)(2,1)S(1)}, bf16[1,16,2880]{2,1,0:T(8,128)(2,1)}, u32[]{:S(2)}) copy-start(bf16[1,16,2880]{2,1,0:T(8,128)(2,1)} %param.22) | copy-start | bytes 276484
  165.9 15.5 %collective-permute-start = (bf16[4,128,2880]{1,2,0:T(8,128)(2,1)S(1)}, bf16[4,128,2880]{1,2,0:T(8,128)(2,1)}, u32[]{:S(2)}, u32[]{:S(2)}) collective-permute-start(bf16[4,128,2880]{1,2,0:T(8,128)(2,1)S(1)} %copy.88), channel_id=1, source_target_pairs={{0,1},{1,0},{2,3},{3,2},{4,5},{5,4},{6,7},{7,6},{8,9},{9,8},{10,11... | collective-permute-start | bytes 8847368 | tf_op jit(solution)/shard_map/ppermute | solution.py:106
  167.9 10.6 %copy-start.13 = (f32[1,640]{1,0:T(1,128)S(1)}, f32[1,640]{1,0:T(1,128)}, u32[]{:S(2)}) copy-start(f32[1,640]{1,0:T(1,128)} %param.20) | copy-start | bytes 7684
  167.9 11.2 %copy-start.8 = (s32[1024]{0:T(1024)S(1)}, s32[1024]{0:T(1024)}, u32[]{:S(2)}) copy-start(s32[1024]{0:T(1024)} %param.17) | copy-start | bytes 12292
  167.9 11.4 %slice-start = ((s32[1024]{0:T(1024)}), s32[128]{0:T(128)S(1)}, s32[]{:S(2)}) async-start(s32[1024]{0:T(1024)} %param.17), calls=%async_computation.6 | async-start | bytes 1024 | tf_op jit(solution)/shard_map/slice | solution.py:154
  167.9 80.3 %all-to-all-start.1 = ((bf16[32,16,2880]{2,1,0:T(8,128)(2,1)}), bf16[32,16,2880]{2,1,0:T(8,128)(2,1)}, u32[]{:S(2)}, u32[]{:S(2)}) async-start(bf16[32,16,2880]{2,1,0:T(8,128)(2,1)} %broadcast_in_dim.47), calls=%async_computation.1 | async-start | bytes 6029312 | tf_op jit(solution)/shard_map/all_to_all | solution.py:63
  178.2 119.7 %reduce-scatter.2.cloned.1.call-start = ((), (), s32[]{:S(2)}) async-start(), calls=%async_computation.4 | async-start | bytes 6782976 | tf_op jit(solution)/shard_map/reduce_scatter | solution.py:181
  179.1 2.0 copy-start.15
  179.1 1.9 copy-start.6
  186.7 8.4 %copy-start.12 = (f32[640]{0:T(1024)S(1)}, f32[640]{0:T(1024)}, u32[]{:S(2)}) copy-start(f32[640]{0:T(1024)} %reduce.6) | copy-start | bytes 7684
  203.6 0.7 copy-start.7
  203.7 0.7 copy-start.16
  203.7 1.2 copy-start.3
  203.7 1.2 copy-start.4
  207.4 6.0 %copy-start.11 = (f32[1,8]{1,0:T(1,128)S(1)}, f32[1,8]{1,0:T(1,128)}, u32[]{:S(2)}) copy-start(f32[1,8]{1,0:T(1,128)} %param.21) | copy-start | bytes 100
  209.9 37.0 %collective-permute-start.1 = (bf16[128,1,128]{0,2,1:T(8,128)(2,1)S(1)}, bf16[128,1,128]{0,2,1:T(8,128)(2,1)S(1)}, u32[]{:S(2)}, u32[]{:S(2)}) collective-permute-start(bf16[128,1,128]{0,2,1:T(8,128)(2,1)S(1)} %pad_maximum_fusion.6), channel_id=1, source_target_pairs={{0,8},{8,16},{16,24},{24,32},{32,40},{40,48},{48,56},{56,64},{64,7... | collective-permute-start | bytes 98312 | tf_op jit(solution)/shard_map/ppermute | solution.py:20
  255.4 42.5 %copy-start.1 = (bf16[128,2880]{1,0:T(8,128)(2,1)S(1)}, bf16[128,2880]{1,0:T(8,128)(2,1)}, u32[]{:S(2)}) copy-start(bf16[128,2880]{1,0:T(8,128)(2,1)} %copy-done) | copy-start | bytes 2211844
  255.4 42.5 %copy-start.10 = (f32[2880]{0:T(1024)S(1)}, f32[2880]{0:T(1024)}, u32[]{:S(2)}) copy-start(f32[2880]{0:T(1024)} %param.23) | copy-start | bytes 34564
Sparse Core Ops, SparseCore 0:
  9.9 95.1 all-gather.3
  120.5 41.9 all-gather.5
  255.6 42.3 reduce-scatter.1

commit v10 on v7

--- a/solution.py
+++ b/solution.py
@@ -88,13 +88,12 @@
     hit_slot = route_slots[..., None] == jnp.arange(capacity, dtype=jnp.int32)
     hits = hit_expert[..., :, None] & hit_slot[..., None, :]
     select = jnp.sum(jnp.where(hits, route_weights[..., None, None], 0.0), axis=1)
-    high = select.astype(jnp.bfloat16)
-    low = (select - high.astype(jnp.float32)).astype(jnp.bfloat16)
-    both = jnp.concatenate([high, low], axis=0)
-    picked = jnp.einsum(
-        "txs,xsm->tm", both, returned[0, :, 0], preferred_element_type=jnp.float32
+    combined = jnp.einsum(
+        "txs,xsm->tm",
+        select.astype(jnp.bfloat16),
+        returned[0, :, 0],
+        preferred_element_type=jnp.float32,
     )
-    combined = picked[:own_rows] + picked[own_rows:]
     hidden = (residual.astype(jnp.float32) + combined).astype(jnp.bfloat16)
     widened = hidden.astype(jnp.float32)
     normalized_rows = (

time: 260 us -> 260 us (level)
    unnamed x23 -> x22, local copies, waits for them, and re-layouts: 9.77 us -> 9.42 us
where the time goes in v10:
time: 260 us; the launch traced here: 259 us
  waiting for transfers between devices  163 us (63%)
  matrix products  30.8 us (12%)
  starting transfers between devices  20.6 us (8%)
  local copies, waits for them, and re-layouts  19.8 us (8%)
  between operations  13.5 us (5%)
  other arithmetic  12 us (5%)
    all_to_all x1, waiting for transfers between devices, shards(): lax.all_to_all(expert_rows, 'expert', split_axis=2, concat_axis=1, tiled=...  83.8 us
    reduce_scatter x1, waiting for transfers between devices, shards(): lax.psum_scatter(projection_step, 'expert', scatter_dimension=0, tiled=True)  41.2 us
    all_gather x1, waiting for transfers between devices, shards(): gathered = lax.all_gather(normalized_rows, 'expert', axis=0, tiled=True)  28 us
    all_to_all x1, starting transfers between devices, gather_fsdp(): lax.all_to_all(spread, 'fsdp', split_axis=0, concat_axis=0, tiled=True)  11.7 us
    unnamed x22, local copies, waits for them, and re-layouts  9.42 us
    ppermute x1, waiting for transfers between devices, passed_along(): return lax.ppermute(block, axis, route)  8.64 us
    dot_general x1, matrix products, shards(): jnp.dot(gathered, qkv_full.reshape(model_width, -1), preferred_element_ty...  8.53 us
    dot_general x1, matrix products, shards(): jnp.dot(attention_result, output_weights, preferred_element_type=jnp.floa...  7.18 us
  transfers between devices with their start and end apart: 6, of which 5 were waited for; matrix products, arithmetic and copies ran while one was open for 18% of the time, Pallas kernels for 0%

profile of v10, /device:TPU:2, one launch (start us, length us, event | category | flops | bytes accessed | tf_op | source)
XLA Modules:
  0.0 259.2 jit_solution(2399133368508011631)
XLA Ops:
  6.5 0.0 all-gather.3.cloned.1.call-start
  6.5 1.8 copy.70
  8.3 0.0 all-gather.3.cloned.1.call-update
  8.3 7.6 %copy.71 = bf16[1,16,8,10,2880]{4,1,3,0,2:T(8,128)(2,1)} copy(bf16[1,16,8,10,2880]{4,2,3,1,0:T(8,128)(2,1)} %param.12) | data formatting | bytes 14745600 | tf_op args[0]
  15.9 5.0 %all-to-all-start = ((bf16[1,16,8,10,2880]{4,1,3,0,2:T(8,128)(2,1)}), bf16[1,16,8,10,2880]{4,1,3,0,2:T(8,128)(2,1)}, u32[]{:S(2)}, u32[]{:S(2)}) async-start(bf16[1,16,8,10,2880]{4,1,3,0,2:T(8,128)(2,1)} %copy.71), calls=%async_computation | async-start | bytes 15073280 | tf_op jit(solution)/shard_map/all_to_all | solution.py:82
  21.0 0.0 all-gather.5.cloned.1.call-start
  21.0 0.0 copy-done
  21.0 0.3 copy.74
  21.3 0.0 copy-done.8
  21.3 0.0 copy-done.9
  21.3 0.1 iota_compare_fusion
  21.5 0.0 copy-done.7
  21.5 1.1 select_reduce_fusion
  22.6 83.8 %all-to-all-done = bf16[1,16,8,10,2880]{4,1,3,0,2:T(8,128)(2,1)} async-done(((bf16[1,16,8,10,2880]{4,1,3,0,2:T(8,128)(2,1)}), bf16[1,16,8,10,2880]{4,1,3,0,2:T(8,128)(2,1)}, u32[]{:S(2)}, u32[]{:S(2)}) %all-to-all-start) | async-done | bytes 7372832 | tf_op jit(solution)/shard_map/all_to_all | solution.py:82
  106.4 6.9 %copy.72 = bf16[1,8,16,1,10,2880]{5,2,1,4,3,0:T(8,128)(2,1)} copy(bf16[1,8,16,1,10,2880]{5,2,4,1,3,0:T(8,128)(2,1)} %bitcast.1) | data formatting | bytes 14745600 | tf_op jit(solution)/shard_map/all_to_all | solution.py:82
  113.3 4.5 %multiply_reduce_fusion = (f32[128]{0:T(128)S(1)}, f32[128,2880]{1,0:T(8,128)S(1)}) fusion(f32[128,2880]{1,0:T(8,128)S(1)} %copy.74, bf16[128,128,10]{1,0,2:T(8,128)(2,1)S(1)} %select_reduce_fusion, bf16[1,128,1,10,2880]{4,1,3,2,0:T(8,128)(2,1)} %bitcast.157), kind=kOutput, calls=%fused_computation.28 | convolution fusion | flops 945561472 | bytes 10650112 | tf_op jit(solution)/shard_map/txs,xsm->tm/dot_general | solution.py:91
  117.8 0.0 copy-done.3
  117.8 0.0 copy-start.6
  117.8 0.0 copy-start.2
  117.8 0.0 slice-start
  117.8 1.1 multiply_convert_fusion
  118.9 0.0 all-gather.5.cloned.1.call-update
  118.9 0.0 copy-done.1
  118.9 1.8 broadcast_in_dim.45
  120.7 11.7 %all-to-all-start.1 = ((bf16[32,16,2880]{2,1,0:T(8,128)(2,1)}), bf16[32,16,2880]{2,1,0:T(8,128)(2,1)}, u32[]{:S(2)}, u32[]{:S(2)}) async-start(bf16[32,16,2880]{2,1,0:T(8,128)(2,1)} %broadcast_in_dim.45), calls=%async_computation.1 | async-start | bytes 6029312 | tf_op jit(solution)/shard_map/all_to_all | solution.py:63
  132.4 0.2 reduce-scatter.2.cloned.1.call-start
  132.6 0.0 copy-done.6
  132.7 0.0 copy-done.2
  132.8 0.1 fusion.80
  132.8 0.1 fusion.79
  132.9 0.0 slice-done
  132.9 0.1 compare_and_fusion.2
  133.0 0.5 multiply_cosine_fusion
  133.6 0.8 compare_and_fusion
  134.4 28.0 %all-gather.5.cloned.1.call-done = bf16[1024,2880]{1,0:T(8,128)(2,1)} async-done(((bf16[128,2880]{1,0:T(8,128)(2,1)}), bf16[1024,2880]{1,0:T(8,128)(2,1)}) %all-gather.5.cloned.1.call-update) | async-done | bytes 5898256 | tf_op jit(solution)/shard_map/all_gather | solution.py:104
  162.4 8.5 %fusion.81 = (bf16[1024,1,640]{0,2,1:T(8,128)(2,1)S(1)}, f32[1024,1,640]{0,2,1:T(8,128)S(1)}) fusion(f32[640]{0:T(1024)S(1)} %reduce.6, bf16[1024,2880]{1,0:T(8,128)(2,1)} %all-gather.5.cloned.1.call-done, bf16[2880,1,640]{2,1,0:T(2,128)(2,1)} %all-gather.3.cloned.1.call-done), kind=kOutput, calls=%fused_computation.117 | convolution fusion | flops 3776184320 | bytes 13519360 | tf_op jit(solution)/shard_map/dot_general | solution.py:108
  170.9 0.2 slice.114
  171.2 0.6 fusion.58
  171.7 0.3 add_convert_fusion.1
  172.1 2.2 fusion.4
  174.2 0.0 copy-start.5
  174.3 2.4 fusion.5
  176.7 3.7 %collective-permute-start = (bf16[128,1,128]{0,2,1:T(8,128)(2,1)S(1)}, bf16[128,1,128]{0,2,1:T(8,128)(2,1)S(1)}, u32[]{:S(2)}, u32[]{:S(2)}) collective-permute-start(bf16[128,1,128]{0,2,1:T(8,128)(2,1)S(1)} %pad_maximum_fusion.5), channel_id=1, source_target_pairs={{0,8},{8,16},{16,24},{24,32},{32,40},{40,48},{48,56},{56,64},{64,7... | collective-permute-start | bytes 98312 | tf_op jit(solution)/shard_map/ppermute | solution.py:20
  180.4 0.0 copy-done.5
  180.4 0.1 broadcast_maximum_fusion
  180.5 2.5 fusion
  182.9 2.5 fusion.1
  185.4 0.1 exponential_add_fusion
  185.5 2.7 %fusion.35 = bf16[448,1,8,64]{0,3,2,1:T(8,128)(2,1)S(1)} fusion(f32[8,448]{1,0:T(8,128)S(1)} %get-tuple-element.33, f32[8,448]{1,0:T(8,128)S(1)} %get-tuple-element.35, f32[576,448,8]{0,1,2:T(8,128)S(1)} %get-tuple-element.42, pred[448,576]{1,0:T(8,128)(4,1)S(1)} %get-tuple-element.47, bf16[1024,1,640]{0,2,1:T(8,128)(2,1)S(1)} %get-tuple-element.39), kind=kOutput, calls=%fused_computation.34 | convolution fusion | flops 274792448 | bytes 10035200 | tf_op jit(solution)/shard_map/jgqk,kjd->qjgd/dot_general | solution.py:55
  188.2 2.7 %fusion.38 = bf16[448,1,8,64]{0,3,2,1:T(8,128)(2,1)S(1)} fusion(f32[8,448]{1,0:T(8,128)S(1)} %get-tuple-element.34, f32[8,448]{1,0:T(8,128)S(1)} %get-tuple-element.36, f32[576,448,8]{0,1,2:T(8,128)S(1)} %get-tuple-element.44, pred[448,576]{1,0:T(8,128)(4,1)S(1)} %get-tuple-element.48, bf16[1024,1,640]{0,2,1:T(8,128)(2,1)S(1)} %get-tuple-element.39), kind=kOutput, calls=%fused_computation.35 | convolution fusion | flops 274792448 | bytes 10035200 | tf_op jit(solution)/shard_map/jgqk,kjd->qjgd/dot_general | solution.py:55
  190.9 8.6 %collective-permute-done = bf16[128,1,128]{0,2,1:T(8,128)(2,1)S(1)} collective-permute-done((bf16[128,1,128]{0,2,1:T(8,128)(2,1)S(1)}, bf16[128,1,128]{0,2,1:T(8,128)(2,1)S(1)}, u32[]{:S(2)}, u32[]{:S(2)}) %collective-permute-start) | collective-permute-done | bytes 32800 | tf_op jit(solution)/shard_map/ppermute | solution.py:20
  199.6 0.3 fusion.82
  199.9 0.1 broadcast_maximum_fusion.2
  200.0 0.2 fusion.42
  200.2 0.1 exponential_add_fusion.2
  200.2 0.3 fusion.41
  200.6 0.3 pad_maximum_fusion
  200.9 0.9 all-to-all-done.1
  201.8 7.2 %convolution_convert_fusion = bf16[1024,2880]{1,0:T(8,128)(2,1)} fusion(bf16[1024,512]{0,1:T(8,128)(2,1)S(1)} %bitcast.159, bf16[512,2880]{1,0:T(8,128)(2,1)} %bitcast.40), kind=kOutput, calls=%fused_computation.12 | convolution fusion | flops 3022848000 | bytes 9895936 | tf_op jit(solution)/shard_map/dot_general | solution.py:166
  209.0 0.0 reduce-scatter.2.cloned.1.call-update
  209.0 41.2 %reduce-scatter.2.cloned.1.call-done = bf16[128,2880]{1,0:T(8,128)(2,1)} async-done(((bf16[1024,2880]{1,0:T(8,128)(2,1)}), bf16[128,2880]{1,0:T(8,128)(2,1)}) %reduce-scatter.2.cloned.1.call-update) | async-done | bytes 737296 | tf_op jit(solution)/shard_map/reduce_scatter | solution.py:171
  250.2 0.0 copy-done.4
  250.2 1.3 add_convert_fusion
  251.5 1.1 copy.77
  (21 shorter events, 0.1 us)
Async XLA Ops:
  6.5 106.8 %all-gather.3.cloned.1.call-start = ((), (), s32[]{:S(2)}) async-start(), calls=%async_computation.3 | async-start | bytes 7603200 | tf_op jit(solution)/shard_map/all_gather | solution.py:83
  15.9 5.1 %copy-start = (bf16[128,2880]{0,1:T(8,128)(2,1)S(1)}, bf16[128,2880]{0,1:T(8,128)(2,1)}, u32[]{:S(2)}) copy-start(bf16[128,2880]{0,1:T(8,128)(2,1)} %param.13) | copy-start | bytes 2211844
  15.9 5.4 %copy-start.8 = (s32[128,4]{0,1:T(4,128)S(1)}, s32[128,4]{0,1:T(4,128)}, u32[]{:S(2)}) copy-start(s32[128,4]{0,1:T(4,128)} %param.16) | copy-start | bytes 6148
  15.9 5.4 %copy-start.9 = (s32[128,4]{0,1:T(4,128)S(1)}, s32[128,4]{0,1:T(4,128)}, u32[]{:S(2)}) copy-start(s32[128,4]{0,1:T(4,128)} %param.14) | copy-start | bytes 6148
  15.9 5.5 %copy-start.7 = (f32[128,4]{0,1:T(4,128)S(1)}, f32[128,4]{0,1:T(4,128)}, u32[]{:S(2)}) copy-start(f32[128,4]{0,1:T(4,128)} %param.15) | copy-start | bytes 6148
  15.9 90.5 %all-to-all-start = ((bf16[1,16,8,10,2880]{4,1,3,0,2:T(8,128)(2,1)}), bf16[1,16,8,10,2880]{4,1,3,0,2:T(8,128)(2,1)}, u32[]{:S(2)}, u32[]{:S(2)}) async-start(bf16[1,16,8,10,2880]{4,1,3,0,2:T(8,128)(2,1)} %copy.71), calls=%async_computation | async-start | bytes 15073280 | tf_op jit(solution)/shard_map/all_to_all | solution.py:82
  21.0 141.4 %all-gather.5.cloned.1.call-start = ((), (), s32[]{:S(2)}) async-start(), calls=%async_computation.4 | async-start | bytes 6782976 | tf_op jit(solution)/shard_map/all_gather | solution.py:104
  113.3 4.5 %copy-start.3 = (f32[2880]{0:T(1024)S(1)}, f32[2880]{0:T(1024)}, u32[]{:S(2)}) copy-start(f32[2880]{0:T(1024)} %param.18) | copy-start | bytes 34564
  113.3 5.6 %copy-start.1 = (bf16[1,16,2880]{2,1,0:T(8,128)(2,1)S(1)}, bf16[1,16,2880]{2,1,0:T(8,128)(2,1)}, u32[]{:S(2)}) copy-start(bf16[1,16,2880]{2,1,0:T(8,128)(2,1)} %param.22) | copy-start | bytes 276484
  117.8 14.9 %copy-start.6 = (f32[1,640]{1,0:T(1,128)S(1)}, f32[1,640]{1,0:T(1,128)}, u32[]{:S(2)}) copy-start(f32[1,640]{1,0:T(1,128)} %param.20) | copy-start | bytes 7684
  117.8 15.0 %copy-start.2 = (s32[1024]{0:T(1024)S(1)}, s32[1024]{0:T(1024)}, u32[]{:S(2)}) copy-start(s32[1024]{0:T(1024)} %param.17) | copy-start | bytes 12292
  117.8 15.1 %slice-start = ((s32[1024]{0:T(1024)}), s32[128]{0:T(128)S(1)}, s32[]{:S(2)}) async-start(s32[1024]{0:T(1024)} %param.17), calls=%async_computation.6 | async-start | bytes 1024 | tf_op jit(solution)/shard_map/slice | solution.py:144
  120.7 81.1 %all-to-all-start.1 = ((bf16[32,16,2880]{2,1,0:T(8,128)(2,1)}), bf16[32,16,2880]{2,1,0:T(8,128)(2,1)}, u32[]{:S(2)}, u32[]{:S(2)}) async-start(bf16[32,16,2880]{2,1,0:T(8,128)(2,1)} %broadcast_in_dim.45), calls=%async_computation.1 | async-start | bytes 6029312 | tf_op jit(solution)/shard_map/all_to_all | solution.py:63
  132.4 117.8 %reduce-scatter.2.cloned.1.call-start = ((), (), s32[]{:S(2)}) async-start(), calls=%async_computation.5 | async-start | bytes 6782976 | tf_op jit(solution)/shard_map/reduce_scatter | solution.py:171
  174.2 6.1 %copy-start.5 = (f32[1,8]{1,0:T(1,128)S(1)}, f32[1,8]{1,0:T(1,128)}, u32[]{:S(2)}) copy-start(f32[1,8]{1,0:T(1,128)} %param.21) | copy-start | bytes 100
  176.7 22.9 %collective-permute-start = (bf16[128,1,128]{0,2,1:T(8,128)(2,1)S(1)}, bf16[128,1,128]{0,2,1:T(8,128)(2,1)S(1)}, u32[]{:S(2)}, u32[]{:S(2)}) collective-permute-start(bf16[128,1,128]{0,2,1:T(8,128)(2,1)S(1)} %pad_maximum_fusion.5), channel_id=1, source_target_pairs={{0,8},{8,16},{16,24},{24,32},{32,40},{40,48},{48,56},{56,64},{64,7... | collective-permute-start | bytes 98312 | tf_op jit(solution)/shard_map/ppermute | solution.py:20
  209.0 41.2 %copy-start.4 = (f32[2880]{0:T(1024)S(1)}, f32[2880]{0:T(1024)}, u32[]{:S(2)}) copy-start(f32[2880]{0:T(1024)} %param.23) | copy-start | bytes 34564
Sparse Core Ops, SparseCore 0:
  9.9 95.1 all-gather.2
  119.0 43.2 all-gather.4
  209.1 41.0 reduce-scatter.1
